TPU v7x, 256 devices: a whole 4x4x8 slice. The times are simulated.
256 devices in a mesh: ctx: 32 (over x_lo, z, core), exp: 8 (over y, x_hi).
Axes of the slice: x: 4 (x_hi: 2, x_lo: 2; x = x_hi * 2 + x_lo), y: 4, z: 8, core: 2. Of those that a mesh axis runs over, the one named last changes fastest.
Arguments:
- hidden: bfloat16 [8192, 2048], P(('ctx', 'exp')), may hold values from -1.5 to 1.5
- lengths: int32 [2], replicated, may hold values from 2048 to 4096, as said below
- routes: int32 [8192, 8], P(('ctx', 'exp')), may hold values from 0 to 127, all different within a row; in each aligned block of 32 rows (0 to 31, 32 to 63, ...) at most 4 rows name the same one
- gates: float32 [8192, 8], P(('ctx', 'exp')), may hold values from 0.05 to 0.5
- attn_gain: float32 [2048], replicated, may hold values from 0.25 to 1.75
- q_weight: bfloat16 [2048, 4096], P('ctx', 'exp'), may hold values from -0.125 to 0.125
- key_value_weight: bfloat16 [2048, 1024], P('ctx'), may hold values from -0.125 to 0.125
- q_gain: float32 [128], replicated, may hold values from 0.25 to 1.75
- k_gain: float32 [128], replicated, may hold values from 0.25 to 1.75
- o_weight: bfloat16 [4096, 2048], P('exp', 'ctx'), may hold values from -0.09375 to 0.09375
- moe_gain: float32 [2048], replicated, may hold values from 0.25 to 1.75
- expert_in: bfloat16 [256, 2048, 768], P(('ctx', 'exp')), may hold values from -0.125 to 0.125
- expert_out: bfloat16 [256, 384, 2048], P(('ctx', 'exp')), may hold values from -0.21875 to 0.21875
Outputs:
- new_hidden: bfloat16 [8192, 2048], P(('ctx', 'exp'))
- cache: bfloat16 [2, 8192, 512], P(None, 'ctx', 'exp')
Inputs may be any that keep to these rules, and one draw needn't show every extreme that they name: `lengths`: one of the two prompts has exactly 4096 positions; the other has 2048 to 4096. `routes`: A row names 8 different experts. Within the 32 rows of each device (aligned blocks of rows) no expert is named more than 4 times, a bound that some block reaches.
All inputs are finite; a program needn't handle non-finite values.
Results may differ from a plain program's by a relative error of at most 0.02.
Values may be sent and summed in bfloat16 or wider, within the bound.
No kernel may reach another device: no remote copies, remote signals or barrier semaphores. Data moves between devices by JAX's collectives and lax.ppermute only.
A program may use at most 128 MiB of HBM per device.

v0:
```python
import jax
import jax.numpy as jnp
from jax import lax
from jax.sharding import PartitionSpec as P

MODEL_WIDTH = 2048
QUERY_HEADS = 32
KEY_VALUE_HEADS = 4
HEAD_SIZE = 128
EXPERTS = 128
TOP = 8


epsilon = 1e-06
rope_base = 1000000.0


def from_behind(block, axis, distance):
    devices = range(lax.axis_size(axis))
    route = [((i - distance) % len(devices), i) for i in devices]
    return lax.ppermute(block, axis, route)


def rms_scale(values, gain):
    mean_square = jnp.mean(values * values, axis=-1, keepdims=True)
    return values * lax.rsqrt(mean_square + epsilon) * gain


def mirrored_position(row_ids, count_ctx, tok_ctx):
    half_rows = tok_ctx // 2
    holder = row_ids // tok_ctx
    within = row_ids % tok_ctx
    block_no = jnp.where(within < half_rows, holder, 2 * count_ctx - 1 - holder)
    return block_no * half_rows + within % half_rows


def document_info(token_positions, lengths):
    first_end = lengths[0]
    second_end = lengths[0] + lengths[1]
    document = (token_positions >= first_end).astype(jnp.int32) + (
        token_positions >= second_end
    ).astype(jnp.int32)
    doc_start = jnp.where(document == 0, 0, jnp.where(document == 1, first_end, second_end))
    return (document, token_positions - doc_start)


def rotate(values, rope_pos):
    head_width = values.shape[-1]
    freq_ids = jnp.arange(head_width // 2, dtype=jnp.float32)
    inverse = rope_base ** (-2.0 * freq_ids / head_width)
    angles = rope_pos.astype(jnp.float32)[:, None] * inverse[None, :]
    cosine = jnp.cos(angles)[:, None, :]
    sine_part = jnp.sin(angles)[:, None, :]
    first_half = values[..., : head_width // 2]
    second_half = values[..., head_width // 2 :]
    return jnp.concatenate(
        [
            first_half * cosine - second_half * sine_part,
            second_half * cosine + first_half * sine_part,
        ],
        axis=-1,
    )


def shards(
    hidden,
    lengths,
    routes,
    gates,
    attn_gain,
    q_weight,
    key_value_weight,
    q_gain,
    k_gain,
    o_weight,
    moe_gain,
    expert_in,
    expert_out,
):
    count_ctx = lax.axis_size("ctx")
    expert_count = lax.axis_size("exp")
    my_ctx = lax.axis_index("ctx")
    my_exp = lax.axis_index("exp")
    tok_dev = hidden.shape[0]
    tok_ctx = tok_dev * expert_count
    half_rows = tok_ctx // 2
    head_groups = QUERY_HEADS // KEY_VALUE_HEADS
    q_dev = QUERY_HEADS // expert_count
    key_value_share = max(1, KEY_VALUE_HEADS // expert_count)
    group_dev = q_dev // key_value_share
    column_share = KEY_VALUE_HEADS * HEAD_SIZE // expert_count
    key_value_leading = my_exp * q_dev // head_groups
    col_offset = my_exp * column_share - key_value_leading * HEAD_SIZE
    score_scale = HEAD_SIZE ** (-0.5)
    query_pos = mirrored_position(
        my_ctx * tok_ctx + jnp.arange(tok_ctx, dtype=jnp.int32), count_ctx, tok_ctx
    )
    query_doc, query_rope = document_info(query_pos, lengths)
    normed_own = rms_scale(hidden.astype(jnp.float32), attn_gain).astype(jnp.bfloat16)
    normed = lax.all_gather(normed_own, "exp", axis=0, tiled=True)
    key_cols = lax.dynamic_slice_in_dim(
        key_value_weight, key_value_leading * HEAD_SIZE, key_value_share * HEAD_SIZE, 1
    )
    value_column_block = lax.dynamic_slice_in_dim(
        key_value_weight,
        KEY_VALUE_HEADS * HEAD_SIZE + key_value_leading * HEAD_SIZE,
        key_value_share * HEAD_SIZE,
        1,
    )
    kv_local = jnp.concatenate([key_cols, value_column_block], axis=1)
    q_raw = jnp.dot(
        normed,
        lax.all_gather(q_weight, "ctx", axis=0, tiled=True),
        preferred_element_type=jnp.float32,
    )
    key_value_plain = jnp.dot(
        normed,
        lax.all_gather(kv_local, "ctx", axis=0, tiled=True),
        preferred_element_type=jnp.float32,
    )
    queries = rotate(
        rms_scale(q_raw.reshape(tok_ctx, q_dev, HEAD_SIZE), q_gain), query_rope
    ).astype(jnp.bfloat16)
    key_row_block = rotate(
        rms_scale(
            key_value_plain[:, : key_value_share * HEAD_SIZE].reshape(
                tok_ctx, key_value_share, HEAD_SIZE
            ),
            k_gain,
        ),
        query_rope,
    ).astype(jnp.bfloat16)
    value_row_block = key_value_plain[:, key_value_share * HEAD_SIZE :].astype(jnp.bfloat16)
    key_values = jnp.stack(
        [key_row_block.reshape(tok_ctx, key_value_share * HEAD_SIZE), value_row_block]
    )
    query_groups = queries.reshape(tok_ctx, key_value_share, group_dev, HEAD_SIZE)

    def attend(state_now, block_kv, offset):
        length_now = block_kv.shape[1]
        key_pos = mirrored_position(
            offset + jnp.arange(length_now, dtype=jnp.int32), count_ctx, tok_ctx
        )
        key_doc, unused_rope = document_info(key_pos, lengths)
        allowed = (query_doc[:, None] == key_doc[None, :]) & (
            key_pos[None, :] <= query_pos[:, None]
        )
        key_part = block_kv[0].reshape(length_now, key_value_share, HEAD_SIZE)
        value_part = block_kv[1].reshape(length_now, key_value_share, HEAD_SIZE)
        scores = (
            jnp.einsum("qkgd,skd->kgqs", query_groups, key_part, preferred_element_type=jnp.float32)
            * score_scale
        )
        weights = jnp.where(allowed[None, None], jnp.exp(scores), 0.0).astype(jnp.bfloat16)
        numerator = state_now[0] + jnp.einsum(
            "kgqs,skd->qkgd", weights, value_part, preferred_element_type=jnp.float32
        )
        denominator = state_now[1] + jnp.sum(weights, axis=-1, dtype=jnp.float32)
        return (numerator, denominator) + tuple(state_now[2:])

    initial = (
        jnp.zeros((tok_ctx, key_value_share, group_dev, HEAD_SIZE), jnp.float32),
        jnp.zeros((key_value_share, group_dev, tok_ctx), jnp.float32),
    )
    first_state = attend(initial, key_values, my_ctx * tok_ctx)

    def turn(step_no, loop_state):
        moving = from_behind(loop_state[0], "ctx", 1)
        source = (my_ctx - step_no) % count_ctx
        return (moving, attend(loop_state[1], moving, source * tok_ctx))

    final_state = lax.fori_loop(1, count_ctx, turn, (key_values, first_state))[1]
    context = (
        (final_state[0] / jnp.transpose(final_state[1], (2, 0, 1))[..., None])
        .astype(jnp.bfloat16)
        .reshape(tok_ctx, q_dev * HEAD_SIZE)
    )
    own_cols = lax.dynamic_slice_in_dim(key_values, col_offset, column_share, 2)
    every_rows = lax.all_gather(own_cols, "ctx", axis=1, tiled=True)

    def block_start(block_no):
        holder = jnp.where(block_no < count_ctx, block_no, 2 * count_ctx - 1 - block_no)
        return holder * tok_ctx + jnp.where(block_no < count_ctx, 0, half_rows)

    first_part = lax.dynamic_slice_in_dim(every_rows, block_start(2 * my_ctx), half_rows, 1)
    second_part = lax.dynamic_slice_in_dim(every_rows, block_start(2 * my_ctx + 1), half_rows, 1)
    cache = jnp.concatenate([first_part, second_part], axis=1)
    attn_part = jnp.dot(
        context,
        lax.all_gather(o_weight, "ctx", axis=1, tiled=True),
        preferred_element_type=jnp.float32,
    )
    attn_own = lax.psum_scatter(
        attn_part.astype(jnp.bfloat16), "exp", scatter_dimension=0, tiled=True
    ).astype(jnp.float32)
    residual_mid = hidden.astype(jnp.float32) + attn_own
    moe_in = rms_scale(residual_mid, moe_gain).astype(jnp.bfloat16)
    devices = count_ctx * expert_count
    slices = max(1, devices // EXPERTS)
    rows_dev = expert_in.shape[0]
    ffs_dev = expert_out.shape[1]
    capacity = max(4, 2 * tok_dev * TOP // EXPERTS)
    route_ids = routes.reshape(-1)
    route_count = route_ids.shape[0]
    expert_hot = (route_ids[:, None] == jnp.arange(EXPERTS, dtype=jnp.int32)[None, :]).astype(
        jnp.int32
    )
    ranking = jnp.sum(jnp.cumsum(expert_hot, axis=0) * expert_hot, axis=1) - 1
    slot_ids = route_ids * capacity + ranking
    slot_hot = (
        slot_ids[:, None] == jnp.arange(EXPERTS * capacity, dtype=jnp.int32)[None, :]
    ).astype(jnp.bfloat16)
    token_hot = (
        (jnp.arange(route_count, dtype=jnp.int32) // TOP)[:, None]
        == jnp.arange(tok_dev, dtype=jnp.int32)[None, :]
    ).astype(jnp.bfloat16)
    placement_map = jnp.einsum(
        "rs,rt->st", slot_hot, token_hot, preferred_element_type=jnp.float32
    ).astype(jnp.bfloat16)
    outgoing = jnp.dot(placement_map, moe_in, preferred_element_type=jnp.float32).astype(
        jnp.bfloat16
    )
    outgoing = jnp.broadcast_to(
        outgoing.reshape(EXPERTS, 1, capacity, MODEL_WIDTH),
        (EXPERTS, slices, capacity, MODEL_WIDTH),
    )
    outgoing = outgoing.reshape(count_ctx, expert_count, rows_dev * capacity, MODEL_WIDTH)
    arrived = lax.all_to_all(
        lax.all_to_all(outgoing, "ctx", split_axis=0, concat_axis=0, tiled=True),
        "exp",
        split_axis=1,
        concat_axis=1,
        tiled=True,
    )
    arrived = arrived.reshape(count_ctx, expert_count, rows_dev, capacity, MODEL_WIDTH)
    gate_up = jnp.einsum("abrcd,rdf->abrcf", arrived, expert_in, preferred_element_type=jnp.float32)
    activated = (jax.nn.silu(gate_up[..., :ffs_dev]) * gate_up[..., ffs_dev:]).astype(jnp.bfloat16)
    produced = jnp.einsum(
        "abrcf,rfd->abrcd", activated, expert_out, preferred_element_type=jnp.float32
    ).astype(jnp.bfloat16)
    produced = produced.reshape(count_ctx, expert_count, rows_dev * capacity, MODEL_WIDTH)
    returned = lax.all_to_all(
        lax.all_to_all(produced, "ctx", split_axis=0, concat_axis=0, tiled=True),
        "exp",
        split_axis=1,
        concat_axis=1,
        tiled=True,
    )
    slice_sum = jnp.sum(
        returned.reshape(EXPERTS, slices, capacity, MODEL_WIDTH), axis=1, dtype=jnp.float32
    ).reshape(EXPERTS * capacity, MODEL_WIDTH)
    gate_hot = slot_hot.astype(jnp.float32) * gates.reshape(-1)[:, None]
    combiner = jnp.einsum(
        "rs,rt->ts", gate_hot, token_hot.astype(jnp.float32), precision=lax.Precision.HIGHEST
    )
    moe_out = jnp.dot(combiner, slice_sum, precision=lax.Precision.HIGHEST)
    new_hidden = (residual_mid + moe_out).astype(jnp.bfloat16)
    return (new_hidden, cache)


def solution(mesh):
    in_specs = (
        P(("ctx", "exp"), None),
        P(),
        P(("ctx", "exp"), None),
        P(("ctx", "exp"), None),
        P(),
        P("ctx", "exp"),
        P("ctx", None),
        P(),
        P(),
        P("exp", "ctx"),
        P(),
        P(("ctx", "exp"), None, None),
        P(("ctx", "exp"), None, None),
    )
    out_specs = (P(("ctx", "exp"), None), P(None, "ctx", "exp"))
    return jax.shard_map(shards, mesh=mesh, in_specs=in_specs, out_specs=out_specs, check_vma=False)
```

profile of v0, /device:TPU:1, one launch (start us, length us, event | category | flops | bytes accessed | tf_op | source)
XLA Modules:
  0.0 1005.6 jit_solution(14960117752500921482)
XLA Ops:
  18.9 45.9 %all-gather.6.cloned.1.call-done = bf16[256,2048]{1,0:T(8,128)(2,1)} async-done(((bf16[32,2048]{1,0:T(8,128)(2,1)}), bf16[256,2048]{1,0:T(8,128)(2,1)}) %all-gather.6.cloned.1.call-update) | async-done | bytes 1048592 | tf_op jit(solution)/shard_map/all_gather | solution.py:100
  64.8 66.3 %all-gather.8.cloned.1.call-done = bf16[2048,256]{1,0:T(8,128)(2,1)} async-done(((bf16[64,256]{1,0:T(8,128)(2,1)}), bf16[2048,256]{1,0:T(8,128)(2,1)}) %all-gather.8.cloned.1.call-update) | async-done | bytes 1048592 | tf_op jit(solution)/shard_map/all_gather | solution.py:118
  135.1 62.0 %all-gather.10.cloned.1.call-done = bf16[2048,512]{1,0:T(8,128)(2,1)} async-done(((bf16[64,512]{1,0:T(8,128)(2,1)}), bf16[2048,512]{1,0:T(8,128)(2,1)}) %all-gather.10.cloned.1.call-update) | async-done | bytes 2097168 | tf_op jit(solution)/shard_map/all_gather | solution.py:113
  214.5 304.8 %while.22 = (s32[]{:T(128)}, bf16[2,256,128]{2,1,0:T(8,128)(2,1)}, f32[256,1,4,128]{3,0,2,1:T(8,128)}, f32[1,4,256]{2,1,0:T(4,128)S(1)}, s32[]{:T(128)}, /*index...) while((s32[]{:T(128)}, bf16[2,256,128]{2,1,0:T(8,128)(2,1)}, ...), condition=%wide.region_6.7_spmd.clone.clone, body=%wide.region_4.6_spmd.clone.clone.sunk | while | flops 135895568 | bytes 3432794 | solution.py:172
  250.3 5.9 collective-permute-done
  260.4 5.9 collective-permute-done
  280.5 5.8 collective-permute-done
  290.4 5.8 collective-permute-done
  300.4 5.8 collective-permute-done
  310.4 5.8 collective-permute-done
  320.4 5.8 collective-permute-done
  330.4 5.8 collective-permute-done
  340.4 5.8 collective-permute-done
  350.4 5.8 collective-permute-done
  360.4 5.8 collective-permute-done
  370.3 5.8 collective-permute-done
  380.3 5.8 collective-permute-done
  390.3 5.8 collective-permute-done
  400.3 5.8 collective-permute-done
  410.3 5.8 collective-permute-done
  440.3 5.8 collective-permute-done
  510.2 5.8 collective-permute-done
  526.7 75.7 %reduce-scatter.2.cloned.1.call-done = bf16[32,2048]{1,0:T(8,128)(2,1)} async-done(((bf16[256,2048]{1,0:T(8,128)(2,1)}), bf16[32,2048]{1,0:T(8,128)(2,1)}) %reduce-scatter.2.cloned.1.call-update) | async-done | bytes 131088 | tf_op jit(solution)/shard_map/reduce_scatter | solution.py:193
  614.6 104.2 %all_to_all.20 = bf16[32,8,4,2048]{3,2,1,0:T(4,128)(2,1)S(1)} all-to-all(bf16[32,8,4,2048]{3,2,1,0:T(4,128)(2,1)S(1)} %bitcast.148), channel_id=1, replica_groups=mesh['ctx'=32,'exp'=8] {'ctx'}, dimensions={0} | all-to-all | bytes 8388608 | tf_op jit(solution)/shard_map/all_to_all | solution.py:229
  720.8 53.0 %all_to_all.21 = bf16[32,8,4,2048]{3,2,0,1:T(4,128)(2,1)S(1)} all-to-all(bf16[32,8,4,2048]{3,2,0,1:T(4,128)(2,1)S(1)} %copy.65), channel_id=1, replica_groups=mesh['ctx'=32,'exp'=8] {'exp'}, dimensions={1} | all-to-all | bytes 8388608 | tf_op jit(solution)/shard_map/all_to_all | solution.py:228
  783.2 8.4 all-to-all-start.2
  792.3 100.5 %all-to-all-done.2 = bf16[32,8,4,2048]{3,1,2,0:T(8,128)(2,1)} async-done(((bf16[32,8,4,2048]{3,1,2,0:T(8,128)(2,1)}), bf16[32,8,4,2048]{3,1,2,0:T(8,128)(2,1)}, u32[]{:S(2)}, u32[]{:S(2)}) %all-to-all-start.2) | async-done | bytes 4194336 | tf_op jit(solution)/shard_map/all_to_all | solution.py:243
  892.8 7.4 copy.67
  907.2 44.1 %all-to-all-done.3 = bf16[32,8,4,2048]{3,2,0,1:T(4,128)(2,1)} async-done(((bf16[32,8,4,2048]{3,2,0,1:T(4,128)(2,1)}), bf16[32,8,4,2048]{3,2,0,1:T(4,128)(2,1)}, u32[]{:S(2)}, u32[]{:S(2)}) %all-to-all-start.3) | async-done | bytes 4194336 | tf_op jit(solution)/shard_map/all_to_all | solution.py:242
  951.3 13.6 %copy_convert_fusion = f32[32,8,4,2048]{3,1,2,0:T(8,128)} fusion(bf16[32,8,4,2048]{3,2,0,1:T(4,128)(2,1)} %all-to-all-done.3), kind=kLoop, calls=%fused_computation.46 | loop fusion | flops 2097152 | bytes 12582912 | tf_op jit(solution)/shard_map/convert_element_type | solution.py:249
  964.8 14.0 %copy.69 = f32[32,8,4,2048]{3,2,1,0:T(4,128)} copy(f32[32,8,4,2048]{3,1,2,0:T(8,128)} %copy_convert_fusion) | data formatting | bytes 16777216 | tf_op jit(solution)/shard_map/convert_element_type | solution.py:249
  978.9 8.8 reduce_sum.85
  (372 shorter events, 279.5 us)
Async XLA Ops:
  7.2 57.6 %all-gather.6.cloned.1.call-start = ((), (), s32[]{:S(2)}) async-start(), calls=%async_computation.5 | async-start | bytes 1179648 | tf_op jit(solution)/shard_map/all_gather | solution.py:100
  10.1 121.0 %all-gather.8.cloned.1.call-start = ((), (), s32[]{:S(2)}) async-start(), calls=%async_computation.6 | async-start | bytes 1081344 | tf_op jit(solution)/shard_map/all_gather | solution.py:118
  11.6 185.5 %all-gather.10.cloned.1.call-start = ((), (), s32[]{:S(2)}) async-start(), calls=%async_computation.7 | async-start | bytes 2162688 | tf_op jit(solution)/shard_map/all_gather | solution.py:113
  12.3 510.2 %all-gather.12.cloned.1.call-start = ((), (), s32[]{:S(2)}) async-start(), calls=%async_computation.8 | async-start | bytes 2162688 | tf_op jit(solution)/shard_map/all_gather | solution.py:190
  12.9 589.5 %reduce-scatter.2.cloned.1.call-start = ((), (), s32[]{:S(2)}) async-start(), calls=%async_computation.9 | async-start | bytes 1179648 | tf_op jit(solution)/shard_map/reduce_scatter | solution.py:193
  229.3 6.8 collective-permute-start
  239.4 6.8 collective-permute-start
  249.5 6.8 collective-permute-start
  259.5 6.8 collective-permute-start
  279.6 6.7 collective-permute-start
  289.6 6.7 collective-permute-start
  299.6 6.7 collective-permute-start
  309.5 6.7 collective-permute-start
  319.5 6.7 collective-permute-start
  329.5 6.7 collective-permute-start
  339.5 6.7 collective-permute-start
  349.5 6.7 collective-permute-start
  359.5 6.7 collective-permute-start
  369.5 6.7 collective-permute-start
  379.5 6.7 collective-permute-start
  389.4 6.7 collective-permute-start
  399.4 6.7 collective-permute-start
  409.4 6.7 collective-permute-start
  419.4 6.7 collective-permute-start
  429.4 6.7 collective-permute-start
  439.4 6.7 collective-permute-start
  449.4 6.7 collective-permute-start
  459.4 6.7 collective-permute-start
  509.3 6.7 collective-permute-start
  783.2 109.6 %all-to-all-start.2 = ((bf16[32,8,4,2048]{3,1,2,0:T(8,128)(2,1)}), bf16[32,8,4,2048]{3,1,2,0:T(8,128)(2,1)}, u32[]{:S(2)}, u32[]{:S(2)}) async-start(bf16[32,8,4,2048]{3,1,2,0:T(8,128)(2,1)} %convolution_convert_fusion), calls=%async_computation.3 | async-start | bytes 8388608 | tf_op jit(solution)/shard_map/all_to_all | solution.py:243
  791.6 114.2 %all-gather.14.cloned.1.call-start = ((), (), s32[]{:S(2)}) async-start(), calls=%async_computation.10 | async-start | bytes 2162688 | tf_op jit(solution)/shard_map/all_gather | solution.py:179
  900.2 51.1 %all-to-all-start.3 = ((bf16[32,8,4,2048]{3,2,0,1:T(4,128)(2,1)}), bf16[32,8,4,2048]{3,2,0,1:T(4,128)(2,1)}, u32[]{:S(2)}, u32[]{:S(2)}) async-start(bf16[32,8,4,2048]{3,2,0,1:T(4,128)(2,1)} %copy.67), calls=%async_computation.4 | async-start | bytes 8388608 | tf_op jit(solution)/shard_map/all_to_all | solution.py:242
  (24 other events, 1295.5 us)
Sparse Core Ops, SparseCore 0:
  11.2 53.5 all-gather.5
  66.7 64.3 all-gather.7
  132.9 64.1 all-gather.9
  198.8 64.5 all-gather.11
  526.0 76.3 reduce-scatter.1
  794.4 101.8 all-gather.13
where the time goes:
time: 1020 us; the launch traced here: 1010 us
  waiting for transfers between devices  567 us (56%)
  blocking collectives  157 us (15%)
  matrix products  110 us (11%)
  local copies, waits for them, and re-layouts  70.4 us (7%)
  other arithmetic  65.3 us (6%)
  starting transfers between devices  19.1 us (2%)
  between operations  16 us (2%)
    ppermute x31, waiting for transfers between devices, from_behind(): return lax.ppermute(block, axis, route)  171 us
    all_to_all x1, blocking collectives, shards(): lax.all_to_all(outgoing, 'ctx', split_axis=0, concat_axis=0, tiled=True)  104 us
    all_to_all x1, waiting for transfers between devices, shards(): lax.all_to_all(produced, 'ctx', split_axis=0, concat_axis=0, tiled=True)  100 us
    reduce_scatter x1, waiting for transfers between devices, shards(): lax.psum_scatter(attn_part.astype(jnp.bfloat16), 'exp', scatter_dimension...  75.7 us
    dot_general x32, matrix products, attend(): jnp.einsum('kgqs,skd->qkgd', weights, value_part, preferred_element_type=...  69 us
    all_gather x1, waiting for transfers between devices, shards(): lax.all_gather(kv_local, 'ctx', axis=0, tiled=True)  66.3 us
    all_gather x1, waiting for transfers between devices, shards(): lax.all_gather(q_weight, 'ctx', axis=0, tiled=True)  62 us
    all_to_all x1, blocking collectives, shards(): lax.all_to_all(lax.all_to_all(outgoing, 'ctx', split_axis=0, concat_axis=...  53 us
  transfers between devices with their start and end apart: 39, of which 37 were waited for; matrix products, arithmetic and copies ran while one was open for 17% of the time, Pallas kernels for 0%

commit v1 on v0

--- a/solution.py
+++ b/solution.py
@@ -108,16 +108,13 @@
         1,
     )
     kv_local = jnp.concatenate([key_cols, value_column_block], axis=1)
-    q_raw = jnp.dot(
-        normed,
-        lax.all_gather(q_weight, "ctx", axis=0, tiled=True),
-        preferred_element_type=jnp.float32,
-    )
-    key_value_plain = jnp.dot(
-        normed,
-        lax.all_gather(kv_local, "ctx", axis=0, tiled=True),
-        preferred_element_type=jnp.float32,
-    )
+    q_width = q_dev * HEAD_SIZE
+    weights_all = lax.all_gather(
+        jnp.concatenate([q_weight, kv_local], axis=1), "ctx", axis=0, tiled=True
+    )
+    projected = jnp.dot(normed, weights_all, preferred_element_type=jnp.float32)
+    q_raw = projected[:, :q_width]
+    key_value_plain = projected[:, q_width:]
     queries = rotate(
         rms_scale(q_raw.reshape(tok_ctx, q_dev, HEAD_SIZE), q_gain), query_rope
     ).astype(jnp.bfloat16)
@@ -162,28 +159,30 @@
         jnp.zeros((tok_ctx, key_value_share, group_dev, HEAD_SIZE), jnp.float32),
         jnp.zeros((key_value_share, group_dev, tok_ctx), jnp.float32),
     )
-    first_state = attend(initial, key_values, my_ctx * tok_ctx)
-
-    def turn(step_no, loop_state):
-        moving = from_behind(loop_state[0], "ctx", 1)
-        source = (my_ctx - step_no) % count_ctx
-        return (moving, attend(loop_state[1], moving, source * tok_ctx))
-
-    final_state = lax.fori_loop(1, count_ctx, turn, (key_values, first_state))[1]
+    every_kv = lax.all_gather(key_values, "ctx", axis=1, tiled=True)
+    total_rows = every_kv.shape[1]
+    chunk = min(1024, total_rows)
+
+    def turn(step_no, state_now):
+        block_kv = lax.dynamic_slice_in_dim(every_kv, step_no * chunk, chunk, 1)
+        return attend(state_now, block_kv, step_no * chunk)
+
+    final_state = lax.fori_loop(0, total_rows // chunk, turn, initial)
     context = (
         (final_state[0] / jnp.transpose(final_state[1], (2, 0, 1))[..., None])
         .astype(jnp.bfloat16)
         .reshape(tok_ctx, q_dev * HEAD_SIZE)
     )
-    own_cols = lax.dynamic_slice_in_dim(key_values, col_offset, column_share, 2)
-    every_rows = lax.all_gather(own_cols, "ctx", axis=1, tiled=True)
-
     def block_start(block_no):
         holder = jnp.where(block_no < count_ctx, block_no, 2 * count_ctx - 1 - block_no)
         return holder * tok_ctx + jnp.where(block_no < count_ctx, 0, half_rows)
 
-    first_part = lax.dynamic_slice_in_dim(every_rows, block_start(2 * my_ctx), half_rows, 1)
-    second_part = lax.dynamic_slice_in_dim(every_rows, block_start(2 * my_ctx + 1), half_rows, 1)
+    first_part = lax.dynamic_slice(
+        every_kv, (0, block_start(2 * my_ctx), col_offset), (2, half_rows, column_share)
+    )
+    second_part = lax.dynamic_slice(
+        every_kv, (0, block_start(2 * my_ctx + 1), col_offset), (2, half_rows, column_share)
+    )
     cache = jnp.concatenate([first_part, second_part], axis=1)
     attn_part = jnp.dot(
         context,
@@ -220,18 +219,14 @@
     outgoing = jnp.dot(placement_map, moe_in, preferred_element_type=jnp.float32).astype(
         jnp.bfloat16
     )
-    outgoing = jnp.broadcast_to(
-        outgoing.reshape(EXPERTS, 1, capacity, MODEL_WIDTH),
-        (EXPERTS, slices, capacity, MODEL_WIDTH),
-    )
-    outgoing = outgoing.reshape(count_ctx, expert_count, rows_dev * capacity, MODEL_WIDTH)
-    arrived = lax.all_to_all(
-        lax.all_to_all(outgoing, "ctx", split_axis=0, concat_axis=0, tiled=True),
-        "exp",
-        split_axis=1,
-        concat_axis=1,
-        tiled=True,
-    )
+    experts_ctx = EXPERTS // count_ctx
+    outgoing = outgoing.reshape(count_ctx, experts_ctx * capacity, MODEL_WIDTH)
+    landed = lax.all_to_all(outgoing, "ctx", split_axis=0, concat_axis=0, tiled=True)
+    landed = jnp.broadcast_to(
+        landed.reshape(count_ctx, experts_ctx, 1, capacity, MODEL_WIDTH),
+        (count_ctx, experts_ctx, slices, capacity, MODEL_WIDTH),
+    ).reshape(count_ctx, expert_count, capacity, MODEL_WIDTH)
+    arrived = lax.all_to_all(landed, "exp", split_axis=1, concat_axis=1, tiled=True)
     arrived = arrived.reshape(count_ctx, expert_count, rows_dev, capacity, MODEL_WIDTH)
     gate_up = jnp.einsum("abrcd,rdf->abrcf", arrived, expert_in, preferred_element_type=jnp.float32)
     activated = (jax.nn.silu(gate_up[..., :ffs_dev]) * gate_up[..., ffs_dev:]).astype(jnp.bfloat16)
@@ -239,16 +234,20 @@
         "abrcf,rfd->abrcd", activated, expert_out, preferred_element_type=jnp.float32
     ).astype(jnp.bfloat16)
     produced = produced.reshape(count_ctx, expert_count, rows_dev * capacity, MODEL_WIDTH)
+    came_back = lax.all_to_all(produced, "exp", split_axis=1, concat_axis=1, tiled=True)
+    part_sum = jnp.sum(
+        came_back.reshape(count_ctx, experts_ctx, slices, capacity, MODEL_WIDTH),
+        axis=2,
+        dtype=jnp.float32,
+    ).astype(jnp.bfloat16)
     returned = lax.all_to_all(
-        lax.all_to_all(produced, "ctx", split_axis=0, concat_axis=0, tiled=True),
-        "exp",
-        split_axis=1,
-        concat_axis=1,
+        part_sum.reshape(count_ctx, experts_ctx * capacity, MODEL_WIDTH),
+        "ctx",
+        split_axis=0,
+        concat_axis=0,
         tiled=True,
     )
-    slice_sum = jnp.sum(
-        returned.reshape(EXPERTS, slices, capacity, MODEL_WIDTH), axis=1, dtype=jnp.float32
-    ).reshape(EXPERTS * capacity, MODEL_WIDTH)
+    slice_sum = returned.reshape(EXPERTS * capacity, MODEL_WIDTH).astype(jnp.float32)
     gate_hot = slot_hot.astype(jnp.float32) * gates.reshape(-1)[:, None]
     combiner = jnp.einsum(
         "rs,rt->ts", gate_hot, token_hot.astype(jnp.float32), precision=lax.Precision.HIGHEST

time: 1020 us -> 616 us (0.60); the launches traced: 1010 us -> 613 us
  waiting for transfers between devices: 567 us -> 317 us
  matrix products: 110 us -> 50.8 us
  other arithmetic: 65.3 us -> 24.7 us
  local copies, waits for them, and re-layouts: 70.4 us -> 31.3 us
    ppermute x31 -> x0, waiting for transfers between devices: 171 us -> none  [from_behind(): return lax.ppermute(block, axis, route)]
    all_to_all x2 -> x1, waiting for transfers between devices: 145 us -> 46.3 us  [shards(): lax.all_to_all(part_sum.reshape(count_ctx, experts_ctx * capacity, MODEL_...]
    dot_general x32 -> x8, matrix products: 69 us -> 12.1 us  [attend(): jnp.einsum('kgqs,skd->qkgd', weights, value_part, preferred_element_type=...]
    all_to_all x1 -> x2, blocking collectives: 53 us -> 103 us  [the longest x1 53.1 us: shards(): lax.all_to_all(landed, 'exp', split_axis=1, concat_axis=1, tiled=True)]
    all_to_all x1, blocking collectives: 104 us -> 59 us  [shards(): lax.all_to_all(outgoing, 'ctx', split_axis=0, concat_axis=0, tiled=True)]
    all_gather x1, waiting for transfers between devices: 0.02 us -> 20.4 us  [shards(): lax.all_gather(o_weight, 'ctx', axis=1, tiled=True)]
    add x63 -> x16, other arithmetic: 22.7 us -> 5.69 us  [mirrored_position(): return block_no * half_rows + within % half_rows]
    while x32, local copies, waits for them, and re-layouts: 22.4 us -> 6.27 us
  transfers between devices with their start and end apart: 39 -> 6, of which waited for: 37 -> 6; matrix products, arithmetic and copies ran while one was open for 17% -> 9% of each run, Pallas kernels for 0% -> 0%
where the time goes in v1:
time: 616 us; the launch traced here: 613 us
  waiting for transfers between devices  317 us (51%)
  blocking collectives  162 us (26%)
  matrix products  50.8 us (8%)
  local copies, waits for them, and re-layouts  31.3 us (5%)
  other arithmetic  24.7 us (4%)
  between operations  15.4 us (2%)
  starting transfers between devices  12.3 us (2%)
    reduce_scatter x1, waiting for transfers between devices, shards(): lax.psum_scatter(attn_part.astype(jnp.bfloat16), 'exp', scatter_dimension...  74.4 us
    all_gather x1, waiting for transfers between devices, shards(): lax.all_gather(jnp.concatenate([q_weight, kv_local], axis=1), 'ctx', axis...  68.4 us
    all_to_all x1, blocking collectives, shards(): lax.all_to_all(outgoing, 'ctx', split_axis=0, concat_axis=0, tiled=True)  59 us
    all_gather x1, waiting for transfers between devices, shards(): every_kv = lax.all_gather(key_values, 'ctx', axis=1, tiled=True)  57.6 us
    all_to_all x1, blocking collectives, shards(): lax.all_to_all(landed, 'exp', split_axis=1, concat_axis=1, tiled=True)  53.1 us
    all_to_all x1, blocking collectives, shards(): lax.all_to_all(produced, 'exp', split_axis=1, concat_axis=1, tiled=True)  49.8 us
    all_gather x1, waiting for transfers between devices, shards(): normed = lax.all_gather(normed_own, 'exp', axis=0, tiled=True)  49 us
    all_to_all x1, waiting for transfers between devices, shards(): lax.all_to_all(part_sum.reshape(count_ctx, experts_ctx * capacity, MODEL_...  46.3 us
  transfers between devices with their start and end apart: 6, of which 6 were waited for; matrix products, arithmetic and copies ran while one was open for 9% of the time, Pallas kernels for 0%

profile of v1, /device:TPU:1, one launch (start us, length us, event | category | flops | bytes accessed | tf_op | source)
XLA Modules:
  0.0 613.5 jit_solution(10730122127005586213)
XLA Ops:
  15.8 49.0 %all-gather.5.cloned.1.call-done = bf16[256,2048]{1,0:T(8,128)(2,1)} async-done(((bf16[32,2048]{1,0:T(8,128)(2,1)}), bf16[256,2048]{1,0:T(8,128)(2,1)}) %all-gather.5.cloned.1.call-update) | async-done | bytes 1048592 | tf_op jit(solution)/shard_map/all_gather | solution.py:100
  64.8 68.4 %all-gather.7.cloned.1.call-done = bf16[2048,768]{1,0:T(8,128)(2,1)} async-done(((bf16[64,768]{1,0:T(8,128)(2,1)}), bf16[2048,768]{1,0:T(8,128)(2,1)}) %all-gather.7.cloned.1.call-update) | async-done | bytes 3145744 | tf_op jit(solution)/shard_map/all_gather | solution.py:112
  133.2 3.2 fusion.85
  139.3 2.3 fusion.83
  146.7 57.6 %all-gather.9.cloned.1.call-done = bf16[2,8192,128]{2,1,0:T(8,128)(2,1)} async-done(((bf16[2,256,128]{2,1,0:T(8,128)(2,1)}), bf16[2,8192,128]{2,1,0:T(8,128)(2,1)}) %all-gather.9.cloned.1.call-update) | async-done | bytes 4194320 | tf_op jit(solution)/shard_map/all_gather | solution.py:162
  204.3 44.5 %while.21 = (s32[]{:T(128)}, f32[256,1,4,128]{0,3,2,1:T(8,128)}, f32[1,4,256]{2,1,0:T(4,128)S(1)}, bf16[2,8192,128]{2,1,0:T(8,128)(2,1)}, s32[2]{0:T(128)S(1)}, ...) while((s32[]{:T(128)}, f32[256,1,4,128]{0,3,2,1:T(8,128)}, ...), condition=%wide.region_5.6_spmd.clone.clone.clone, body=%wide.region_3.5_spmd.clone.clone.clone.sunk | while | flops 543215872 | bytes 10785070 | solution.py:170
  205.4 2.1 convert_reduce_fusion.2
  211.0 2.1 convert_reduce_fusion.2
  216.5 2.1 convert_reduce_fusion.2
  222.1 2.1 convert_reduce_fusion.2
  227.6 2.1 convert_reduce_fusion.2
  233.2 2.1 convert_reduce_fusion.2
  238.7 2.1 convert_reduce_fusion.2
  244.3 2.1 convert_reduce_fusion.2
  249.9 20.4 %all-gather.11.cloned.1.call-done = bf16[512,2048]{0,1:T(8,128)(2,1)} async-done(((bf16[512,64]{0,1:T(8,128)(2,1)}), bf16[512,2048]{0,1:T(8,128)(2,1)}) %all-gather.11.cloned.1.call-update) | async-done | bytes 2097168 | tf_op jit(solution)/shard_map/all_gather | solution.py:189
  270.3 3.3 convolution_convert_fusion.2
  274.6 74.4 %reduce-scatter.2.cloned.1.call-done = bf16[32,2048]{1,0:T(8,128)(2,1)} async-done(((bf16[256,2048]{1,0:T(8,128)(2,1)}), bf16[32,2048]{1,0:T(8,128)(2,1)}) %reduce-scatter.2.cloned.1.call-update) | async-done | bytes 131088 | tf_op jit(solution)/shard_map/reduce_scatter | solution.py:192
  350.0 3.2 convolution_convert_fusion.1
  353.3 59.0 %all_to_all.20 = bf16[32,16,2048]{2,1,0:T(8,128)(2,1)} all-to-all(bf16[32,16,2048]{2,1,0:T(8,128)(2,1)} %bitcast.128), channel_id=1, replica_groups=mesh['ctx'=32,'exp'=8] {'ctx'}, dimensions={0} | all-to-all | bytes 4194304 | tf_op jit(solution)/shard_map/all_to_all | solution.py:224
  412.3 4.2 broadcast_in_dim.90
  416.5 2.6 copy.100
  419.1 2.6 broadcast_in_dim.91
  421.7 53.1 %all_to_all.21 = bf16[32,8,4,2048]{3,2,0,1:T(4,128)(2,1)S(1)} all-to-all(bf16[32,8,4,2048]{3,2,0,1:T(4,128)(2,1)S(1)} %bitcast.127), channel_id=1, replica_groups=mesh['ctx'=32,'exp'=8] {'exp'}, dimensions={1} | all-to-all | bytes 8388608 | tf_op jit(solution)/shard_map/all_to_all | solution.py:229
  474.8 5.0 fusion.32
  479.8 2.3 convolution_convert_fusion
  482.1 3.2 copy.102
  485.4 49.8 %all_to_all.22 = bf16[32,8,4,2048]{3,2,0,1:T(4,128)(2,1)S(1)} all-to-all(bf16[32,8,4,2048]{3,2,0,1:T(4,128)(2,1)S(1)} %copy.102), channel_id=1, replica_groups=mesh['ctx'=32,'exp'=8] {'exp'}, dimensions={1} | all-to-all | bytes 8388608 | tf_op jit(solution)/shard_map/all_to_all | solution.py:237
  535.1 3.4 bitcast_reduce_fusion
  539.7 2.5 copy.105
  542.2 12.1 %all-to-all-start.3 = ((bf16[32,16,2048]{2,1,0:T(8,128)(2,1)}), bf16[32,16,2048]{2,1,0:T(8,128)(2,1)}, u32[]{:S(2)}, u32[]{:S(2)}) async-start(bf16[32,16,2048]{2,1,0:T(8,128)(2,1)} %copy.105), calls=%async_computation.4 | async-start | bytes 4194304 | tf_op jit(solution)/shard_map/all_to_all | solution.py:243
  557.3 46.3 %all-to-all-done.3 = bf16[32,16,2048]{2,1,0:T(8,128)(2,1)} async-done(((bf16[32,16,2048]{2,1,0:T(8,128)(2,1)}), bf16[32,16,2048]{2,1,0:T(8,128)(2,1)}, u32[]{:S(2)}, u32[]{:S(2)}) %all-to-all-start.3) | async-done | bytes 2097184 | tf_op jit(solution)/shard_map/all_to_all | solution.py:243
  603.6 3.4 fusion.31
  (151 shorter events, 49.2 us)
Async XLA Ops:
  7.2 467.6 %copy-start = (bf16[1,2048,768]{2,1,0:T(8,128)(2,1)S(1)}, bf16[1,2048,768]{2,1,0:T(8,128)(2,1)}, u32[]{:S(2)}) copy-start(bf16[1,2048,768]{2,1,0:T(8,128)(2,1)} %param.26) | copy-start | bytes 9437188
  7.2 57.6 %all-gather.5.cloned.1.call-start = ((), (), s32[]{:S(2)}) async-start(), calls=%async_computation.5 | async-start | bytes 1179648 | tf_op jit(solution)/shard_map/all_gather | solution.py:100
  10.1 123.1 %all-gather.7.cloned.1.call-start = ((), (), s32[]{:S(2)}) async-start(), calls=%async_computation.6 | async-start | bytes 3244032 | tf_op jit(solution)/shard_map/all_gather | solution.py:112
  10.2 126.4 %copy-start.10 = (f32[128]{0:T(128)S(1)}, f32[128]{0:T(128)}, u32[]{:S(2)}) copy-start(f32[128]{0:T(128)} %param.23) | copy-start | bytes 1540
  12.5 191.9 %all-gather.9.cloned.1.call-start = ((), (), s32[]{:S(2)}) async-start(), calls=%async_computation.7 | async-start | bytes 4325376 | tf_op jit(solution)/shard_map/all_gather | solution.py:162
  136.4 0.9 copy-start.5
  136.4 8.6 %copy-start.11 = (f32[128]{0:T(128)S(1)}, f32[128]{0:T(128)}, u32[]{:S(2)}) copy-start(f32[128]{0:T(128)} %param.22) | copy-start | bytes 1540
  138.1 132.3 %all-gather.11.cloned.1.call-start = ((), (), s32[]{:S(2)}) async-start(), calls=%async_computation.8 | async-start | bytes 2162688 | tf_op jit(solution)/shard_map/all_gather | solution.py:189
  138.7 210.3 %reduce-scatter.2.cloned.1.call-start = ((), (), s32[]{:S(2)}) async-start(), calls=%async_computation.9 | async-start | bytes 1179648 | tf_op jit(solution)/shard_map/reduce_scatter | solution.py:192
  141.5 62.8 %copy-start.6 = (s32[2]{0:T(128)S(1)}, s32[2]{0:T(128)}, u32[]{:S(2)}) copy-start(s32[2]{0:T(128)} %param.16) | copy-start | bytes 28
  205.4 2.2 copy-start.1
  209.1 0.8 copy-start.2
  211.0 2.2 copy-start.1
  214.6 0.8 copy-start.2
  216.5 2.2 copy-start.1
  220.2 0.8 copy-start.2
  222.0 2.2 copy-start.1
  225.7 0.8 copy-start.2
  227.6 2.2 copy-start.1
  231.3 0.8 copy-start.2
  233.2 2.2 copy-start.1
  238.7 2.2 copy-start.1
  242.4 0.8 copy-start.2
  244.3 2.2 copy-start.1
  248.0 0.8 copy-start.2
  248.8 24.9 %copy-start.8 = (s32[32,8]{0,1:T(8,128)S(1)}, s32[32,8]{0,1:T(8,128)}, u32[]{:S(2)}) copy-start(s32[32,8]{0,1:T(8,128)} %param.17) | copy-start | bytes 3076
  248.8 100.2 %copy-start.3 = (bf16[32,2048]{1,0:T(8,128)(2,1)S(1)}, bf16[32,2048]{1,0:T(8,128)(2,1)}, u32[]{:S(2)}) copy-start(bf16[32,2048]{1,0:T(8,128)(2,1)} %param.15) | copy-start | bytes 393220
  248.8 101.2 %copy-start.7 = (f32[2048]{0:T(1024)S(1)}, f32[2048]{0:T(1024)}, u32[]{:S(2)}) copy-start(f32[2048]{0:T(1024)} %param.25) | copy-start | bytes 24580
  474.8 5.0 copy-start.12
  542.2 12.1 %copy-start.9 = (f32[32,8]{0,1:T(8,128)S(1)}, f32[32,8]{0,1:T(8,128)}, u32[]{:S(2)}) copy-start(f32[32,8]{0,1:T(8,128)} %param.18) | copy-start | bytes 3076
  542.2 61.4 %copy-start.4 = (bf16[32,2048]{1,0:T(8,128)(2,1)S(1)}, bf16[32,2048]{1,0:T(8,128)(2,1)}, u32[]{:S(2)}) copy-start(bf16[32,2048]{1,0:T(8,128)(2,1)} %reduce-scatter.2.cloned.1.call-done) | copy-start | bytes 393220
  542.2 61.4 %all-to-all-start.3 = ((bf16[32,16,2048]{2,1,0:T(8,128)(2,1)}), bf16[32,16,2048]{2,1,0:T(8,128)(2,1)}, u32[]{:S(2)}, u32[]{:S(2)}) async-start(bf16[32,16,2048]{2,1,0:T(8,128)(2,1)} %copy.105), calls=%async_computation.4 | async-start | bytes 4194304 | tf_op jit(solution)/shard_map/all_to_all | solution.py:243
  (1 other events, 0.8 us)
Sparse Core Ops, SparseCore 0:
  11.2 53.5 all-gather.4
  66.7 66.5 all-gather.6
  138.2 66.0 all-gather.8
  206.0 64.2 all-gather.10
  274.1 74.8 reduce-scatter.1

commit v2 on v1

--- a/solution.py
+++ b/solution.py
@@ -97,7 +97,13 @@
     )
     query_doc, query_rope = document_info(query_pos, lengths)
     normed_own = rms_scale(hidden.astype(jnp.float32), attn_gain).astype(jnp.bfloat16)
-    normed = lax.all_gather(normed_own, "exp", axis=0, tiled=True)
+    normed = lax.all_to_all(
+        jnp.broadcast_to(normed_own[None], (expert_count,) + normed_own.shape),
+        "exp",
+        split_axis=0,
+        concat_axis=0,
+        tiled=True,
+    ).reshape(tok_ctx, MODEL_WIDTH)
     key_cols = lax.dynamic_slice_in_dim(
         key_value_weight, key_value_leading * HEAD_SIZE, key_value_share * HEAD_SIZE, 1
     )
@@ -159,7 +165,14 @@
         jnp.zeros((tok_ctx, key_value_share, group_dev, HEAD_SIZE), jnp.float32),
         jnp.zeros((key_value_share, group_dev, tok_ctx), jnp.float32),
     )
-    every_kv = lax.all_gather(key_values, "ctx", axis=1, tiled=True)
+    pair = [(i, i ^ 1) for i in range(expert_count)]
+    every_kv, partner_in, partner_out = lax.optimization_barrier(
+        (
+            lax.all_gather(key_values, "ctx", axis=1, tiled=True),
+            lax.ppermute(expert_in, "exp", pair),
+            lax.ppermute(expert_out, "exp", pair),
+        )
+    )
     total_rows = every_kv.shape[1]
     chunk = min(1024, total_rows)
 
@@ -189,9 +202,14 @@
         lax.all_gather(o_weight, "ctx", axis=1, tiled=True),
         preferred_element_type=jnp.float32,
     )
-    attn_own = lax.psum_scatter(
-        attn_part.astype(jnp.bfloat16), "exp", scatter_dimension=0, tiled=True
-    ).astype(jnp.float32)
+    attn_pieces = lax.all_to_all(
+        attn_part.astype(jnp.bfloat16).reshape(expert_count, tok_dev, MODEL_WIDTH),
+        "exp",
+        split_axis=0,
+        concat_axis=0,
+        tiled=True,
+    )
+    attn_own = jnp.sum(attn_pieces, axis=0, dtype=jnp.float32)
     residual_mid = hidden.astype(jnp.float32) + attn_own
     moe_in = rms_scale(residual_mid, moe_gain).astype(jnp.bfloat16)
     devices = count_ctx * expert_count
@@ -220,28 +238,29 @@
         jnp.bfloat16
     )
     experts_ctx = EXPERTS // count_ctx
+    share = capacity // slices
+    expert_in_both = jnp.concatenate([expert_in, partner_in], axis=0)
+    expert_out_both = jnp.concatenate([expert_out, partner_out], axis=0)
     outgoing = outgoing.reshape(count_ctx, experts_ctx * capacity, MODEL_WIDTH)
     landed = lax.all_to_all(outgoing, "ctx", split_axis=0, concat_axis=0, tiled=True)
-    landed = jnp.broadcast_to(
-        landed.reshape(count_ctx, experts_ctx, 1, capacity, MODEL_WIDTH),
-        (count_ctx, experts_ctx, slices, capacity, MODEL_WIDTH),
-    ).reshape(count_ctx, expert_count, capacity, MODEL_WIDTH)
+    landed = landed.reshape(count_ctx, expert_count, share, MODEL_WIDTH)
     arrived = lax.all_to_all(landed, "exp", split_axis=1, concat_axis=1, tiled=True)
-    arrived = arrived.reshape(count_ctx, expert_count, rows_dev, capacity, MODEL_WIDTH)
-    gate_up = jnp.einsum("abrcd,rdf->abrcf", arrived, expert_in, preferred_element_type=jnp.float32)
+    tokens_in = arrived.reshape(-1, MODEL_WIDTH)
+    gate_up = jnp.einsum(
+        "td,sdf->stf", tokens_in, expert_in_both, preferred_element_type=jnp.float32
+    )
     activated = (jax.nn.silu(gate_up[..., :ffs_dev]) * gate_up[..., ffs_dev:]).astype(jnp.bfloat16)
     produced = jnp.einsum(
-        "abrcf,rfd->abrcd", activated, expert_out, preferred_element_type=jnp.float32
-    ).astype(jnp.bfloat16)
-    produced = produced.reshape(count_ctx, expert_count, rows_dev * capacity, MODEL_WIDTH)
+        "stf,sfd->std", activated, expert_out_both, preferred_element_type=jnp.float32
+    ).astype(jnp.bfloat16)
+    produced = (
+        jnp.sum(produced, axis=0, dtype=jnp.float32)
+        .astype(jnp.bfloat16)
+        .reshape(count_ctx, expert_count, share, MODEL_WIDTH)
+    )
     came_back = lax.all_to_all(produced, "exp", split_axis=1, concat_axis=1, tiled=True)
-    part_sum = jnp.sum(
-        came_back.reshape(count_ctx, experts_ctx, slices, capacity, MODEL_WIDTH),
-        axis=2,
-        dtype=jnp.float32,
-    ).astype(jnp.bfloat16)
     returned = lax.all_to_all(
-        part_sum.reshape(count_ctx, experts_ctx * capacity, MODEL_WIDTH),
+        came_back.reshape(count_ctx, experts_ctx * capacity, MODEL_WIDTH),
         "ctx",
         split_axis=0,
         concat_axis=0,

time: 616 us -> 500 us (0.81)
  waiting for transfers between devices: 317 us -> 249 us
  blocking collectives: 162 us -> 111 us
  starting transfers between devices: 12.3 us -> 29.2 us
  other arithmetic: 24.7 us -> 16.6 us
    ppermute x0 -> x2, waiting for transfers between devices: none -> 130 us  [the longest x1 130 us: shards(): lax.ppermute(expert_out, 'exp', pair)]
    all_gather x2 -> x1, waiting for transfers between devices: 107 us -> 0.01 us  [shards(): lax.all_gather(key_values, 'ctx', axis=1, tiled=True)]
    reduce_scatter x1 -> x0, waiting for transfers between devices: 74.4 us -> none  [shards(): lax.psum_scatter(attn_part.astype(jnp.bfloat16), 'exp', scatter_dimension...]
    all_to_all x1 -> x3, waiting for transfers between devices: 46.3 us -> 78 us  [the longest x1 46.8 us: shards(): lax.all_to_all(came_back.reshape(count_ctx, experts_ctx * capacity, MODEL...]
    all_gather x1, waiting for transfers between devices: 68.4 us -> 41.2 us  [shards(): lax.all_gather(jnp.concatenate([q_weight, kv_local], axis=1), 'ctx', axis...]
    all_to_all x1, blocking collectives: 53.1 us -> 28.5 us  [shards(): lax.all_to_all(landed, 'exp', split_axis=1, concat_axis=1, tiled=True)]
    all_to_all x1, blocking collectives: 49.8 us -> 27.3 us  [shards(): lax.all_to_all(produced, 'exp', split_axis=1, concat_axis=1, tiled=True)]
    all_gather x1, waiting for transfers between devices: 20.4 us -> 0.02 us  [shards(): lax.all_gather(o_weight, 'ctx', axis=1, tiled=True)]
  transfers between devices with their start and end apart: 6 -> 8, of which waited for: 6 -> 5; matrix products, arithmetic and copies ran while one was open for 9% -> 10% of each run, Pallas kernels for 0% -> 0%
where the time goes in v2:
time: 500 us; the launch traced here: 498 us
  waiting for transfers between devices  249 us (50%)
  blocking collectives  111 us (22%)
  matrix products  50.5 us (10%)
  starting transfers between devices  29.2 us (6%)
  local copies, waits for them, and re-layouts  25.3 us (5%)
  other arithmetic  16.6 us (3%)
  between operations  15.5 us (3%)
    ppermute x1, waiting for transfers between devices, shards(): lax.ppermute(expert_out, 'exp', pair)  130 us
    all_to_all x1, blocking collectives, shards(): lax.all_to_all(outgoing, 'ctx', split_axis=0, concat_axis=0, tiled=True)  55 us
    all_to_all x1, waiting for transfers between devices, shards(): lax.all_to_all(came_back.reshape(count_ctx, experts_ctx * capacity, MODEL...  46.8 us
    all_gather x1, waiting for transfers between devices, shards(): lax.all_gather(jnp.concatenate([q_weight, kv_local], axis=1), 'ctx', axis...  41.2 us
    all_to_all x1, blocking collectives, shards(): lax.all_to_all(landed, 'exp', split_axis=1, concat_axis=1, tiled=True)  28.5 us
    all_to_all x1, blocking collectives, shards(): lax.all_to_all(produced, 'exp', split_axis=1, concat_axis=1, tiled=True)  27.3 us
    dot_general x8, matrix products, attend(): jnp.einsum('qkgd,skd->kgqs', query_groups, key_part, preferred_element_ty...  16.6 us
    all_to_all x1, waiting for transfers between devices, shards(): lax.all_to_all(jnp.broadcast_to(normed_own[None], (expert_count,) + norme...  16.1 us
  transfers between devices with their start and end apart: 8, of which 5 were waited for; matrix products, arithmetic and copies ran while one was open for 10% of the time, Pallas kernels for 0%

profile of v2, /device:TPU:1, one launch (start us, length us, event | category | flops | bytes accessed | tf_op | source)
XLA Modules:
  0.0 497.7 jit_solution(2509761672089677757)
XLA Ops:
  12.7 7.5 %all-to-all-start = ((bf16[8,32,2048]{2,1,0:T(8,128)(2,1)}), bf16[8,32,2048]{2,1,0:T(8,128)(2,1)S(1)}, u32[]{:S(2)}, u32[]{:S(2)}) async-start(bf16[8,32,2048]{2,1,0:T(8,128)(2,1)} %broadcast_in_dim.89), calls=%async_computation | async-start | bytes 2097152 | tf_op jit(solution)/shard_map/all_to_all | solution.py:100
  22.8 16.1 %all-to-all-done = bf16[8,32,2048]{2,1,0:T(8,128)(2,1)S(1)} async-done(((bf16[8,32,2048]{2,1,0:T(8,128)(2,1)}), bf16[8,32,2048]{2,1,0:T(8,128)(2,1)S(1)}, u32[]{:S(2)}, u32[]{:S(2)}) %all-to-all-start) | async-done | bytes 1048608 | tf_op jit(solution)/shard_map/all_to_all | solution.py:100
  38.8 41.2 %all-gather.4.cloned.1.call-done = bf16[2048,768]{1,0:T(8,128)(2,1)} async-done(((bf16[64,768]{1,0:T(8,128)(2,1)}), bf16[2048,768]{1,0:T(8,128)(2,1)}) %all-gather.4.cloned.1.call-update) | async-done | bytes 3145744 | tf_op jit(solution)/shard_map/all_gather | solution.py:118
  80.0 3.3 fusion.88
  85.1 3.0 copy.106
  88.1 2.5 collective-permute-start
  94.4 130.1 %collective-permute-done.1 = bf16[1,384,2048]{2,1,0:T(8,128)(2,1)} collective-permute-done((bf16[1,384,2048]{2,1,0:T(8,128)(2,1)}, bf16[1,384,2048]{2,1,0:T(8,128)(2,1)}, u32[]{:S(2)}, u32[]{:S(2)}) %collective-permute-start.1) | collective-permute-done | bytes 1572896 | tf_op jit(solution)/shard_map/ppermute | solution.py:173
  224.6 37.6 %while.21 = (s32[]{:T(128)}, f32[256,1,4,128]{0,3,2,1:T(8,128)S(1)}, f32[1,4,256]{2,1,0:T(4,128)S(1)}, bf16[2,8192,128]{2,1,0:T(8,128)(2,1)}, s32[2]{0:T(128)S(1...) while((s32[]{:T(128)}, ...), condition=%wide.region_5.6_spmd.clone.clone.clone, body=%wide.region_3.5_spmd.clone.clone.clone.sunk | while | flops 543215872 | bytes 6590702 | solution.py:183
  225.7 2.1 convert_reduce_fusion.4
  230.4 2.1 convert_reduce_fusion.4
  235.1 2.1 convert_reduce_fusion.4
  239.8 2.1 convert_reduce_fusion.4
  244.5 2.1 convert_reduce_fusion.4
  249.2 2.1 convert_reduce_fusion.4
  253.9 2.1 convert_reduce_fusion.4
  258.6 2.1 convert_reduce_fusion.4
  262.3 3.3 convolution_convert_fusion.1
  265.6 6.3 %all-to-all-start.1 = ((bf16[8,32,2048]{2,1,0:T(8,128)(2,1)}), bf16[8,32,2048]{2,1,0:T(8,128)(2,1)S(1)}, u32[]{:S(2)}, u32[]{:S(2)}) async-start(bf16[8,32,2048]{2,1,0:T(8,128)(2,1)} %bitcast.12), calls=%async_computation.1 | async-start | bytes 2097152 | tf_op jit(solution)/shard_map/all_to_all | solution.py:205
  272.4 15.1 %all-to-all-done.1 = bf16[8,32,2048]{2,1,0:T(8,128)(2,1)S(1)} async-done(((bf16[8,32,2048]{2,1,0:T(8,128)(2,1)}), bf16[8,32,2048]{2,1,0:T(8,128)(2,1)S(1)}, u32[]{:S(2)}, u32[]{:S(2)}) %all-to-all-start.1) | async-done | bytes 1048608 | tf_op jit(solution)/shard_map/all_to_all | solution.py:205
  288.8 55.0 %all_to_all.30 = bf16[32,16,2048]{2,1,0:T(8,128)(2,1)S(1)} all-to-all(bf16[32,16,2048]{2,1,0:T(8,128)(2,1)S(1)} %bitcast.106), channel_id=1, replica_groups=mesh['ctx'=32,'exp'=8] {'ctx'}, dimensions={0} | all-to-all | bytes 4194304 | tf_op jit(solution)/shard_map/all_to_all | solution.py:245
  345.0 2.2 copy.116
  347.1 28.5 %all_to_all.31 = bf16[32,8,2,2048]{3,2,0,1:T(2,128)(2,1)S(1)} all-to-all(bf16[32,8,2,2048]{3,2,0,1:T(2,128)(2,1)S(1)} %copy.116), channel_id=1, replica_groups=mesh['ctx'=32,'exp'=8] {'exp'}, dimensions={1} | all-to-all | bytes 4194304 | tf_op jit(solution)/shard_map/all_to_all | solution.py:247
  375.7 2.3 copy.117
  378.0 2.2 reshape.550
  380.2 6.3 %fusion.36 = f32[2,512,768]{1,2,0:T(8,128)S(1)} fusion(bf16[512,2048,1]{1,0,2:T(8,128)(2,1)} %reshape.550, bf16[1,2048,768]{1,2,0:T(8,128)(2,1)} %collective-permute-done, bf16[1,2048,768]{1,2,0:T(8,128)(2,1)} %copy.106), kind=kOutput, calls=%fused_computation.64 | convolution fusion | flops 3224371200 | bytes 11534336 | tf_op jit(solution)/shard_map/td,sdf->stf/dot_general | solution.py:249
  386.6 5.7 %convert_reduce_fusion.1 = bf16[512,2048]{1,0:T(8,128)(2,1)} fusion(bf16[1,384,2048]{2,1,0:T(8,128)(2,1)} %collective-permute-done.1, bf16[1,384,2048]{2,1,0:T(8,128)(2,1)S(1)} %copy-done.10, f32[2,512,768]{1,2,0:T(8,128)S(1)} %fusion.36), kind=kOutput, calls=%fused_computation.55 | convolution fusion | flops 1617690624 | bytes 8388608 | tf_op jit(solution)/shard_map/stf,sfd->std/dot_general | solution.py:253
  392.2 3.2 reshape.533
  397.1 27.3 %all_to_all.32 = bf16[32,8,2,2048]{3,2,0,1:T(2,128)(2,1)S(1)} all-to-all(bf16[32,8,2,2048]{3,2,0,1:T(2,128)(2,1)S(1)} %copy.119), channel_id=1, replica_groups=mesh['ctx'=32,'exp'=8] {'exp'}, dimensions={1} | all-to-all | bytes 4194304 | tf_op jit(solution)/shard_map/all_to_all | solution.py:261
  425.3 2.5 copy.121
  427.8 12.4 %all-to-all-start.5 = ((bf16[32,16,2048]{2,1,0:T(8,128)(2,1)}), bf16[32,16,2048]{2,1,0:T(8,128)(2,1)S(1)}, u32[]{:S(2)}, u32[]{:S(2)}) async-start(bf16[32,16,2048]{2,1,0:T(8,128)(2,1)} %copy.121), calls=%async_computation.5 | async-start | bytes 4194304 | tf_op jit(solution)/shard_map/all_to_all | solution.py:262
  442.5 46.8 %all-to-all-done.5 = bf16[32,16,2048]{2,1,0:T(8,128)(2,1)S(1)} async-done(((bf16[32,16,2048]{2,1,0:T(8,128)(2,1)}), bf16[32,16,2048]{2,1,0:T(8,128)(2,1)S(1)}, u32[]{:S(2)}, u32[]{:S(2)}) %all-to-all-start.5) | async-done | bytes 2097184 | tf_op jit(solution)/shard_map/all_to_all | solution.py:262
  489.4 1.8 fusion.35
  (125 shorter events, 40.7 us)
Async XLA Ops:
  7.2 13.0 %copy-start.4 = (s32[2]{0:T(128)S(1)}, s32[2]{0:T(128)}, u32[]{:S(2)}) copy-start(s32[2]{0:T(128)} %param.16) | copy-start | bytes 28
  7.2 72.8 %all-gather.4.cloned.1.call-start = ((), (), s32[]{:S(2)}) async-start(), calls=%async_computation.6 | async-start | bytes 3244032 | tf_op jit(solution)/shard_map/all_gather | solution.py:118
  12.7 26.2 %all-to-all-start = ((bf16[8,32,2048]{2,1,0:T(8,128)(2,1)}), bf16[8,32,2048]{2,1,0:T(8,128)(2,1)S(1)}, u32[]{:S(2)}, u32[]{:S(2)}) async-start(bf16[8,32,2048]{2,1,0:T(8,128)(2,1)} %broadcast_in_dim.89), calls=%async_computation | async-start | bytes 2097152 | tf_op jit(solution)/shard_map/all_to_all | solution.py:100
  20.1 204.4 %all-gather.6.cloned.1.call-start = ((), (), s32[]{:S(2)}) async-start(), calls=%async_computation.7 | async-start | bytes 4325376 | tf_op jit(solution)/shard_map/all_gather | solution.py:171
  38.8 41.2 %copy-start.2 = (bf16[8,32,2048]{2,1,0:T(8,128)(2,1)}, bf16[8,32,2048]{2,1,0:T(8,128)(2,1)S(1)}, u32[]{:S(2)}) copy-start(bf16[8,32,2048]{2,1,0:T(8,128)(2,1)S(1)} %all-to-all-done) | copy-start | bytes 3145732
  80.0 3.5 copy-start.8
  80.0 5.1 %copy-start.1 = (bf16[1,2048,768]{2,1,0:T(8,128)(2,1)S(1)}, bf16[1,2048,768]{2,1,0:T(8,128)(2,1)}, u32[]{:S(2)}) copy-start(bf16[1,2048,768]{2,1,0:T(8,128)(2,1)} %param.26) | copy-start | bytes 9437188
  83.4 0.9 copy-start.3
  85.0 6.1 %copy-start.6 = (s32[32,8]{0,1:T(8,128)S(1)}, s32[32,8]{0,1:T(8,128)}, u32[]{:S(2)}) copy-start(s32[32,8]{0,1:T(8,128)} %param.17) | copy-start | bytes 3076
  85.0 177.2 %all-gather.8.cloned.1.call-start = ((), (), s32[]{:S(2)}) async-start(), calls=%async_computation.8 | async-start | bytes 2162688 | tf_op jit(solution)/shard_map/all_gather | solution.py:202
  88.1 5.7 %copy-start.9 = (f32[128]{0:T(128)S(1)}, f32[128]{0:T(128)}, u32[]{:S(2)}) copy-start(f32[128]{0:T(128)} %param.22) | copy-start | bytes 1540
  88.1 136.5 %collective-permute-start = (bf16[1,2048,768]{1,2,0:T(8,128)(2,1)}, bf16[1,2048,768]{1,2,0:T(8,128)(2,1)}, u32[]{:S(2)}, u32[]{:S(2)}) collective-permute-start(bf16[1,2048,768]{1,2,0:T(8,128)(2,1)} %copy.106), channel_id=1, source_target_pairs={{0,1},{1,0},{2,3},{3,2},{4,5},{5,4},{6,7},{7,6},{8,9},{9,8},{10,11... | collective-permute-start | bytes 9437192 | tf_op jit(solution)/shard_map/ppermute | solution.py:172
  90.6 134.0 %collective-permute-start.1 = (bf16[1,384,2048]{2,1,0:T(8,128)(2,1)}, bf16[1,384,2048]{2,1,0:T(8,128)(2,1)}, u32[]{:S(2)}, u32[]{:S(2)}) collective-permute-start(bf16[1,384,2048]{2,1,0:T(8,128)(2,1)} %param.27), channel_id=1, source_target_pairs={{0,1},{1,0},{2,3},{3,2},{4,5},{5,4},{6,7},{7,6},{8,9},{9,8},{10,11... | collective-permute-start | bytes 4718600 | tf_op jit(solution)/shard_map/ppermute | solution.py:173
  265.6 22.0 %copy-start = (bf16[32,2048]{1,0:T(8,128)(2,1)S(1)}, bf16[32,2048]{1,0:T(8,128)(2,1)}, u32[]{:S(2)}) copy-start(bf16[32,2048]{1,0:T(8,128)(2,1)} %param.15) | copy-start | bytes 393220
  265.6 22.2 %copy-start.5 = (f32[2048]{0:T(1024)S(1)}, f32[2048]{0:T(1024)}, u32[]{:S(2)}) copy-start(f32[2048]{0:T(1024)} %param.25) | copy-start | bytes 24580
  265.6 21.9 %all-to-all-start.1 = ((bf16[8,32,2048]{2,1,0:T(8,128)(2,1)}), bf16[8,32,2048]{2,1,0:T(8,128)(2,1)S(1)}, u32[]{:S(2)}, u32[]{:S(2)}) async-start(bf16[8,32,2048]{2,1,0:T(8,128)(2,1)} %bitcast.12), calls=%async_computation.1 | async-start | bytes 2097152 | tf_op jit(solution)/shard_map/all_to_all | solution.py:205
  380.2 6.3 %copy-start.10 = (bf16[1,384,2048]{2,1,0:T(8,128)(2,1)S(1)}, bf16[1,384,2048]{2,1,0:T(8,128)(2,1)}, u32[]{:S(2)}) copy-start(bf16[1,384,2048]{2,1,0:T(8,128)(2,1)} %param.27) | copy-start | bytes 4718596
  427.8 12.4 %copy-start.7 = (f32[32,8]{0,1:T(8,128)S(1)}, f32[32,8]{0,1:T(8,128)}, u32[]{:S(2)}) copy-start(f32[32,8]{0,1:T(8,128)} %param.18) | copy-start | bytes 3076
  427.8 61.6 %all-to-all-start.5 = ((bf16[32,16,2048]{2,1,0:T(8,128)(2,1)}), bf16[32,16,2048]{2,1,0:T(8,128)(2,1)S(1)}, u32[]{:S(2)}, u32[]{:S(2)}) async-start(bf16[32,16,2048]{2,1,0:T(8,128)(2,1)} %copy.121), calls=%async_computation.5 | async-start | bytes 4194304 | tf_op jit(solution)/shard_map/all_to_all | solution.py:262
Sparse Core Ops, SparseCore 0:
  10.4 69.5 all-gather.3
  85.2 66.5 all-gather.5
  153.6 64.2 all-gather.7

commit v3 on v2

--- a/solution.py
+++ b/solution.py
@@ -115,8 +115,15 @@
     )
     kv_local = jnp.concatenate([key_cols, value_column_block], axis=1)
     q_width = q_dev * HEAD_SIZE
-    weights_all = lax.all_gather(
-        jnp.concatenate([q_weight, kv_local], axis=1), "ctx", axis=0, tiled=True
+    pair = [(i, i ^ 1) for i in range(expert_count)]
+    rows_half = expert_in.shape[1] // 2
+    weights_all, partner_out = lax.optimization_barrier(
+        (
+            lax.all_gather(
+                jnp.concatenate([q_weight, kv_local], axis=1), "ctx", axis=0, tiled=True
+            ),
+            lax.ppermute(expert_out, "exp", pair),
+        )
     )
     projected = jnp.dot(normed, weights_all, preferred_element_type=jnp.float32)
     q_raw = projected[:, :q_width]
@@ -165,12 +172,10 @@
         jnp.zeros((tok_ctx, key_value_share, group_dev, HEAD_SIZE), jnp.float32),
         jnp.zeros((key_value_share, group_dev, tok_ctx), jnp.float32),
     )
-    pair = [(i, i ^ 1) for i in range(expert_count)]
-    every_kv, partner_in, partner_out = lax.optimization_barrier(
+    every_kv, partner_in_low = lax.optimization_barrier(
         (
             lax.all_gather(key_values, "ctx", axis=1, tiled=True),
-            lax.ppermute(expert_in, "exp", pair),
-            lax.ppermute(expert_out, "exp", pair),
+            lax.ppermute(expert_in[:, :rows_half], "exp", pair),
         )
     )
     total_rows = every_kv.shape[1]
@@ -180,7 +185,12 @@
         block_kv = lax.dynamic_slice_in_dim(every_kv, step_no * chunk, chunk, 1)
         return attend(state_now, block_kv, step_no * chunk)
 
-    final_state = lax.fori_loop(0, total_rows // chunk, turn, initial)
+    final_state, partner_in_high = lax.optimization_barrier(
+        (
+            lax.fori_loop(0, total_rows // chunk, turn, initial),
+            lax.ppermute(expert_in[:, rows_half:], "exp", pair),
+        )
+    )
     context = (
         (final_state[0] / jnp.transpose(final_state[1], (2, 0, 1))[..., None])
         .astype(jnp.bfloat16)
@@ -239,6 +249,7 @@
     )
     experts_ctx = EXPERTS // count_ctx
     share = capacity // slices
+    partner_in = jnp.concatenate([partner_in_low, partner_in_high], axis=1)
     expert_in_both = jnp.concatenate([expert_in, partner_in], axis=0)
     expert_out_both = jnp.concatenate([expert_out, partner_out], axis=0)
     outgoing = outgoing.reshape(count_ctx, experts_ctx * capacity, MODEL_WIDTH)

time: 500 us -> 458 us (0.916)
  waiting for transfers between devices: 249 us -> 203 us
  local copies, waits for them, and re-layouts: 25.3 us -> 31.5 us
    ppermute x1, waiting for transfers between devices: 130 us -> 33.6 us  [shards(): lax.ppermute(expert_out, 'exp', pair)]
    ppermute x1 -> x2, waiting for transfers between devices: 0.01 us -> 51.5 us  [the longest x1 51.5 us: shards(): lax.ppermute(expert_in[:, :rows_half], 'exp', pair)]
    all_gather x1, waiting for transfers between devices: 0.02 us -> 28.4 us  [shards(): lax.all_gather(o_weight, 'ctx', axis=1, tiled=True)]
    all_gather x1, waiting for transfers between devices: 41.2 us -> 23.5 us  [shards(): lax.all_gather(jnp.concatenate([q_weight, kv_local], axis=1), 'ctx', axis...]
    all_to_all x1, waiting for transfers between devices: 16.1 us -> 0.01 us  [shards(): lax.all_to_all(jnp.broadcast_to(normed_own[None], (expert_count,) + norme...]
  transfers between devices with their start and end apart: 8 -> 9, of which waited for: 5 -> 7; matrix products, arithmetic and copies ran while one was open for 10% -> 12% of each run, Pallas kernels for 0% -> 0%
where the time goes in v3:
time: 458 us; the launch traced here: 456 us
  waiting for transfers between devices  203 us (44%)
  blocking collectives  112 us (24%)
  matrix products  47.9 us (10%)
  local copies, waits for them, and re-layouts  31.5 us (7%)
  starting transfers between devices  29.5 us (6%)
  other arithmetic  16.5 us (4%)
  between operations  15.5 us (3%)
    all_to_all x1, blocking collectives, shards(): lax.all_to_all(outgoing, 'ctx', split_axis=0, concat_axis=0, tiled=True)  55.8 us
    ppermute x1, waiting for transfers between devices, shards(): lax.ppermute(expert_in[:, :rows_half], 'exp', pair)  51.5 us
    all_to_all x1, waiting for transfers between devices, shards(): lax.all_to_all(came_back.reshape(count_ctx, experts_ctx * capacity, MODEL...  46.8 us
    ppermute x1, waiting for transfers between devices, shards(): lax.ppermute(expert_out, 'exp', pair)  33.6 us
    all_to_all x1, blocking collectives, shards(): lax.all_to_all(landed, 'exp', split_axis=1, concat_axis=1, tiled=True)  28.7 us
    all_gather x1, waiting for transfers between devices, shards(): lax.all_gather(o_weight, 'ctx', axis=1, tiled=True)  28.4 us
    all_to_all x1, blocking collectives, shards(): lax.all_to_all(produced, 'exp', split_axis=1, concat_axis=1, tiled=True)  27.4 us
    all_gather x1, waiting for transfers between devices, shards(): lax.all_gather(jnp.concatenate([q_weight, kv_local], axis=1), 'ctx', axis...  23.5 us
  transfers between devices with their start and end apart: 9, of which 7 were waited for; matrix products, arithmetic and copies ran while one was open for 12% of the time, Pallas kernels for 0%

profile of v3, /device:TPU:1, one launch (start us, length us, event | category | flops | bytes accessed | tf_op | source)
XLA Modules:
  0.0 456.2 jit_solution(15234685198489687409)
XLA Ops:
  9.5 3.6 collective-permute-start
  16.3 4.2 all-to-all-start
  23.1 33.6 %collective-permute-done = bf16[1,384,2048]{2,1,0:T(8,128)(2,1)S(1)} collective-permute-done((bf16[1,384,2048]{2,1,0:T(8,128)(2,1)}, bf16[1,384,2048]{2,1,0:T(8,128)(2,1)S(1)}, u32[]{:S(2)}, u32[]{:S(2)}) %collective-permute-start) | collective-permute-done | bytes 1572896 | tf_op jit(solution)/shard_map/ppermute | solution.py:125
  56.7 23.5 %all-gather.4.cloned.1.call-done = bf16[2048,768]{1,0:T(8,128)(2,1)} async-done(((bf16[64,768]{1,0:T(8,128)(2,1)}), bf16[2048,768]{1,0:T(8,128)(2,1)}) %all-gather.4.cloned.1.call-update) | async-done | bytes 3145744 | tf_op jit(solution)/shard_map/all_gather | solution.py:122
  80.2 2.9 fusion.91
  84.8 3.2 copy.112
  88.0 2.5 fusion.88
  90.7 2.2 collective-permute-start.1
  97.1 51.5 %collective-permute-done.1 = bf16[1,1024,768]{1,2,0:T(8,128)(2,1)} collective-permute-done((bf16[1,1024,768]{1,2,0:T(8,128)(2,1)}, bf16[1,1024,768]{1,2,0:T(8,128)(2,1)}, u32[]{:S(2)}, u32[]{:S(2)}) %collective-permute-start.1) | collective-permute-done | bytes 1572896 | tf_op jit(solution)/shard_map/ppermute | solution.py:178
  148.6 2.8 all-gather.6.cloned.1.call-done
  151.3 37.5 %while.21 = (s32[]{:T(128)}, f32[256,1,4,128]{0,3,2,1:T(8,128)S(1)}, f32[1,4,256]{2,1,0:T(4,128)S(1)}, bf16[2,8192,128]{2,1,0:T(8,128)(2,1)}, s32[2]{0:T(128)S(1...) while((s32[]{:T(128)}, ...), condition=%wide.region_5.6_spmd.clone.clone.clone, body=%wide.region_3.5_spmd.clone.clone.clone.sunk | while | flops 543215872 | bytes 6590702 | solution.py:190
  152.4 2.1 convert_reduce_fusion.4
  157.1 2.1 convert_reduce_fusion.4
  161.8 2.1 convert_reduce_fusion.4
  166.5 2.1 convert_reduce_fusion.4
  175.9 2.1 convert_reduce_fusion.4
  189.0 28.4 %all-gather.8.cloned.1.call-done = bf16[512,2048]{0,1:T(8,128)(2,1)} async-done(((bf16[512,64]{0,1:T(8,128)(2,1)}), bf16[512,2048]{0,1:T(8,128)(2,1)}) %all-gather.8.cloned.1.call-update) | async-done | bytes 2097168 | tf_op jit(solution)/shard_map/all_gather | solution.py:212
  217.4 3.4 convolution_convert_fusion.1
  220.7 6.3 %all-to-all-start.1 = ((bf16[8,32,2048]{2,1,0:T(8,128)(2,1)}), bf16[8,32,2048]{2,1,0:T(8,128)(2,1)S(1)}, u32[]{:S(2)}, u32[]{:S(2)}) async-start(bf16[8,32,2048]{2,1,0:T(8,128)(2,1)} %bitcast.12), calls=%async_computation.1 | async-start | bytes 2097152 | tf_op jit(solution)/shard_map/all_to_all | solution.py:215
  227.5 16.2 %all-to-all-done.1 = bf16[8,32,2048]{2,1,0:T(8,128)(2,1)S(1)} async-done(((bf16[8,32,2048]{2,1,0:T(8,128)(2,1)}), bf16[8,32,2048]{2,1,0:T(8,128)(2,1)S(1)}, u32[]{:S(2)}, u32[]{:S(2)}) %all-to-all-start.1) | async-done | bytes 1048608 | tf_op jit(solution)/shard_map/all_to_all | solution.py:215
  245.1 55.8 %all_to_all.30 = bf16[32,16,2048]{2,1,0:T(8,128)(2,1)S(1)} all-to-all(bf16[32,16,2048]{2,1,0:T(8,128)(2,1)S(1)} %bitcast.106), channel_id=1, replica_groups=mesh['ctx'=32,'exp'=8] {'ctx'}, dimensions={0} | all-to-all | bytes 4194304 | tf_op jit(solution)/shard_map/all_to_all | solution.py:256
  302.1 2.2 copy.123
  304.3 28.7 %all_to_all.31 = bf16[32,8,2,2048]{3,2,0,1:T(2,128)(2,1)S(1)} all-to-all(bf16[32,8,2,2048]{3,2,0,1:T(2,128)(2,1)S(1)} %copy.123), channel_id=1, replica_groups=mesh['ctx'=32,'exp'=8] {'exp'}, dimensions={1} | all-to-all | bytes 4194304 | tf_op jit(solution)/shard_map/all_to_all | solution.py:258
  333.0 3.6 copy.124
  336.5 4.3 reshape.550
  340.8 5.9 %fusion.38 = f32[2,512,768]{1,2,0:T(8,128)S(1)} fusion(bf16[512,2048,1]{1,0,2:T(8,128)(2,1)} %reshape.550, bf16[1,1024,768]{1,2,0:T(8,128)(2,1)} %collective-permute-done.2, bf16[1,1024,768]{1,2,0:T(8,128)(2,1)} %collective-permute-done.1, bf16[1,2048,768]{1,2,0:T(8,128)(2,1)S(1)} %copy-done.1), kind=kOutput, calls=%fused_computation.66 | convolution fusion | flops 3240099840 | bytes 11534336 | tf_op jit(solution)/shard_map/td,sdf->stf/dot_general | solution.py:260
  346.8 3.9 convert_reduce_fusion.1
  350.7 3.2 reshape.533
  355.6 27.4 %all_to_all.32 = bf16[32,8,2,2048]{3,2,0,1:T(2,128)(2,1)S(1)} all-to-all(bf16[32,8,2,2048]{3,2,0,1:T(2,128)(2,1)S(1)} %copy.126), channel_id=1, replica_groups=mesh['ctx'=32,'exp'=8] {'exp'}, dimensions={1} | all-to-all | bytes 4194304 | tf_op jit(solution)/shard_map/all_to_all | solution.py:272
  383.9 2.5 copy.128
  386.4 12.2 %all-to-all-start.5 = ((bf16[32,16,2048]{2,1,0:T(8,128)(2,1)}), bf16[32,16,2048]{2,1,0:T(8,128)(2,1)S(1)}, u32[]{:S(2)}, u32[]{:S(2)}) async-start(bf16[32,16,2048]{2,1,0:T(8,128)(2,1)} %copy.128), calls=%async_computation.5 | async-start | bytes 4194304 | tf_op jit(solution)/shard_map/all_to_all | solution.py:273
  401.0 46.8 %all-to-all-done.5 = bf16[32,16,2048]{2,1,0:T(8,128)(2,1)S(1)} async-done(((bf16[32,16,2048]{2,1,0:T(8,128)(2,1)}), bf16[32,16,2048]{2,1,0:T(8,128)(2,1)S(1)}, u32[]{:S(2)}, u32[]{:S(2)}) %all-to-all-start.5) | async-done | bytes 2097184 | tf_op jit(solution)/shard_map/all_to_all | solution.py:273
  (132 shorter events, 49.0 us)
Async XLA Ops:
  7.2 13.4 %copy-start.4 = (s32[2]{0:T(128)S(1)}, s32[2]{0:T(128)}, u32[]{:S(2)}) copy-start(s32[2]{0:T(128)} %param.16) | copy-start | bytes 28
  7.2 73.0 %all-gather.4.cloned.1.call-start = ((), (), s32[]{:S(2)}) async-start(), calls=%async_computation.6 | async-start | bytes 3244032 | tf_op jit(solution)/shard_map/all_gather | solution.py:122
  9.5 47.2 %collective-permute-start = (bf16[1,384,2048]{2,1,0:T(8,128)(2,1)}, bf16[1,384,2048]{2,1,0:T(8,128)(2,1)S(1)}, u32[]{:S(2)}, u32[]{:S(2)}) collective-permute-start(bf16[1,384,2048]{2,1,0:T(8,128)(2,1)} %param.27), channel_id=1, source_target_pairs={{0,1},{1,0},{2,3},{3,2},{4,5},{5,4},{6,7},{7,6},{8,9},{9,8},{10,11... | collective-permute-start | bytes 4718600 | tf_op jit(solution)/shard_map/ppermute | solution.py:125
  16.3 63.9 %all-to-all-start = ((bf16[8,32,2048]{2,1,0:T(8,128)(2,1)}), bf16[8,32,2048]{2,1,0:T(8,128)(2,1)S(1)}, u32[]{:S(2)}, u32[]{:S(2)}) async-start(bf16[8,32,2048]{2,1,0:T(8,128)(2,1)} %broadcast_in_dim.89), calls=%async_computation | async-start | bytes 2097152 | tf_op jit(solution)/shard_map/all_to_all | solution.py:100
  20.5 130.8 %all-gather.6.cloned.1.call-start = ((), (), s32[]{:S(2)}) async-start(), calls=%async_computation.7 | async-start | bytes 4325376 | tf_op jit(solution)/shard_map/all_gather | solution.py:177
  56.7 26.4 %copy-start.11 = (bf16[1,384,2048]{2,1,0:T(8,128)(2,1)}, bf16[1,384,2048]{2,1,0:T(8,128)(2,1)S(1)}, u32[]{:S(2)}) copy-start(bf16[1,384,2048]{2,1,0:T(8,128)(2,1)S(1)} %collective-permute-done) | copy-start | bytes 4718596
  80.2 3.1 copy-start.8
  83.1 0.9 copy-start.3
  84.8 132.6 %all-gather.8.cloned.1.call-start = ((), (), s32[]{:S(2)}) async-start(), calls=%async_computation.8 | async-start | bytes 2162688 | tf_op jit(solution)/shard_map/all_gather | solution.py:212
  88.0 2.7 copy-start
  88.0 5.7 %copy-start.6 = (s32[32,8]{0,1:T(8,128)S(1)}, s32[32,8]{0,1:T(8,128)}, u32[]{:S(2)}) copy-start(s32[32,8]{0,1:T(8,128)} %param.17) | copy-start | bytes 3076
  90.7 5.7 %copy-start.9 = (f32[128]{0:T(128)S(1)}, f32[128]{0:T(128)}, u32[]{:S(2)}) copy-start(f32[128]{0:T(128)} %param.22) | copy-start | bytes 1540
  90.7 57.8 %collective-permute-start.1 = (bf16[1,1024,768]{1,2,0:T(8,128)(2,1)}, bf16[1,1024,768]{1,2,0:T(8,128)(2,1)}, u32[]{:S(2)}, u32[]{:S(2)}) collective-permute-start(bf16[1,1024,768]{1,2,0:T(8,128)(2,1)} %get-tuple-element.394), channel_id=1, source_target_pairs={{0,1},{1,0},{2,3},{3,2},{4,5},{5,4},{6,7},{7,6},{8,9},{9,8},{10,11... | collective-permute-start | bytes 4718600 | tf_op jit(solution)/shard_map/ppermute | solution.py:178
  93.0 95.9 %collective-permute-start.2 = (bf16[1,1024,768]{1,2,0:T(8,128)(2,1)}, bf16[1,1024,768]{1,2,0:T(8,128)(2,1)}, u32[]{:S(2)}, u32[]{:S(2)}) collective-permute-start(bf16[1,1024,768]{1,2,0:T(8,128)(2,1)} %get-tuple-element.393), channel_id=1, source_target_pairs={{0,1},{1,0},{2,3},{3,2},{4,5},{5,4},{6,7},{7,6},{8,9},{9,8},{10,11... | collective-permute-start | bytes 4718600 | tf_op jit(solution)/shard_map/ppermute | solution.py:191
  220.7 23.2 %copy-start.2 = (bf16[32,2048]{1,0:T(8,128)(2,1)S(1)}, bf16[32,2048]{1,0:T(8,128)(2,1)}, u32[]{:S(2)}) copy-start(bf16[32,2048]{1,0:T(8,128)(2,1)} %param.15) | copy-start | bytes 393220
  220.7 23.4 %copy-start.5 = (f32[2048]{0:T(1024)S(1)}, f32[2048]{0:T(1024)}, u32[]{:S(2)}) copy-start(f32[2048]{0:T(1024)} %param.25) | copy-start | bytes 24580
  220.7 23.0 %all-to-all-start.1 = ((bf16[8,32,2048]{2,1,0:T(8,128)(2,1)}), bf16[8,32,2048]{2,1,0:T(8,128)(2,1)S(1)}, u32[]{:S(2)}, u32[]{:S(2)}) async-start(bf16[8,32,2048]{2,1,0:T(8,128)(2,1)} %bitcast.12), calls=%async_computation.1 | async-start | bytes 2097152 | tf_op jit(solution)/shard_map/all_to_all | solution.py:215
  336.5 4.3 copy-start.1
  340.8 5.9 %copy-start.10 = (bf16[1,384,2048]{2,1,0:T(8,128)(2,1)S(1)}, bf16[1,384,2048]{2,1,0:T(8,128)(2,1)}, u32[]{:S(2)}) copy-start(bf16[1,384,2048]{2,1,0:T(8,128)(2,1)} %param.27) | copy-start | bytes 4718596
  340.8 5.9 %copy-start.12 = (bf16[1,384,2048]{2,1,0:T(8,128)(2,1)S(1)}, bf16[1,384,2048]{2,1,0:T(8,128)(2,1)}, u32[]{:S(2)}) copy-start(bf16[1,384,2048]{2,1,0:T(8,128)(2,1)} %copy-done.11) | copy-start | bytes 4718596
  386.4 12.3 %copy-start.7 = (f32[32,8]{0,1:T(8,128)S(1)}, f32[32,8]{0,1:T(8,128)}, u32[]{:S(2)}) copy-start(f32[32,8]{0,1:T(8,128)} %param.18) | copy-start | bytes 3076
  386.4 61.5 %all-to-all-start.5 = ((bf16[32,16,2048]{2,1,0:T(8,128)(2,1)}), bf16[32,16,2048]{2,1,0:T(8,128)(2,1)S(1)}, u32[]{:S(2)}, u32[]{:S(2)}) async-start(bf16[32,16,2048]{2,1,0:T(8,128)(2,1)} %copy.128), calls=%async_computation.5 | async-start | bytes 4194304 | tf_op jit(solution)/shard_map/all_to_all | solution.py:273
Sparse Core Ops, SparseCore 0:
  10.4 69.7 all-gather.3
  84.9 66.4 all-gather.5
  153.2 64.1 all-gather.7

commit v4 on v3

--- a/solution.py
+++ b/solution.py
@@ -120,12 +120,16 @@
     weights_all, partner_out = lax.optimization_barrier(
         (
             lax.all_gather(
-                jnp.concatenate([q_weight, kv_local], axis=1), "ctx", axis=0, tiled=True
+                jnp.concatenate([q_weight, kv_local, o_weight.T], axis=1), "ctx", axis=0, tiled=True
             ),
             lax.ppermute(expert_out, "exp", pair),
         )
     )
-    projected = jnp.dot(normed, weights_all, preferred_element_type=jnp.float32)
+    kv_width = kv_local.shape[1]
+    projected = jnp.dot(
+        normed, weights_all[:, : q_width + kv_width], preferred_element_type=jnp.float32
+    )
+    o_turned = weights_all[:, q_width + kv_width :]
     q_raw = projected[:, :q_width]
     key_value_plain = projected[:, q_width:]
     queries = rotate(
@@ -207,10 +211,8 @@
         every_kv, (0, block_start(2 * my_ctx + 1), col_offset), (2, half_rows, column_share)
     )
     cache = jnp.concatenate([first_part, second_part], axis=1)
-    attn_part = jnp.dot(
-        context,
-        lax.all_gather(o_weight, "ctx", axis=1, tiled=True),
-        preferred_element_type=jnp.float32,
+    attn_part = lax.dot_general(
+        context, o_turned, (((1,), (1,)), ((), ())), preferred_element_type=jnp.float32
     )
     attn_pieces = lax.all_to_all(
         attn_part.astype(jnp.bfloat16).reshape(expert_count, tok_dev, MODEL_WIDTH),
@@ -252,10 +254,8 @@
     partner_in = jnp.concatenate([partner_in_low, partner_in_high], axis=1)
     expert_in_both = jnp.concatenate([expert_in, partner_in], axis=0)
     expert_out_both = jnp.concatenate([expert_out, partner_out], axis=0)
-    outgoing = outgoing.reshape(count_ctx, experts_ctx * capacity, MODEL_WIDTH)
-    landed = lax.all_to_all(outgoing, "ctx", split_axis=0, concat_axis=0, tiled=True)
-    landed = landed.reshape(count_ctx, expert_count, share, MODEL_WIDTH)
-    arrived = lax.all_to_all(landed, "exp", split_axis=1, concat_axis=1, tiled=True)
+    outgoing = outgoing.reshape(devices, share, MODEL_WIDTH)
+    arrived = lax.all_to_all(outgoing, ("ctx", "exp"), split_axis=0, concat_axis=0, tiled=True)
     tokens_in = arrived.reshape(-1, MODEL_WIDTH)
     gate_up = jnp.einsum(
         "td,sdf->stf", tokens_in, expert_in_both, preferred_element_type=jnp.float32
@@ -267,16 +267,9 @@
     produced = (
         jnp.sum(produced, axis=0, dtype=jnp.float32)
         .astype(jnp.bfloat16)
-        .reshape(count_ctx, expert_count, share, MODEL_WIDTH)
-    )
-    came_back = lax.all_to_all(produced, "exp", split_axis=1, concat_axis=1, tiled=True)
-    returned = lax.all_to_all(
-        came_back.reshape(count_ctx, experts_ctx * capacity, MODEL_WIDTH),
-        "ctx",
-        split_axis=0,
-        concat_axis=0,
-        tiled=True,
-    )
+        .reshape(devices, share, MODEL_WIDTH)
+    )
+    returned = lax.all_to_all(produced, ("ctx", "exp"), split_axis=0, concat_axis=0, tiled=True)
     slice_sum = returned.reshape(EXPERTS * capacity, MODEL_WIDTH).astype(jnp.float32)
     gate_hot = slot_hot.astype(jnp.float32) * gates.reshape(-1)[:, None]
     combiner = jnp.einsum(

time: 458 us -> 377 us (0.82)
  blocking collectives: 112 us -> 61.5 us
  waiting for transfers between devices: 203 us -> 186 us
  local copies, waits for them, and re-layouts: 31.5 us -> 23.6 us
  starting transfers between devices: 29.5 us -> 24.2 us
    all_to_all x3 -> x1, blocking collectives: 112 us -> 61.5 us  [shards(): lax.all_to_all(outgoing, ('ctx', 'exp'), split_axis=0, concat_axis=0, til...]
    all_gather x2 -> x1, waiting for transfers between devices: 51.9 us -> 17.4 us  [shards(): lax.all_gather(jnp.concatenate([q_weight, kv_local, o_weight.T], axis=1),...]
    ppermute x1, waiting for transfers between devices: 33.6 us -> 43.6 us  [shards(): lax.ppermute(expert_out, 'exp', pair)]
    all_to_all x3 -> x0, local copies, waits for them, and re-layouts: 5.63 us -> none  [the longest x1 3.59 us: shards(): lax.all_to_all(landed, 'exp', split_axis=1, concat_axis=1, tiled=True)]
    all_to_all x1, starting transfers between devices: 12.2 us -> 6.88 us  [shards(): lax.all_to_all(produced, ('ctx', 'exp'), split_axis=0, concat_axis=0, til...]
  transfers between devices with their start and end apart: 9 -> 8, of which waited for: 7 -> 7; matrix products, arithmetic and copies ran while one was open for 12% -> 14% of each run, Pallas kernels for 0% -> 0%
where the time goes in v4:
time: 377 us; the launch traced here: 376 us
  waiting for transfers between devices  186 us (49%)
  blocking collectives  61.5 us (16%)
  matrix products  48 us (13%)
  starting transfers between devices  24.2 us (6%)
  local copies, waits for them, and re-layouts  23.6 us (6%)
  other arithmetic  16.5 us (4%)
  between operations  15.7 us (4%)
    all_to_all x1, blocking collectives, shards(): lax.all_to_all(outgoing, ('ctx', 'exp'), split_axis=0, concat_axis=0, til...  61.5 us
    all_to_all x1, waiting for transfers between devices, shards(): lax.all_to_all(produced, ('ctx', 'exp'), split_axis=0, concat_axis=0, til...  50.5 us
    ppermute x1, waiting for transfers between devices, shards(): lax.ppermute(expert_in[:, :rows_half], 'exp', pair)  49.6 us
    ppermute x1, waiting for transfers between devices, shards(): lax.ppermute(expert_out, 'exp', pair)  43.6 us
    all_gather x1, waiting for transfers between devices, shards(): lax.all_gather(jnp.concatenate([q_weight, kv_local, o_weight.T], axis=1),...  17.4 us
    dot_general x8, matrix products, attend(): jnp.einsum('qkgd,skd->kgqs', query_groups, key_part, preferred_element_ty...  16.6 us
    all_to_all x1, waiting for transfers between devices, shards(): lax.all_to_all(attn_part.astype(jnp.bfloat16).reshape(expert_count, tok_d...  16.2 us
    dot_general x8, matrix products, attend(): jnp.einsum('kgqs,skd->qkgd', weights, value_part, preferred_element_type=...  12 us
  transfers between devices with their start and end apart: 8, of which 7 were waited for; matrix products, arithmetic and copies ran while one was open for 14% of the time, Pallas kernels for 0%

profile of v4, /device:TPU:1, one launch (start us, length us, event | category | flops | bytes accessed | tf_op | source)
XLA Modules:
  0.0 376.1 jit_solution(14686212503209090353)
XLA Ops:
  9.6 3.6 collective-permute-start
  16.4 4.2 %all-to-all-start = ((bf16[8,32,2048]{2,1,0:T(8,128)(2,1)}), bf16[8,32,2048]{2,1,0:T(8,128)(2,1)S(1)}, u32[]{:S(2)}, u32[]{:S(2)}) async-start(bf16[8,32,2048]{2,1,0:T(8,128)(2,1)} %broadcast_in_dim.89), calls=%async_computation | async-start | bytes 2097152 | tf_op jit(solution)/shard_map/all_to_all | solution.py:100
  23.1 43.6 %collective-permute-done = bf16[1,384,2048]{2,1,0:T(8,128)(2,1)S(1)} collective-permute-done((bf16[1,384,2048]{2,1,0:T(8,128)(2,1)}, bf16[1,384,2048]{2,1,0:T(8,128)(2,1)S(1)}, u32[]{:S(2)}, u32[]{:S(2)}) %collective-permute-start) | collective-permute-done | bytes 1572896 | tf_op jit(solution)/shard_map/ppermute | solution.py:125
  66.7 17.4 %all-gather.3.cloned.1.call-done = bf16[2048,1280]{1,0:T(8,128)(2,1)} async-done(((bf16[64,1280]{1,0:T(8,128)(2,1)}), bf16[2048,1280]{1,0:T(8,128)(2,1)}) %all-gather.3.cloned.1.call-update) | async-done | bytes 5242896 | tf_op jit(solution)/shard_map/all_gather | solution.py:122
  84.2 3.3 all-to-all-done
  87.5 2.9 fusion.37
  92.0 3.2 copy.52
  95.2 2.3 fusion.91
  98.1 2.7 collective-permute-start.2
  104.1 49.6 %collective-permute-done.1 = bf16[1,1024,768]{1,2,0:T(8,128)(2,1)} collective-permute-done((bf16[1,1024,768]{1,2,0:T(8,128)(2,1)}, bf16[1,1024,768]{1,2,0:T(8,128)(2,1)}, u32[]{:S(2)}, u32[]{:S(2)}) %collective-permute-start.1) | collective-permute-done | bytes 1572896 | tf_op jit(solution)/shard_map/ppermute | solution.py:182
  153.7 5.5 %all-gather.5.cloned.1.call-done = bf16[2,8192,128]{2,1,0:T(8,128)(2,1)} async-done(((bf16[2,256,128]{2,1,0:T(8,128)(2,1)}), bf16[2,8192,128]{2,1,0:T(8,128)(2,1)}) %all-gather.5.cloned.1.call-update) | async-done | bytes 4194320 | tf_op jit(solution)/shard_map/all_gather | solution.py:181
  159.2 37.4 %while.21 = (s32[]{:T(128)}, f32[256,1,4,128]{0,3,2,1:T(8,128)S(1)}, f32[1,4,256]{2,1,0:T(4,128)S(1)}, bf16[2,8192,128]{2,1,0:T(8,128)(2,1)}, s32[2]{0:T(128)S(1...) while((s32[]{:T(128)}, ...), condition=%wide.region_5.6_spmd.clone.clone.clone, body=%wide.region_3.5_spmd.clone.clone.clone.sunk | while | flops 543215872 | bytes 6590702 | solution.py:194
  160.2 2.1 convert_reduce_fusion.4
  164.9 2.1 convert_reduce_fusion.4
  169.6 2.1 convert_reduce_fusion.4
  174.3 2.1 convert_reduce_fusion.4
  179.0 2.1 convert_reduce_fusion.4
  183.6 2.1 convert_reduce_fusion.4
  188.3 2.1 convert_reduce_fusion.4
  196.7 3.3 convolution_convert_fusion.1
  200.1 6.4 %all-to-all-start.1 = ((bf16[8,32,2048]{2,1,0:T(8,128)(2,1)}), bf16[8,32,2048]{2,1,0:T(8,128)(2,1)S(1)}, u32[]{:S(2)}, u32[]{:S(2)}) async-start(bf16[8,32,2048]{2,1,0:T(8,128)(2,1)} %bitcast.13), calls=%async_computation.1 | async-start | bytes 2097152 | tf_op jit(solution)/shard_map/all_to_all | solution.py:217
  207.0 16.2 %all-to-all-done.1 = bf16[8,32,2048]{2,1,0:T(8,128)(2,1)S(1)} async-done(((bf16[8,32,2048]{2,1,0:T(8,128)(2,1)}), bf16[8,32,2048]{2,1,0:T(8,128)(2,1)S(1)}, u32[]{:S(2)}, u32[]{:S(2)}) %all-to-all-start.1) | async-done | bytes 1048608 | tf_op jit(solution)/shard_map/all_to_all | solution.py:217
  224.5 2.6 reshape.524
  227.2 61.5 %all_to_all.20 = bf16[256,2,2048]{2,1,0:T(2,128)(2,1)} all-to-all(bf16[256,2,2048]{2,1,0:T(2,128)(2,1)} %reshape.524), channel_id=1, replica_groups=mesh['ctx'=32,'exp'=8] {'ctx','exp'}, dimensions={0} | all-to-all | bytes 4194304 | tf_op jit(solution)/shard_map/all_to_all | solution.py:258
  288.7 4.2 %reshape.542 = bf16[512,2048,1]{1,0,2:T(8,128)(2,1)} reshape(bf16[256,2,2048]{2,1,0:T(2,128)(2,1)} %all_to_all.20) | data formatting | bytes 4194304 | tf_op jit(solution)/shard_map/reshape | solution.py:259
  292.9 5.9 %fusion.41 = f32[2,512,768]{1,2,0:T(8,128)S(1)} fusion(bf16[512,2048,1]{1,0,2:T(8,128)(2,1)} %reshape.542, bf16[1,1024,768]{1,2,0:T(8,128)(2,1)} %collective-permute-done.2, bf16[1,1024,768]{1,2,0:T(8,128)(2,1)} %collective-permute-done.1, bf16[1,2048,768]{1,2,0:T(8,128)(2,1)S(1)} %copy-done.1), kind=kOutput, calls=%fused_computation.69 | convolution fusion | flops 3240099840 | bytes 11534336 | tf_op jit(solution)/shard_map/td,sdf->stf/dot_general | solution.py:260
  298.8 2.4 convert_reduce_fusion.1
  301.3 2.6 reshape.526
  303.9 6.9 %all-to-all-start.3 = ((bf16[256,2,2048]{2,1,0:T(2,128)(2,1)}), bf16[256,2,2048]{2,1,0:T(2,128)(2,1)S(1)}, u32[]{:S(2)}, u32[]{:S(2)}) async-start(bf16[256,2,2048]{2,1,0:T(2,128)(2,1)} %reshape.526), calls=%async_computation.3 | async-start | bytes 4194304 | tf_op jit(solution)/shard_map/all_to_all | solution.py:272
  313.2 50.5 %all-to-all-done.3 = bf16[256,2,2048]{2,1,0:T(2,128)(2,1)S(1)} async-done(((bf16[256,2,2048]{2,1,0:T(2,128)(2,1)}), bf16[256,2,2048]{2,1,0:T(2,128)(2,1)S(1)}, u32[]{:S(2)}, u32[]{:S(2)}) %all-to-all-start.3) | async-done | bytes 2097184 | tf_op jit(solution)/shard_map/all_to_all | solution.py:272
  363.7 2.2 reshape.527
  365.9 3.4 fusion.39
  (123 shorter events, 38.9 us)
Async XLA Ops:
  7.2 77.0 %all-gather.3.cloned.1.call-start = ((), (), s32[]{:S(2)}) async-start(), calls=%async_computation.4 | async-start | bytes 5406720 | tf_op jit(solution)/shard_map/all_gather | solution.py:122
  8.0 12.6 %copy-start.4 = (s32[2]{0:T(128)S(1)}, s32[2]{0:T(128)}, u32[]{:S(2)}) copy-start(s32[2]{0:T(128)} %param.16) | copy-start | bytes 28
  9.6 57.2 %collective-permute-start = (bf16[1,384,2048]{2,1,0:T(8,128)(2,1)}, bf16[1,384,2048]{2,1,0:T(8,128)(2,1)S(1)}, u32[]{:S(2)}, u32[]{:S(2)}) collective-permute-start(bf16[1,384,2048]{2,1,0:T(8,128)(2,1)} %param.27), channel_id=1, source_target_pairs={{0,1},{1,0},{2,3},{3,2},{4,5},{5,4},{6,7},{7,6},{8,9},{9,8},{10,11... | collective-permute-start | bytes 4718600 | tf_op jit(solution)/shard_map/ppermute | solution.py:125
  16.4 71.1 %all-to-all-start = ((bf16[8,32,2048]{2,1,0:T(8,128)(2,1)}), bf16[8,32,2048]{2,1,0:T(8,128)(2,1)S(1)}, u32[]{:S(2)}, u32[]{:S(2)}) async-start(bf16[8,32,2048]{2,1,0:T(8,128)(2,1)} %broadcast_in_dim.89), calls=%async_computation | async-start | bytes 2097152 | tf_op jit(solution)/shard_map/all_to_all | solution.py:100
  20.6 138.6 %all-gather.5.cloned.1.call-start = ((), (), s32[]{:S(2)}) async-start(), calls=%async_computation.5 | async-start | bytes 4325376 | tf_op jit(solution)/shard_map/all_gather | solution.py:181
  66.7 23.6 %copy-start.11 = (bf16[1,384,2048]{2,1,0:T(8,128)(2,1)}, bf16[1,384,2048]{2,1,0:T(8,128)(2,1)S(1)}, u32[]{:S(2)}) copy-start(bf16[1,384,2048]{2,1,0:T(8,128)(2,1)S(1)} %collective-permute-done) | copy-start | bytes 4718596
  87.5 3.1 copy-start.8
  90.4 0.9 copy-start.3
  95.2 2.6 copy-start
  95.2 5.5 %copy-start.6 = (s32[32,8]{0,1:T(8,128)S(1)}, s32[32,8]{0,1:T(8,128)}, u32[]{:S(2)}) copy-start(s32[32,8]{0,1:T(8,128)} %param.17) | copy-start | bytes 3076
  97.8 5.7 %copy-start.9 = (f32[128]{0:T(128)S(1)}, f32[128]{0:T(128)}, u32[]{:S(2)}) copy-start(f32[128]{0:T(128)} %param.22) | copy-start | bytes 1540
  97.8 55.9 %collective-permute-start.1 = (bf16[1,1024,768]{1,2,0:T(8,128)(2,1)}, bf16[1,1024,768]{1,2,0:T(8,128)(2,1)}, u32[]{:S(2)}, u32[]{:S(2)}) collective-permute-start(bf16[1,1024,768]{1,2,0:T(8,128)(2,1)} %get-tuple-element.388), channel_id=1, source_target_pairs={{0,1},{1,0},{2,3},{3,2},{4,5},{5,4},{6,7},{7,6},{8,9},{9,8},{10,11... | collective-permute-start | bytes 4718600 | tf_op jit(solution)/shard_map/ppermute | solution.py:182
  98.1 98.6 %collective-permute-start.2 = (bf16[1,1024,768]{1,2,0:T(8,128)(2,1)}, bf16[1,1024,768]{1,2,0:T(8,128)(2,1)}, u32[]{:S(2)}, u32[]{:S(2)}) collective-permute-start(bf16[1,1024,768]{1,2,0:T(8,128)(2,1)} %get-tuple-element.387), channel_id=1, source_target_pairs={{0,1},{1,0},{2,3},{3,2},{4,5},{5,4},{6,7},{7,6},{8,9},{9,8},{10,11... | collective-permute-start | bytes 4718600 | tf_op jit(solution)/shard_map/ppermute | solution.py:195
  200.0 23.3 %copy-start.2 = (bf16[32,2048]{1,0:T(8,128)(2,1)S(1)}, bf16[32,2048]{1,0:T(8,128)(2,1)}, u32[]{:S(2)}) copy-start(bf16[32,2048]{1,0:T(8,128)(2,1)} %param.15) | copy-start | bytes 393220
  200.0 23.5 %copy-start.5 = (f32[2048]{0:T(1024)S(1)}, f32[2048]{0:T(1024)}, u32[]{:S(2)}) copy-start(f32[2048]{0:T(1024)} %param.25) | copy-start | bytes 24580
  200.1 23.1 %all-to-all-start.1 = ((bf16[8,32,2048]{2,1,0:T(8,128)(2,1)}), bf16[8,32,2048]{2,1,0:T(8,128)(2,1)S(1)}, u32[]{:S(2)}, u32[]{:S(2)}) async-start(bf16[8,32,2048]{2,1,0:T(8,128)(2,1)} %bitcast.13), calls=%async_computation.1 | async-start | bytes 2097152 | tf_op jit(solution)/shard_map/all_to_all | solution.py:217
  288.7 4.3 %copy-start.1 = (bf16[1,2048,768]{1,2,0:T(8,128)(2,1)S(1)}, bf16[1,2048,768]{1,2,0:T(8,128)(2,1)}, u32[]{:S(2)}) copy-start(bf16[1,2048,768]{1,2,0:T(8,128)(2,1)} %copy-done) | copy-start | bytes 9437188
  292.9 5.9 %copy-start.10 = (bf16[1,384,2048]{2,1,0:T(8,128)(2,1)S(1)}, bf16[1,384,2048]{2,1,0:T(8,128)(2,1)}, u32[]{:S(2)}) copy-start(bf16[1,384,2048]{2,1,0:T(8,128)(2,1)} %param.27) | copy-start | bytes 4718596
  292.9 5.9 %copy-start.12 = (bf16[1,384,2048]{2,1,0:T(8,128)(2,1)S(1)}, bf16[1,384,2048]{2,1,0:T(8,128)(2,1)}, u32[]{:S(2)}) copy-start(bf16[1,384,2048]{2,1,0:T(8,128)(2,1)} %copy-done.11) | copy-start | bytes 4718596
  303.9 6.9 %copy-start.7 = (f32[32,8]{0,1:T(8,128)S(1)}, f32[32,8]{0,1:T(8,128)}, u32[]{:S(2)}) copy-start(f32[32,8]{0,1:T(8,128)} %param.18) | copy-start | bytes 3076
  303.9 59.8 %all-to-all-start.3 = ((bf16[256,2,2048]{2,1,0:T(2,128)(2,1)}), bf16[256,2,2048]{2,1,0:T(2,128)(2,1)S(1)}, u32[]{:S(2)}, u32[]{:S(2)}) async-start(bf16[256,2,2048]{2,1,0:T(2,128)(2,1)} %reshape.526), calls=%async_computation.3 | async-start | bytes 4194304 | tf_op jit(solution)/shard_map/all_to_all | solution.py:272
Sparse Core Ops, SparseCore 0:
  9.8 74.2 all-gather.2
  92.1 67.0 all-gather.4

commit v5 on v4

--- a/solution.py
+++ b/solution.py
@@ -2,6 +2,8 @@
 import jax.numpy as jnp
 from jax import lax
 from jax.sharding import PartitionSpec as P
+from jax.experimental import pallas as pl
+from jax.experimental.pallas import tpu as pltpu
 
 MODEL_WIDTH = 2048
 QUERY_HEADS = 32
@@ -60,6 +62,50 @@
         ],
         axis=-1,
     )
+
+
+def attention_sums(q_rows, every_kv, q_pos, q_doc, k_pos, k_doc, scale, chunk):
+    rows, width = q_rows.shape
+    total = every_kv.shape[1]
+
+    def body(q_ref, k_ref, v_ref, qp_ref, qd_ref, kp_ref, kd_ref, num_ref, den_ref):
+        @pl.when(pl.program_id(0) == 0)
+        def _():
+            num_ref[...] = jnp.zeros_like(num_ref)
+            den_ref[...] = jnp.zeros_like(den_ref)
+
+        scores = (
+            lax.dot_general(
+                q_ref[...], k_ref[...], (((1,), (1,)), ((), ())),
+                preferred_element_type=jnp.float32,
+            )
+            * scale
+        )
+        allowed = (qd_ref[...] == kd_ref[...]) & (kp_ref[...] <= qp_ref[...])
+        weights = jnp.where(allowed, jnp.exp(scores), 0.0).astype(jnp.bfloat16)
+        num_ref[...] += jnp.dot(weights, v_ref[...], preferred_element_type=jnp.float32)
+        den_ref[...] += jnp.sum(weights.astype(jnp.float32), axis=1, keepdims=True)
+
+    whole = lambda i: (0, 0)
+    return pl.pallas_call(
+        body,
+        grid=(total // chunk,),
+        in_specs=[
+            pl.BlockSpec((rows, width), whole),
+            pl.BlockSpec((None, chunk, width), lambda i: (0, i, 0)),
+            pl.BlockSpec((None, chunk, width), lambda i: (1, i, 0)),
+            pl.BlockSpec((rows, 1), whole),
+            pl.BlockSpec((rows, 1), whole),
+            pl.BlockSpec((1, chunk), lambda i: (0, i)),
+            pl.BlockSpec((1, chunk), lambda i: (0, i)),
+        ],
+        out_specs=[pl.BlockSpec((rows, width), whole), pl.BlockSpec((rows, 1), whole)],
+        out_shape=[
+            jax.ShapeDtypeStruct((rows, width), jnp.float32),
+            jax.ShapeDtypeStruct((rows, 1), jnp.float32),
+        ],
+        compiler_params=pltpu.CompilerParams(dimension_semantics=("arbitrary",)),
+    )(q_rows, every_kv, every_kv, q_pos, q_doc, k_pos, k_doc)
 
 
 def shards(
@@ -148,34 +194,7 @@
     key_values = jnp.stack(
         [key_row_block.reshape(tok_ctx, key_value_share * HEAD_SIZE), value_row_block]
     )
-    query_groups = queries.reshape(tok_ctx, key_value_share, group_dev, HEAD_SIZE)
-
-    def attend(state_now, block_kv, offset):
-        length_now = block_kv.shape[1]
-        key_pos = mirrored_position(
-            offset + jnp.arange(length_now, dtype=jnp.int32), count_ctx, tok_ctx
-        )
-        key_doc, unused_rope = document_info(key_pos, lengths)
-        allowed = (query_doc[:, None] == key_doc[None, :]) & (
-            key_pos[None, :] <= query_pos[:, None]
-        )
-        key_part = block_kv[0].reshape(length_now, key_value_share, HEAD_SIZE)
-        value_part = block_kv[1].reshape(length_now, key_value_share, HEAD_SIZE)
-        scores = (
-            jnp.einsum("qkgd,skd->kgqs", query_groups, key_part, preferred_element_type=jnp.float32)
-            * score_scale
-        )
-        weights = jnp.where(allowed[None, None], jnp.exp(scores), 0.0).astype(jnp.bfloat16)
-        numerator = state_now[0] + jnp.einsum(
-            "kgqs,skd->qkgd", weights, value_part, preferred_element_type=jnp.float32
-        )
-        denominator = state_now[1] + jnp.sum(weights, axis=-1, dtype=jnp.float32)
-        return (numerator, denominator) + tuple(state_now[2:])
-
-    initial = (
-        jnp.zeros((tok_ctx, key_value_share, group_dev, HEAD_SIZE), jnp.float32),
-        jnp.zeros((key_value_share, group_dev, tok_ctx), jnp.float32),
-    )
+
     every_kv, partner_in_low = lax.optimization_barrier(
         (
             lax.all_gather(key_values, "ctx", axis=1, tiled=True),
@@ -184,22 +203,27 @@
     )
     total_rows = every_kv.shape[1]
     chunk = min(1024, total_rows)
-
-    def turn(step_no, state_now):
-        block_kv = lax.dynamic_slice_in_dim(every_kv, step_no * chunk, chunk, 1)
-        return attend(state_now, block_kv, step_no * chunk)
-
-    final_state, partner_in_high = lax.optimization_barrier(
+    key_pos = mirrored_position(jnp.arange(total_rows, dtype=jnp.int32), count_ctx, tok_ctx)
+    key_doc, unused_rope = document_info(key_pos, lengths)
+    q_rows = jnp.transpose(queries, (1, 0, 2)).reshape(q_dev * tok_ctx, HEAD_SIZE)
+    sums, partner_in_high = lax.optimization_barrier(
         (
-            lax.fori_loop(0, total_rows // chunk, turn, initial),
+            attention_sums(
+                q_rows,
+                every_kv,
+                jnp.tile(query_pos, q_dev)[:, None],
+                jnp.tile(query_doc, q_dev)[:, None],
+                key_pos[None, :],
+                key_doc[None, :],
+                score_scale,
+                chunk,
+            ),
             lax.ppermute(expert_in[:, rows_half:], "exp", pair),
         )
     )
-    context = (
-        (final_state[0] / jnp.transpose(final_state[1], (2, 0, 1))[..., None])
-        .astype(jnp.bfloat16)
-        .reshape(tok_ctx, q_dev * HEAD_SIZE)
-    )
+    numerator = jnp.transpose(sums[0].reshape(q_dev, tok_ctx, HEAD_SIZE), (1, 0, 2))
+    denominator = jnp.transpose(sums[1].reshape(q_dev, tok_ctx, 1), (1, 0, 2))
+    context = (numerator / denominator).astype(jnp.bfloat16).reshape(tok_ctx, q_dev * HEAD_SIZE)
     def block_start(block_no):
         holder = jnp.where(block_no < count_ctx, block_no, 2 * count_ctx - 1 - block_no)
         return holder * tok_ctx + jnp.where(block_no < count_ctx, 0, half_rows)

time: 377 us -> 378 us (level)
  matrix products: 48 us -> 21.4 us
  Pallas kernels: 0 us -> 20.3 us
  local copies, waits for them, and re-layouts: 23.6 us -> 32.7 us
  blocking collectives: 61.5 us -> 65.7 us
  waiting for transfers between devices: 186 us -> 182 us
    dot_general x16 -> x0, matrix products: 28.6 us -> none  [the longest x8 16.6 us: attend(): jnp.einsum('qkgd,skd->kgqs', query_groups, key_part, preferred_element_ty...]
    pallas_call x0 -> x1, Pallas kernels: none -> 20.3 us  [attention_sums(): pl.pallas_call(body, grid=(total // chunk,), in_specs=[pl.BlockSpec((rows...]
    ppermute x1, waiting for transfers between devices: 49.6 us -> 39 us  [shards(): lax.ppermute(expert_in[:, :rows_half], 'exp', pair)]
    ppermute x1, waiting for transfers between devices: 0.01 us -> 8.77 us  [shards(): lax.ppermute(expert_in[:, rows_half:], 'exp', pair)]
    all_to_all x1, blocking collectives: 61.5 us -> 65.7 us  [shards(): lax.all_to_all(outgoing, ('ctx', 'exp'), split_axis=0, concat_axis=0, til...]
  transfers between devices with their start and end apart: 8 -> 8, of which waited for: 7 -> 8; matrix products, arithmetic and copies ran while one was open for 14% -> 7% of each run, Pallas kernels for 0% -> 5%
where the time goes in v5:
time: 378 us; the launch traced here: 377 us
  waiting for transfers between devices  182 us (48%)
  blocking collectives  65.7 us (17%)
  local copies, waits for them, and re-layouts  32.7 us (9%)
  starting transfers between devices  22.3 us (6%)
  matrix products  21.4 us (6%)
  Pallas kernels  20.3 us (5%)
  other arithmetic  16.9 us (4%)
  between operations  15.7 us (4%)
    all_to_all x1, blocking collectives, shards(): lax.all_to_all(outgoing, ('ctx', 'exp'), split_axis=0, concat_axis=0, til...  65.7 us
    all_to_all x1, waiting for transfers between devices, shards(): lax.all_to_all(produced, ('ctx', 'exp'), split_axis=0, concat_axis=0, til...  50.5 us
    ppermute x1, waiting for transfers between devices, shards(): lax.ppermute(expert_out, 'exp', pair)  43.6 us
    ppermute x1, waiting for transfers between devices, shards(): lax.ppermute(expert_in[:, :rows_half], 'exp', pair)  39 us
    pallas_call x1, Pallas kernels, attention_sums(): pl.pallas_call(body, grid=(total // chunk,), in_specs=[pl.BlockSpec((rows...  20.3 us
    all_gather x1, waiting for transfers between devices, shards(): lax.all_gather(jnp.concatenate([q_weight, kv_local, o_weight.T], axis=1),...  17.4 us
    all_to_all x1, waiting for transfers between devices, shards(): lax.all_to_all(attn_part.astype(jnp.bfloat16).reshape(expert_count, tok_d...  13.4 us
    ppermute x1, waiting for transfers between devices, shards(): lax.ppermute(expert_in[:, rows_half:], 'exp', pair)  8.77 us
  transfers between devices with their start and end apart: 8, of which 8 were waited for; matrix products, arithmetic and copies ran while one was open for 7% of the time, Pallas kernels for 5%

profile of v5, /device:TPU:1, one launch (start us, length us, event | category | flops | bytes accessed | tf_op | source)
XLA Modules:
  0.0 377.1 jit_solution(2336246960458425045)
XLA Ops:
  8.0 1.6 pad_maximum_fusion
  9.6 3.6 collective-permute-start
  16.4 4.2 %all-to-all-start = ((bf16[8,32,2048]{2,1,0:T(8,128)(2,1)}), bf16[8,32,2048]{2,1,0:T(8,128)(2,1)S(1)}, u32[]{:S(2)}, u32[]{:S(2)}) async-start(bf16[8,32,2048]{2,1,0:T(8,128)(2,1)} %broadcast_in_dim.8), calls=%async_computation | async-start | bytes 2097152 | tf_op jit(solution)/shard_map/all_to_all | solution.py:146
  23.2 43.6 %collective-permute-done = bf16[1,384,2048]{2,1,0:T(8,128)(2,1)S(1)} collective-permute-done((bf16[1,384,2048]{2,1,0:T(8,128)(2,1)}, bf16[1,384,2048]{2,1,0:T(8,128)(2,1)S(1)}, u32[]{:S(2)}, u32[]{:S(2)}) %collective-permute-start) | collective-permute-done | bytes 1572896 | tf_op jit(solution)/shard_map/ppermute | solution.py:171
  66.7 17.4 %all-gather.3.cloned.1.call-done = bf16[2048,1280]{1,0:T(8,128)(2,1)} async-done(((bf16[64,1280]{1,0:T(8,128)(2,1)}), bf16[2048,1280]{1,0:T(8,128)(2,1)}) %all-gather.3.cloned.1.call-update) | async-done | bytes 5242896 | tf_op jit(solution)/shard_map/all_gather | solution.py:168
  84.2 3.3 all-to-all-done
  87.5 2.9 fusion.9
  92.0 3.2 copy.52
  95.2 2.0 fusion.65
  97.5 2.7 collective-permute-start.2
  105.8 1.9 slice.76
  107.7 2.0 reshape.490
  114.2 39.0 %collective-permute-done.1 = bf16[1,1024,768]{1,2,0:T(8,128)(2,1)} collective-permute-done((bf16[1,1024,768]{1,2,0:T(8,128)(2,1)}, bf16[1,1024,768]{1,2,0:T(8,128)(2,1)}, u32[]{:S(2)}, u32[]{:S(2)}) %collective-permute-start.1) | collective-permute-done | bytes 1572896 | tf_op jit(solution)/shard_map/ppermute | solution.py:201
  153.1 6.1 %all-gather.5.cloned.1.call-done.k_ref.v_ref = bf16[2,8192,128]{2,1,0:T(8,128)(2,1)} async-done(((bf16[2,256,128]{2,1,0:T(8,128)(2,1)}), bf16[2,8192,128]{2,1,0:T(8,128)(2,1)}) %all-gather.5.cloned.1.call-update) | async-done | bytes 4194320 | tf_op jit(solution)/shard_map/all_gather | solution.py:200
  159.2 20.3 %shard_map.140 = (f32[1024,128]{1,0:T(8,128)}, f32[1024,1]{1,0:T(8,128)}) custom-call(bf16[1024,128]{1,0:T(8,128)(2,1)} %bitcast.55, bf16[2,8192,128]{2,1,0:T(8,128)(2,1)} %all-gather.5.cloned.1.call-done.k_ref.v_ref, bf16[2,8192,128]{2,1,0:T(8,128)(2,1)} %all-gather.5.cloned.1.call-done.k_ref.v_ref, s32[1024,1]{1,0:T(8,128)} %bitcast.53, ...), custom_call_target="tpu_custom_call" | custom-call | tf_op jit(solution)/shard_map/pallas_call | solution.py:90
  179.5 8.8 %collective-permute-done.2 = bf16[1,1024,768]{1,2,0:T(8,128)(2,1)} collective-permute-done((bf16[1,1024,768]{1,2,0:T(8,128)(2,1)}, bf16[1,1024,768]{1,2,0:T(8,128)(2,1)}, u32[]{:S(2)}, u32[]{:S(2)}) %collective-permute-start.2) | collective-permute-done | bytes 1572896 | tf_op jit(solution)/shard_map/ppermute | solution.py:221
  188.3 2.0 copy.56
  192.6 3.4 convolution_convert_fusion.1
  196.0 4.5 %all-to-all-start.1 = ((bf16[8,32,2048]{2,1,0:T(8,128)(2,1)}), bf16[8,32,2048]{2,1,0:T(8,128)(2,1)}, u32[]{:S(2)}, u32[]{:S(2)}) async-start(bf16[8,32,2048]{2,1,0:T(8,128)(2,1)} %bitcast.57), calls=%async_computation.1 | async-start | bytes 2097152 | tf_op jit(solution)/shard_map/all_to_all | solution.py:241
  201.7 13.4 %all-to-all-done.1 = bf16[8,32,2048]{2,1,0:T(8,128)(2,1)} async-done(((bf16[8,32,2048]{2,1,0:T(8,128)(2,1)}), bf16[8,32,2048]{2,1,0:T(8,128)(2,1)}, u32[]{:S(2)}, u32[]{:S(2)}) %all-to-all-start.1) | async-done | bytes 1048608 | tf_op jit(solution)/shard_map/all_to_all | solution.py:241
  215.1 1.4 convert_reduce_fusion.1
  216.7 3.0 convolution_convert_fusion
  219.7 4.4 %reshape.498 = bf16[256,2,2048]{2,1,0:T(2,128)(2,1)} reshape(bf16[512,2048]{1,0:T(8,128)(2,1)} %convolution_convert_fusion) | data formatting | bytes 4194304 | tf_op jit(solution)/shard_map/reshape | solution.py:281
  224.1 65.7 %all_to_all.20 = bf16[256,2,2048]{2,1,0:T(2,128)(2,1)} all-to-all(bf16[256,2,2048]{2,1,0:T(2,128)(2,1)} %reshape.498), channel_id=1, replica_groups=mesh['ctx'=32,'exp'=8] {'ctx','exp'}, dimensions={0} | all-to-all | bytes 4194304 | tf_op jit(solution)/shard_map/all_to_all | solution.py:282
  289.8 4.1 %reshape.502 = bf16[512,2048,1]{1,0,2:T(8,128)(2,1)} reshape(bf16[256,2,2048]{2,1,0:T(2,128)(2,1)} %all_to_all.20) | data formatting | bytes 4194304 | tf_op jit(solution)/shard_map/reshape | solution.py:283
  293.9 5.9 %fusion.13 = f32[2,512,768]{1,2,0:T(8,128)S(1)} fusion(bf16[512,2048,1]{1,0,2:T(8,128)(2,1)} %reshape.502, bf16[1,1024,768]{1,2,0:T(8,128)(2,1)} %collective-permute-done.2, bf16[1,1024,768]{1,2,0:T(8,128)(2,1)} %collective-permute-done.1, bf16[1,2048,768]{1,2,0:T(8,128)(2,1)S(1)} %copy.52), kind=kOutput, calls=%fused_computation.18 | convolution fusion | flops 3240099840 | bytes 11534336 | tf_op jit(solution)/shard_map/td,sdf->stf/dot_general | solution.py:284
  299.8 2.4 convert_reduce_fusion
  302.2 2.6 reshape.500
  304.9 6.9 %all-to-all-start.3 = ((bf16[256,2,2048]{2,1,0:T(2,128)(2,1)}), bf16[256,2,2048]{2,1,0:T(2,128)(2,1)S(1)}, u32[]{:S(2)}, u32[]{:S(2)}) async-start(bf16[256,2,2048]{2,1,0:T(2,128)(2,1)} %reshape.500), calls=%async_computation.3 | async-start | bytes 4194304 | tf_op jit(solution)/shard_map/all_to_all | solution.py:296
  314.2 50.5 %all-to-all-done.3 = bf16[256,2,2048]{2,1,0:T(2,128)(2,1)S(1)} async-done(((bf16[256,2,2048]{2,1,0:T(2,128)(2,1)}), bf16[256,2,2048]{2,1,0:T(2,128)(2,1)S(1)}, u32[]{:S(2)}, u32[]{:S(2)}) %all-to-all-start.3) | async-done | bytes 2097184 | tf_op jit(solution)/shard_map/all_to_all | solution.py:296
  364.6 2.2 reshape.501
  366.9 3.4 fusion.11
  (84 shorter events, 23.1 us)
Async XLA Ops:
  7.2 77.0 %all-gather.3.cloned.1.call-start = ((), (), s32[]{:S(2)}) async-start(), calls=%async_computation.4 | async-start | bytes 5406720 | tf_op jit(solution)/shard_map/all_gather | solution.py:168
  8.0 12.7 %copy-start.7 = (s32[2]{0:T(128)S(1)}, s32[2]{0:T(128)}, u32[]{:S(2)}) copy-start(s32[2]{0:T(128)} %param.14) | copy-start | bytes 28
  9.6 57.2 %collective-permute-start = (bf16[1,384,2048]{2,1,0:T(8,128)(2,1)}, bf16[1,384,2048]{2,1,0:T(8,128)(2,1)S(1)}, u32[]{:S(2)}, u32[]{:S(2)}) collective-permute-start(bf16[1,384,2048]{2,1,0:T(8,128)(2,1)} %param.25), channel_id=1, source_target_pairs={{0,1},{1,0},{2,3},{3,2},{4,5},{5,4},{6,7},{7,6},{8,9},{9,8},{10,11... | collective-permute-start | bytes 4718600 | tf_op jit(solution)/shard_map/ppermute | solution.py:171
  16.4 71.1 %all-to-all-start = ((bf16[8,32,2048]{2,1,0:T(8,128)(2,1)}), bf16[8,32,2048]{2,1,0:T(8,128)(2,1)S(1)}, u32[]{:S(2)}, u32[]{:S(2)}) async-start(bf16[8,32,2048]{2,1,0:T(8,128)(2,1)} %broadcast_in_dim.8), calls=%async_computation | async-start | bytes 2097152 | tf_op jit(solution)/shard_map/all_to_all | solution.py:146
  20.6 138.6 %all-gather.5.cloned.1.call-start = ((), (), s32[]{:S(2)}) async-start(), calls=%async_computation.5 | async-start | bytes 4325376 | tf_op jit(solution)/shard_map/all_gather | solution.py:200
  66.7 23.6 %copy-start.11 = (bf16[1,384,2048]{2,1,0:T(8,128)(2,1)}, bf16[1,384,2048]{2,1,0:T(8,128)(2,1)S(1)}, u32[]{:S(2)}) copy-start(bf16[1,384,2048]{2,1,0:T(8,128)(2,1)S(1)} %collective-permute-done) | copy-start | bytes 4718596
  87.5 3.1 copy-start.8
  90.4 0.9 copy-start.1
  95.2 5.0 %copy-start.5 = (s32[32,8]{0,1:T(8,128)S(1)}, s32[32,8]{0,1:T(8,128)}, u32[]{:S(2)}) copy-start(s32[32,8]{0,1:T(8,128)} %param.15) | copy-start | bytes 3076
  97.2 55.9 %collective-permute-start.1 = (bf16[1,1024,768]{1,2,0:T(8,128)(2,1)}, bf16[1,1024,768]{1,2,0:T(8,128)(2,1)}, u32[]{:S(2)}, u32[]{:S(2)}) collective-permute-start(bf16[1,1024,768]{1,2,0:T(8,128)(2,1)} %get-tuple-element.31), channel_id=1, source_target_pairs={{0,1},{1,0},{2,3},{3,2},{4,5},{5,4},{6,7},{7,6},{8,9},{9,8},{10,11... | collective-permute-start | bytes 4718600 | tf_op jit(solution)/shard_map/ppermute | solution.py:201
  97.5 90.7 %collective-permute-start.2 = (bf16[1,1024,768]{1,2,0:T(8,128)(2,1)}, bf16[1,1024,768]{1,2,0:T(8,128)(2,1)}, u32[]{:S(2)}, u32[]{:S(2)}) collective-permute-start(bf16[1,1024,768]{1,2,0:T(8,128)(2,1)} %get-tuple-element.30), channel_id=1, source_target_pairs={{0,1},{1,0},{2,3},{3,2},{4,5},{5,4},{6,7},{7,6},{8,9},{9,8},{10,11... | collective-permute-start | bytes 4718600 | tf_op jit(solution)/shard_map/ppermute | solution.py:221
  102.2 9.0 %copy-start.9 = (f32[128]{0:T(128)S(1)}, f32[128]{0:T(128)}, u32[]{:S(2)}) copy-start(f32[128]{0:T(128)} %param.20) | copy-start | bytes 1540
  192.6 8.0 %copy-start.2 = (s32[2,128]{0,1:T(8,128)S(1)}, s32[2,128]{0,1:T(8,128)}, u32[]{:S(2)}) copy-start(s32[2,128]{0,1:T(8,128)} %copy.59) | copy-start | bytes 3076
  196.0 20.5 %copy-start = (bf16[32,2048]{1,0:T(8,128)(2,1)S(1)}, bf16[32,2048]{1,0:T(8,128)(2,1)}, u32[]{:S(2)}) copy-start(bf16[32,2048]{1,0:T(8,128)(2,1)} %param.13) | copy-start | bytes 393220
  196.0 20.6 %copy-start.3 = (f32[2048]{0:T(1024)S(1)}, f32[2048]{0:T(1024)}, u32[]{:S(2)}) copy-start(f32[2048]{0:T(1024)} %param.23) | copy-start | bytes 24580
  196.0 19.1 %all-to-all-start.1 = ((bf16[8,32,2048]{2,1,0:T(8,128)(2,1)}), bf16[8,32,2048]{2,1,0:T(8,128)(2,1)}, u32[]{:S(2)}, u32[]{:S(2)}) async-start(bf16[8,32,2048]{2,1,0:T(8,128)(2,1)} %bitcast.57), calls=%async_computation.1 | async-start | bytes 2097152 | tf_op jit(solution)/shard_map/all_to_all | solution.py:241
  293.9 5.9 %copy-start.10 = (bf16[1,384,2048]{2,1,0:T(8,128)(2,1)S(1)}, bf16[1,384,2048]{2,1,0:T(8,128)(2,1)}, u32[]{:S(2)}) copy-start(bf16[1,384,2048]{2,1,0:T(8,128)(2,1)} %param.25) | copy-start | bytes 4718596
  293.9 5.9 %copy-start.12 = (bf16[1,384,2048]{2,1,0:T(8,128)(2,1)S(1)}, bf16[1,384,2048]{2,1,0:T(8,128)(2,1)}, u32[]{:S(2)}) copy-start(bf16[1,384,2048]{2,1,0:T(8,128)(2,1)} %copy-done.11) | copy-start | bytes 4718596
  304.9 6.9 %copy-start.6 = (f32[32,8]{0,1:T(8,128)S(1)}, f32[32,8]{0,1:T(8,128)}, u32[]{:S(2)}) copy-start(f32[32,8]{0,1:T(8,128)} %param.16) | copy-start | bytes 3076
  304.9 7.1 %copy-start.4 = (s32[256]{0:T(256)S(1)}, s32[256]{0:T(256)}, u32[]{:S(2)}) copy-start(s32[256]{0:T(256)} %get-tuple-element.45) | copy-start | bytes 3076
  304.9 59.8 %all-to-all-start.3 = ((bf16[256,2,2048]{2,1,0:T(2,128)(2,1)}), bf16[256,2,2048]{2,1,0:T(2,128)(2,1)S(1)}, u32[]{:S(2)}, u32[]{:S(2)}) async-start(bf16[256,2,2048]{2,1,0:T(2,128)(2,1)} %reshape.500), calls=%async_computation.3 | async-start | bytes 4194304 | tf_op jit(solution)/shard_map/all_to_all | solution.py:296
Sparse Core Ops, SparseCore 0:
  9.8 74.2 all-gather.2
  92.2 67.0 all-gather.4

commit v6 on v5

--- a/solution.py
+++ b/solution.py
@@ -195,31 +195,21 @@
         [key_row_block.reshape(tok_ctx, key_value_share * HEAD_SIZE), value_row_block]
     )
 
-    every_kv, partner_in_low = lax.optimization_barrier(
-        (
-            lax.all_gather(key_values, "ctx", axis=1, tiled=True),
-            lax.ppermute(expert_in[:, :rows_half], "exp", pair),
-        )
-    )
+    every_kv = lax.all_gather(key_values, "ctx", axis=1, tiled=True)
     total_rows = every_kv.shape[1]
     chunk = min(1024, total_rows)
     key_pos = mirrored_position(jnp.arange(total_rows, dtype=jnp.int32), count_ctx, tok_ctx)
     key_doc, unused_rope = document_info(key_pos, lengths)
     q_rows = jnp.transpose(queries, (1, 0, 2)).reshape(q_dev * tok_ctx, HEAD_SIZE)
-    sums, partner_in_high = lax.optimization_barrier(
-        (
-            attention_sums(
-                q_rows,
-                every_kv,
-                jnp.tile(query_pos, q_dev)[:, None],
-                jnp.tile(query_doc, q_dev)[:, None],
-                key_pos[None, :],
-                key_doc[None, :],
-                score_scale,
-                chunk,
-            ),
-            lax.ppermute(expert_in[:, rows_half:], "exp", pair),
-        )
+    sums = attention_sums(
+        q_rows,
+        every_kv,
+        jnp.tile(query_pos, q_dev)[:, None],
+        jnp.tile(query_doc, q_dev)[:, None],
+        key_pos[None, :],
+        key_doc[None, :],
+        score_scale,
+        chunk,
     )
     numerator = jnp.transpose(sums[0].reshape(q_dev, tok_ctx, HEAD_SIZE), (1, 0, 2))
     denominator = jnp.transpose(sums[1].reshape(q_dev, tok_ctx, 1), (1, 0, 2))
@@ -244,6 +234,13 @@
         split_axis=0,
         concat_axis=0,
         tiled=True,
+    )
+    attn_pieces, partner_in_low, partner_in_high = lax.optimization_barrier(
+        (
+            attn_pieces,
+            lax.ppermute(expert_in[:, :rows_half], "exp", pair),
+            lax.ppermute(expert_in[:, rows_half:], "exp", pair),
+        )
     )
     attn_own = jnp.sum(attn_pieces, axis=0, dtype=jnp.float32)
     residual_mid = hidden.astype(jnp.float32) + attn_own

time: 378 us -> 370 us (0.979)
  waiting for transfers between devices: 182 us -> 176 us
  blocking collectives: 65.7 us -> 61.5 us
    all_gather x1, waiting for transfers between devices: 6.07 us -> 45.1 us  [shards(): every_kv = lax.all_gather(key_values, 'ctx', axis=1, tiled=True)]
    ppermute x1, waiting for transfers between devices: 39 us -> 0.01 us  [shards(): lax.ppermute(expert_in[:, :rows_half], 'exp', pair)]
    ppermute x1, waiting for transfers between devices: 8.77 us -> 0.01 us  [shards(): lax.ppermute(expert_in[:, rows_half:], 'exp', pair)]
    all_to_all x1, blocking collectives: 65.7 us -> 61.5 us  [shards(): lax.all_to_all(outgoing, ('ctx', 'exp'), split_axis=0, concat_axis=0, til...]
  transfers between devices with their start and end apart: 8 -> 8, of which waited for: 8 -> 6; matrix products, arithmetic and copies ran while one was open for 7% -> 9% of each run, Pallas kernels for 5% -> 6%
where the time goes in v6:
time: 370 us; the launch traced here: 368 us
  waiting for transfers between devices  176 us (48%)
  blocking collectives  61.5 us (17%)
  local copies, waits for them, and re-layouts  32.7 us (9%)
  starting transfers between devices  24.2 us (7%)
  matrix products  21.4 us (6%)
  Pallas kernels  20.3 us (5%)
  other arithmetic  16.3 us (4%)
  between operations  15.7 us (4%)
    all_to_all x1, blocking collectives, shards(): lax.all_to_all(outgoing, ('ctx', 'exp'), split_axis=0, concat_axis=0, til...  61.5 us
    all_to_all x1, waiting for transfers between devices, shards(): lax.all_to_all(produced, ('ctx', 'exp'), split_axis=0, concat_axis=0, til...  50.5 us
    all_gather x1, waiting for transfers between devices, shards(): every_kv = lax.all_gather(key_values, 'ctx', axis=1, tiled=True)  45.1 us
    ppermute x1, waiting for transfers between devices, shards(): lax.ppermute(expert_out, 'exp', pair)  43.6 us
    pallas_call x1, Pallas kernels, attention_sums(): pl.pallas_call(body, grid=(total // chunk,), in_specs=[pl.BlockSpec((rows...  20.3 us
    all_gather x1, waiting for transfers between devices, shards(): lax.all_gather(jnp.concatenate([q_weight, kv_local, o_weight.T], axis=1),...  17.4 us
    all_to_all x1, waiting for transfers between devices, shards(): lax.all_to_all(attn_part.astype(jnp.bfloat16).reshape(expert_count, tok_d...  16.3 us
  transfers between devices with their start and end apart: 8, of which 6 were waited for; matrix products, arithmetic and copies ran while one was open for 9% of the time, Pallas kernels for 6%

profile of v6, /device:TPU:1, one launch (start us, length us, event | category | flops | bytes accessed | tf_op | source)
XLA Modules:
  0.0 368.3 jit_solution(5381209713345747263)
XLA Ops:
  8.0 1.6 pad_maximum_fusion
  9.6 3.6 collective-permute-start
  16.4 4.2 %all-to-all-start = ((bf16[8,32,2048]{2,1,0:T(8,128)(2,1)}), bf16[8,32,2048]{2,1,0:T(8,128)(2,1)S(1)}, u32[]{:S(2)}, u32[]{:S(2)}) async-start(bf16[8,32,2048]{2,1,0:T(8,128)(2,1)} %broadcast_in_dim.8), calls=%async_computation | async-start | bytes 2097152 | tf_op jit(solution)/shard_map/all_to_all | solution.py:146
  23.2 43.6 %collective-permute-done = bf16[1,384,2048]{2,1,0:T(8,128)(2,1)S(1)} collective-permute-done((bf16[1,384,2048]{2,1,0:T(8,128)(2,1)}, bf16[1,384,2048]{2,1,0:T(8,128)(2,1)S(1)}, u32[]{:S(2)}, u32[]{:S(2)}) %collective-permute-start) | collective-permute-done | bytes 1572896 | tf_op jit(solution)/shard_map/ppermute | solution.py:171
  66.7 17.4 %all-gather.3.cloned.1.call-done = bf16[2048,1280]{1,0:T(8,128)(2,1)} async-done(((bf16[64,1280]{1,0:T(8,128)(2,1)}), bf16[2048,1280]{1,0:T(8,128)(2,1)}) %all-gather.3.cloned.1.call-update) | async-done | bytes 5242896 | tf_op jit(solution)/shard_map/all_gather | solution.py:168
  84.2 3.3 all-to-all-done
  87.5 2.9 fusion.9
  92.0 3.2 copy.55
  95.2 2.0 fusion.65
  97.5 2.7 collective-permute-start.1
  105.8 1.9 slice.76
  107.6 2.0 reshape.490
  109.6 1.4 multiply_reduce_fusion
  111.1 1.4 multiply_multiply_fusion
  114.1 45.1 %all-gather.5.cloned.1.call-done.k_ref.v_ref = bf16[2,8192,128]{2,1,0:T(8,128)(2,1)} async-done(((bf16[2,256,128]{2,1,0:T(8,128)(2,1)}), bf16[2,8192,128]{2,1,0:T(8,128)(2,1)}) %all-gather.5.cloned.1.call-update) | async-done | bytes 4194320 | tf_op jit(solution)/shard_map/all_gather | solution.py:198
  159.2 20.3 %shard_map.140 = (f32[1024,128]{1,0:T(8,128)}, f32[1024,1]{1,0:T(8,128)}) custom-call(bf16[1024,128]{1,0:T(8,128)(2,1)} %bitcast.55, bf16[2,8192,128]{2,1,0:T(8,128)(2,1)} %all-gather.5.cloned.1.call-done.k_ref.v_ref, bf16[2,8192,128]{2,1,0:T(8,128)(2,1)} %all-gather.5.cloned.1.call-done.k_ref.v_ref, s32[1024,1]{1,0:T(8,128)} %bitcast.54, ...), custom_call_target="tpu_custom_call" | custom-call | tf_op jit(solution)/shard_map/pallas_call | solution.py:90
  179.5 2.1 copy.54
  183.9 3.4 convolution_convert_fusion.1
  187.3 6.4 %all-to-all-start.1 = ((bf16[8,32,2048]{2,1,0:T(8,128)(2,1)}), bf16[8,32,2048]{2,1,0:T(8,128)(2,1)}, u32[]{:S(2)}, u32[]{:S(2)}) async-start(bf16[8,32,2048]{2,1,0:T(8,128)(2,1)} %bitcast.57), calls=%async_computation.1 | async-start | bytes 2097152 | tf_op jit(solution)/shard_map/all_to_all | solution.py:231
  194.2 16.3 %all-to-all-done.1 = bf16[8,32,2048]{2,1,0:T(8,128)(2,1)} async-done(((bf16[8,32,2048]{2,1,0:T(8,128)(2,1)}), bf16[8,32,2048]{2,1,0:T(8,128)(2,1)}, u32[]{:S(2)}, u32[]{:S(2)}) %all-to-all-start.1) | async-done | bytes 1048608 | tf_op jit(solution)/shard_map/all_to_all | solution.py:231
  210.5 1.4 convert_reduce_fusion.1
  212.1 3.0 convolution_convert_fusion
  215.1 4.4 %reshape.498 = bf16[256,2,2048]{2,1,0:T(2,128)(2,1)} reshape(bf16[512,2048]{1,0:T(8,128)(2,1)} %convolution_convert_fusion) | data formatting | bytes 4194304 | tf_op jit(solution)/shard_map/reshape | solution.py:278
  219.5 61.5 %all_to_all.20 = bf16[256,2,2048]{2,1,0:T(2,128)(2,1)} all-to-all(bf16[256,2,2048]{2,1,0:T(2,128)(2,1)} %reshape.498), channel_id=1, replica_groups=mesh['ctx'=32,'exp'=8] {'ctx','exp'}, dimensions={0} | all-to-all | bytes 4194304 | tf_op jit(solution)/shard_map/all_to_all | solution.py:279
  281.0 4.1 %reshape.502 = bf16[512,2048,1]{1,0,2:T(8,128)(2,1)} reshape(bf16[256,2,2048]{2,1,0:T(2,128)(2,1)} %all_to_all.20) | data formatting | bytes 4194304 | tf_op jit(solution)/shard_map/reshape | solution.py:280
  285.1 5.9 %fusion.13 = f32[2,512,768]{1,2,0:T(8,128)S(1)} fusion(bf16[512,2048,1]{1,0,2:T(8,128)(2,1)} %reshape.502, bf16[1,1024,768]{1,2,0:T(8,128)(2,1)} %collective-permute-done.2, bf16[1,1024,768]{1,2,0:T(8,128)(2,1)} %collective-permute-done.1, bf16[1,2048,768]{1,2,0:T(8,128)(2,1)S(1)} %copy.55), kind=kOutput, calls=%fused_computation.18 | convolution fusion | flops 3240099840 | bytes 11534336 | tf_op jit(solution)/shard_map/td,sdf->stf/dot_general | solution.py:281
  291.0 2.4 convert_reduce_fusion
  293.4 2.6 reshape.500
  296.1 6.9 %all-to-all-start.3 = ((bf16[256,2,2048]{2,1,0:T(2,128)(2,1)}), bf16[256,2,2048]{2,1,0:T(2,128)(2,1)S(1)}, u32[]{:S(2)}, u32[]{:S(2)}) async-start(bf16[256,2,2048]{2,1,0:T(2,128)(2,1)} %reshape.500), calls=%async_computation.3 | async-start | bytes 4194304 | tf_op jit(solution)/shard_map/all_to_all | solution.py:293
  305.4 50.5 %all-to-all-done.3 = bf16[256,2,2048]{2,1,0:T(2,128)(2,1)S(1)} async-done(((bf16[256,2,2048]{2,1,0:T(2,128)(2,1)}), bf16[256,2,2048]{2,1,0:T(2,128)(2,1)S(1)}, u32[]{:S(2)}, u32[]{:S(2)}) %all-to-all-start.3) | async-done | bytes 2097184 | tf_op jit(solution)/shard_map/all_to_all | solution.py:293
  355.8 2.2 reshape.501
  358.0 3.4 fusion.11
  (84 shorter events, 19.7 us)
Async XLA Ops:
  7.2 77.0 %all-gather.3.cloned.1.call-start = ((), (), s32[]{:S(2)}) async-start(), calls=%async_computation.4 | async-start | bytes 5406720 | tf_op jit(solution)/shard_map/all_gather | solution.py:168
  8.0 12.7 %copy-start.7 = (s32[2]{0:T(128)S(1)}, s32[2]{0:T(128)}, u32[]{:S(2)}) copy-start(s32[2]{0:T(128)} %param.14) | copy-start | bytes 28
  9.6 57.2 %collective-permute-start = (bf16[1,384,2048]{2,1,0:T(8,128)(2,1)}, bf16[1,384,2048]{2,1,0:T(8,128)(2,1)S(1)}, u32[]{:S(2)}, u32[]{:S(2)}) collective-permute-start(bf16[1,384,2048]{2,1,0:T(8,128)(2,1)} %param.25), channel_id=1, source_target_pairs={{0,1},{1,0},{2,3},{3,2},{4,5},{5,4},{6,7},{7,6},{8,9},{9,8},{10,11... | collective-permute-start | bytes 4718600 | tf_op jit(solution)/shard_map/ppermute | solution.py:171
  16.4 71.1 %all-to-all-start = ((bf16[8,32,2048]{2,1,0:T(8,128)(2,1)}), bf16[8,32,2048]{2,1,0:T(8,128)(2,1)S(1)}, u32[]{:S(2)}, u32[]{:S(2)}) async-start(bf16[8,32,2048]{2,1,0:T(8,128)(2,1)} %broadcast_in_dim.8), calls=%async_computation | async-start | bytes 2097152 | tf_op jit(solution)/shard_map/all_to_all | solution.py:146
  20.6 138.6 %all-gather.5.cloned.1.call-start = ((), (), s32[]{:S(2)}) async-start(), calls=%async_computation.5 | async-start | bytes 4325376 | tf_op jit(solution)/shard_map/all_gather | solution.py:198
  66.7 23.6 %copy-start.11 = (bf16[1,384,2048]{2,1,0:T(8,128)(2,1)}, bf16[1,384,2048]{2,1,0:T(8,128)(2,1)S(1)}, u32[]{:S(2)}) copy-start(bf16[1,384,2048]{2,1,0:T(8,128)(2,1)S(1)} %collective-permute-done) | copy-start | bytes 4718596
  87.5 3.1 copy-start.8
  90.4 0.9 copy-start.1
  95.2 5.0 %copy-start.5 = (s32[32,8]{0,1:T(8,128)S(1)}, s32[32,8]{0,1:T(8,128)}, u32[]{:S(2)}) copy-start(s32[32,8]{0,1:T(8,128)} %param.15) | copy-start | bytes 3076
  97.2 96.9 %collective-permute-start.2 = (bf16[1,1024,768]{1,2,0:T(8,128)(2,1)}, bf16[1,1024,768]{1,2,0:T(8,128)(2,1)}, u32[]{:S(2)}, u32[]{:S(2)}) collective-permute-start(bf16[1,1024,768]{1,2,0:T(8,128)(2,1)} %get-tuple-element.26), channel_id=1, source_target_pairs={{0,1},{1,0},{2,3},{3,2},{4,5},{5,4},{6,7},{7,6},{8,9},{9,8},{10,11... | collective-permute-start | bytes 4718600 | tf_op jit(solution)/shard_map/ppermute | solution.py:242
  97.5 96.7 %collective-permute-start.1 = (bf16[1,1024,768]{1,2,0:T(8,128)(2,1)}, bf16[1,1024,768]{1,2,0:T(8,128)(2,1)}, u32[]{:S(2)}, u32[]{:S(2)}) collective-permute-start(bf16[1,1024,768]{1,2,0:T(8,128)(2,1)} %get-tuple-element.27), channel_id=1, source_target_pairs={{0,1},{1,0},{2,3},{3,2},{4,5},{5,4},{6,7},{7,6},{8,9},{9,8},{10,11... | collective-permute-start | bytes 4718600 | tf_op jit(solution)/shard_map/ppermute | solution.py:241
  101.8 9.3 %copy-start.9 = (f32[128]{0:T(128)S(1)}, f32[128]{0:T(128)}, u32[]{:S(2)}) copy-start(f32[128]{0:T(128)} %param.20) | copy-start | bytes 1540
  183.9 9.8 %copy-start.2 = (s32[2,128]{0,1:T(8,128)S(1)}, s32[2,128]{0,1:T(8,128)}, u32[]{:S(2)}) copy-start(s32[2,128]{0,1:T(8,128)} %copy.59) | copy-start | bytes 3076
  187.3 24.6 %copy-start = (bf16[32,2048]{1,0:T(8,128)(2,1)S(1)}, bf16[32,2048]{1,0:T(8,128)(2,1)}, u32[]{:S(2)}) copy-start(bf16[32,2048]{1,0:T(8,128)(2,1)} %param.13) | copy-start | bytes 393220
  187.3 24.8 %copy-start.3 = (f32[2048]{0:T(1024)S(1)}, f32[2048]{0:T(1024)}, u32[]{:S(2)}) copy-start(f32[2048]{0:T(1024)} %param.23) | copy-start | bytes 24580
  187.3 23.2 %all-to-all-start.1 = ((bf16[8,32,2048]{2,1,0:T(8,128)(2,1)}), bf16[8,32,2048]{2,1,0:T(8,128)(2,1)}, u32[]{:S(2)}, u32[]{:S(2)}) async-start(bf16[8,32,2048]{2,1,0:T(8,128)(2,1)} %bitcast.57), calls=%async_computation.1 | async-start | bytes 2097152 | tf_op jit(solution)/shard_map/all_to_all | solution.py:231
  285.1 5.9 %copy-start.10 = (bf16[1,384,2048]{2,1,0:T(8,128)(2,1)S(1)}, bf16[1,384,2048]{2,1,0:T(8,128)(2,1)}, u32[]{:S(2)}) copy-start(bf16[1,384,2048]{2,1,0:T(8,128)(2,1)} %param.25) | copy-start | bytes 4718596
  285.1 5.9 %copy-start.12 = (bf16[1,384,2048]{2,1,0:T(8,128)(2,1)S(1)}, bf16[1,384,2048]{2,1,0:T(8,128)(2,1)}, u32[]{:S(2)}) copy-start(bf16[1,384,2048]{2,1,0:T(8,128)(2,1)} %copy-done.11) | copy-start | bytes 4718596
  296.1 6.9 %copy-start.6 = (f32[32,8]{0,1:T(8,128)S(1)}, f32[32,8]{0,1:T(8,128)}, u32[]{:S(2)}) copy-start(f32[32,8]{0,1:T(8,128)} %param.16) | copy-start | bytes 3076
  296.1 7.1 %copy-start.4 = (s32[256]{0:T(256)S(1)}, s32[256]{0:T(256)}, u32[]{:S(2)}) copy-start(s32[256]{0:T(256)} %get-tuple-element.38) | copy-start | bytes 3076
  296.1 59.8 %all-to-all-start.3 = ((bf16[256,2,2048]{2,1,0:T(2,128)(2,1)}), bf16[256,2,2048]{2,1,0:T(2,128)(2,1)S(1)}, u32[]{:S(2)}, u32[]{:S(2)}) async-start(bf16[256,2,2048]{2,1,0:T(2,128)(2,1)} %reshape.500), calls=%async_computation.3 | async-start | bytes 4194304 | tf_op jit(solution)/shard_map/all_to_all | solution.py:293
Sparse Core Ops, SparseCore 0:
  9.8 74.2 all-gather.2
  92.2 67.0 all-gather.4

commit v7 on v6

--- a/solution.py
+++ b/solution.py
@@ -83,8 +83,11 @@
         )
         allowed = (qd_ref[...] == kd_ref[...]) & (kp_ref[...] <= qp_ref[...])
         weights = jnp.where(allowed, jnp.exp(scores), 0.0).astype(jnp.bfloat16)
-        num_ref[...] += jnp.dot(weights, v_ref[...], preferred_element_type=jnp.float32)
-        den_ref[...] += jnp.sum(weights.astype(jnp.float32), axis=1, keepdims=True)
+        values = v_ref[...]
+        values_one = jnp.concatenate([values, jnp.ones_like(values)], axis=1)
+        both = jnp.dot(weights, values_one, preferred_element_type=jnp.float32)
+        num_ref[...] += both[:, :width]
+        den_ref[...] += both[:, width : width + 1]
 
     whole = lambda i: (0, 0)
     return pl.pallas_call(
@@ -267,36 +270,37 @@
     placement_map = jnp.einsum(
         "rs,rt->st", slot_hot, token_hot, preferred_element_type=jnp.float32
     ).astype(jnp.bfloat16)
-    outgoing = jnp.dot(placement_map, moe_in, preferred_element_type=jnp.float32).astype(
-        jnp.bfloat16
-    )
     experts_ctx = EXPERTS // count_ctx
     share = capacity // slices
+    outgoing = jnp.einsum(
+        "dct,tf->dcf",
+        placement_map.reshape(devices, share, tok_dev),
+        moe_in,
+        preferred_element_type=jnp.float32,
+    ).astype(jnp.bfloat16)
     partner_in = jnp.concatenate([partner_in_low, partner_in_high], axis=1)
     expert_in_both = jnp.concatenate([expert_in, partner_in], axis=0)
     expert_out_both = jnp.concatenate([expert_out, partner_out], axis=0)
-    outgoing = outgoing.reshape(devices, share, MODEL_WIDTH)
     arrived = lax.all_to_all(outgoing, ("ctx", "exp"), split_axis=0, concat_axis=0, tiled=True)
-    tokens_in = arrived.reshape(-1, MODEL_WIDTH)
     gate_up = jnp.einsum(
-        "td,sdf->stf", tokens_in, expert_in_both, preferred_element_type=jnp.float32
+        "dcf,sfh->sdch", arrived, expert_in_both, preferred_element_type=jnp.float32
     )
     activated = (jax.nn.silu(gate_up[..., :ffs_dev]) * gate_up[..., ffs_dev:]).astype(jnp.bfloat16)
     produced = jnp.einsum(
-        "stf,sfd->std", activated, expert_out_both, preferred_element_type=jnp.float32
-    ).astype(jnp.bfloat16)
-    produced = (
-        jnp.sum(produced, axis=0, dtype=jnp.float32)
-        .astype(jnp.bfloat16)
-        .reshape(devices, share, MODEL_WIDTH)
-    )
+        "sdch,shf->sdcf", activated, expert_out_both, preferred_element_type=jnp.float32
+    ).astype(jnp.bfloat16)
+    produced = jnp.sum(produced, axis=0, dtype=jnp.float32).astype(jnp.bfloat16)
     returned = lax.all_to_all(produced, ("ctx", "exp"), split_axis=0, concat_axis=0, tiled=True)
-    slice_sum = returned.reshape(EXPERTS * capacity, MODEL_WIDTH).astype(jnp.float32)
     gate_hot = slot_hot.astype(jnp.float32) * gates.reshape(-1)[:, None]
     combiner = jnp.einsum(
         "rs,rt->ts", gate_hot, token_hot.astype(jnp.float32), precision=lax.Precision.HIGHEST
     )
-    moe_out = jnp.dot(combiner, slice_sum, precision=lax.Precision.HIGHEST)
+    moe_out = jnp.einsum(
+        "tdc,dcf->tf",
+        combiner.reshape(tok_dev, devices, share),
+        returned.astype(jnp.float32),
+        precision=lax.Precision.HIGHEST,
+    )
     new_hidden = (residual_mid + moe_out).astype(jnp.bfloat16)
     return (new_hidden, cache)
 

time: 370 us -> 353 us (0.954)
  local copies, waits for them, and re-layouts: 32.7 us -> 25.2 us
  Pallas kernels: 20.3 us -> 13.8 us
    reshape x4 -> x0, local copies, waits for them, and re-layouts: 13.3 us -> none  [the longest x1 4.38 us: shards(): outgoing = outgoing.reshape(devices, share, MODEL_WIDTH)]
    pallas_call x1, Pallas kernels: 20.3 us -> 13.8 us  [attention_sums(): pl.pallas_call(body, grid=(total // chunk,), in_specs=[pl.BlockSpec((rows...]
    dot_general x4 -> x5, matrix products: 14.7 us -> 12.7 us  [the longest x1 5.52 us: shards(): jnp.einsum('dcf,sfh->sdch', arrived, expert_in_both, preferred_element_ty...]
  transfers between devices with their start and end apart: 8 -> 8, of which waited for: 6 -> 6; matrix products, arithmetic and copies ran while one was open for 9% -> 10% of each run, Pallas kernels for 6% -> 4%
where the time goes in v7:
time: 353 us; the launch traced here: 352 us
  waiting for transfers between devices  176 us (50%)
  blocking collectives  61.2 us (17%)
  local copies, waits for them, and re-layouts  25.2 us (7%)
  starting transfers between devices  24.2 us (7%)
  matrix products  19.6 us (6%)
  other arithmetic  16.2 us (5%)
  between operations  15.7 us (4%)
  Pallas kernels  13.8 us (4%)
    all_to_all x1, blocking collectives, shards(): lax.all_to_all(outgoing, ('ctx', 'exp'), split_axis=0, concat_axis=0, til...  61.2 us
    all_to_all x1, waiting for transfers between devices, shards(): lax.all_to_all(produced, ('ctx', 'exp'), split_axis=0, concat_axis=0, til...  50.2 us
    all_gather x1, waiting for transfers between devices, shards(): every_kv = lax.all_gather(key_values, 'ctx', axis=1, tiled=True)  45.6 us
    ppermute x1, waiting for transfers between devices, shards(): lax.ppermute(expert_out, 'exp', pair)  43.6 us
    all_gather x1, waiting for transfers between devices, shards(): lax.all_gather(jnp.concatenate([q_weight, kv_local, o_weight.T], axis=1),...  17.4 us
    all_to_all x1, waiting for transfers between devices, shards(): lax.all_to_all(attn_part.astype(jnp.bfloat16).reshape(expert_count, tok_d...  15.5 us
    pallas_call x1, Pallas kernels, attention_sums(): pl.pallas_call(body, grid=(total // chunk,), in_specs=[pl.BlockSpec((rows...  13.8 us
  transfers between devices with their start and end apart: 8, of which 6 were waited for; matrix products, arithmetic and copies ran while one was open for 10% of the time, Pallas kernels for 4%

profile of v7, /device:TPU:1, one launch (start us, length us, event | category | flops | bytes accessed | tf_op | source)
XLA Modules:
  0.0 351.6 jit_solution(16165860828510841787)
XLA Ops:
  8.0 1.6 pad_maximum_fusion
  9.6 3.6 %collective-permute-start = (bf16[1,384,2048]{2,1,0:T(8,128)(2,1)}, bf16[1,384,2048]{2,1,0:T(8,128)(2,1)S(1)}, u32[]{:S(2)}, u32[]{:S(2)}) collective-permute-start(bf16[1,384,2048]{2,1,0:T(8,128)(2,1)} %param.25), channel_id=1, source_target_pairs={{0,1},{1,0},{2,3},{3,2},{4,5},{5,4},{6,7},{7,6},{8,9},{9,8},{10,11... | collective-permute-start | bytes 4718600 | tf_op jit(solution)/shard_map/ppermute | solution.py:174
  16.4 4.2 %all-to-all-start = ((bf16[8,32,2048]{2,1,0:T(8,128)(2,1)}), bf16[8,32,2048]{2,1,0:T(8,128)(2,1)S(1)}, u32[]{:S(2)}, u32[]{:S(2)}) async-start(bf16[8,32,2048]{2,1,0:T(8,128)(2,1)} %broadcast_in_dim.8), calls=%async_computation | async-start | bytes 2097152 | tf_op jit(solution)/shard_map/all_to_all | solution.py:149
  23.2 43.6 %collective-permute-done = bf16[1,384,2048]{2,1,0:T(8,128)(2,1)S(1)} collective-permute-done((bf16[1,384,2048]{2,1,0:T(8,128)(2,1)}, bf16[1,384,2048]{2,1,0:T(8,128)(2,1)S(1)}, u32[]{:S(2)}, u32[]{:S(2)}) %collective-permute-start) | collective-permute-done | bytes 1572896 | tf_op jit(solution)/shard_map/ppermute | solution.py:174
  66.7 17.4 %all-gather.3.cloned.1.call-done = bf16[2048,1280]{1,0:T(8,128)(2,1)} async-done(((bf16[64,1280]{1,0:T(8,128)(2,1)}), bf16[2048,1280]{1,0:T(8,128)(2,1)}) %all-gather.3.cloned.1.call-update) | async-done | bytes 5242896 | tf_op jit(solution)/shard_map/all_gather | solution.py:171
  84.2 3.3 all-to-all-done
  87.5 2.9 fusion.7
  92.0 3.2 copy.86
  95.2 2.0 fusion.69
  97.5 2.7 collective-permute-start.1
  104.0 1.3 fusion.56
  105.3 1.9 slice.76
  107.2 2.0 reshape.484
  109.2 1.4 multiply_reduce_fusion
  110.6 1.4 multiply_multiply_fusion
  113.6 45.6 %all-gather.5.cloned.1.call-done.k_ref.v_ref = bf16[2,8192,128]{2,1,0:T(8,128)(2,1)} async-done(((bf16[2,256,128]{2,1,0:T(8,128)(2,1)}), bf16[2,8192,128]{2,1,0:T(8,128)(2,1)}) %all-gather.5.cloned.1.call-update) | async-done | bytes 4194320 | tf_op jit(solution)/shard_map/all_gather | solution.py:201
  159.2 13.8 %shard_map.140 = (f32[1024,128]{1,0:T(8,128)}, f32[1024,1]{1,0:T(8,128)}) custom-call(bf16[1024,128]{1,0:T(8,128)(2,1)} %bitcast.80, bf16[2,8192,128]{2,1,0:T(8,128)(2,1)} %all-gather.5.cloned.1.call-done.k_ref.v_ref, bf16[2,8192,128]{2,1,0:T(8,128)(2,1)} %all-gather.5.cloned.1.call-done.k_ref.v_ref, s32[1024,1]{1,0:T(8,128)} %bitcast.79, ...), custom_call_target="tpu_custom_call" | custom-call | tf_op jit(solution)/shard_map/pallas_call | solution.py:93
  173.1 2.1 copy.85
  175.1 1.2 reduce.3
  177.5 3.3 convolution_convert_fusion.1
  180.8 6.4 %all-to-all-start.1 = ((bf16[8,32,2048]{2,1,0:T(8,128)(2,1)}), bf16[8,32,2048]{2,1,0:T(8,128)(2,1)}, u32[]{:S(2)}, u32[]{:S(2)}) async-start(bf16[8,32,2048]{2,1,0:T(8,128)(2,1)} %bitcast.82), calls=%async_computation.1 | async-start | bytes 2097152 | tf_op jit(solution)/shard_map/all_to_all | solution.py:234
  188.6 15.5 %all-to-all-done.1 = bf16[8,32,2048]{2,1,0:T(8,128)(2,1)} async-done(((bf16[8,32,2048]{2,1,0:T(8,128)(2,1)}), bf16[8,32,2048]{2,1,0:T(8,128)(2,1)}, u32[]{:S(2)}, u32[]{:S(2)}) %all-to-all-start.1) | async-done | bytes 1048608 | tf_op jit(solution)/shard_map/all_to_all | solution.py:234
  204.1 1.4 convert_reduce_fusion.1
  205.6 1.7 convolution_convert_fusion
  207.3 2.2 copy.97
  209.5 61.2 %all_to_all.20 = bf16[256,2,2048]{2,1,0:T(2,128)(2,1)S(1)} all-to-all(bf16[256,2,2048]{2,1,0:T(2,128)(2,1)S(1)} %copy.97), channel_id=1, replica_groups=mesh['ctx'=32,'exp'=8] {'ctx','exp'}, dimensions={0} | all-to-all | bytes 4194304 | tf_op jit(solution)/shard_map/all_to_all | solution.py:284
  270.7 5.5 %fusion.15 = f32[2,256,2,768]{1,3,2,0:T(8,128)S(1)} fusion(bf16[256,2,2048]{2,1,0:T(2,128)(2,1)S(1)} %all_to_all.20, bf16[1,1024,768]{1,2,0:T(8,128)(2,1)} %collective-permute-done.2, bf16[1,1024,768]{1,2,0:T(8,128)(2,1)} %collective-permute-done.1, bf16[1,2048,768]{1,2,0:T(8,128)(2,1)S(1)} %copy.86), kind=kOutput, calls=%fused_computation.22 | convolution fusion | flops 3240099840 | bytes 11534336 | tf_op jit(solution)/shard_map/dcf,sfh->sdch/dot_general | solution.py:285
  276.2 2.4 convert_reduce_fusion
  278.7 3.5 copy.100
  282.2 6.9 %all-to-all-start.3 = ((bf16[256,2,2048]{2,1,0:T(2,128)(2,1)}), bf16[256,2,2048]{2,1,0:T(2,128)(2,1)S(1)}, u32[]{:S(2)}, u32[]{:S(2)}) async-start(bf16[256,2,2048]{2,1,0:T(2,128)(2,1)} %copy.100), calls=%async_computation.3 | async-start | bytes 4194304 | tf_op jit(solution)/shard_map/all_to_all | solution.py:293
  291.8 50.2 %all-to-all-done.3 = bf16[256,2,2048]{2,1,0:T(2,128)(2,1)S(1)} async-done(((bf16[256,2,2048]{2,1,0:T(2,128)(2,1)}), bf16[256,2,2048]{2,1,0:T(2,128)(2,1)S(1)}, u32[]{:S(2)}, u32[]{:S(2)}) %all-to-all-start.3) | async-done | bytes 2097184 | tf_op jit(solution)/shard_map/all_to_all | solution.py:293
  341.9 2.8 fusion.10
  (84 shorter events, 17.8 us)
Async XLA Ops:
  7.2 77.0 %all-gather.3.cloned.1.call-start = ((), (), s32[]{:S(2)}) async-start(), calls=%async_computation.4 | async-start | bytes 5406720 | tf_op jit(solution)/shard_map/all_gather | solution.py:171
  8.0 12.7 %copy-start.5 = (s32[2]{0:T(128)S(1)}, s32[2]{0:T(128)}, u32[]{:S(2)}) copy-start(s32[2]{0:T(128)} %param.14) | copy-start | bytes 28
  9.6 57.2 %collective-permute-start = (bf16[1,384,2048]{2,1,0:T(8,128)(2,1)}, bf16[1,384,2048]{2,1,0:T(8,128)(2,1)S(1)}, u32[]{:S(2)}, u32[]{:S(2)}) collective-permute-start(bf16[1,384,2048]{2,1,0:T(8,128)(2,1)} %param.25), channel_id=1, source_target_pairs={{0,1},{1,0},{2,3},{3,2},{4,5},{5,4},{6,7},{7,6},{8,9},{9,8},{10,11... | collective-permute-start | bytes 4718600 | tf_op jit(solution)/shard_map/ppermute | solution.py:174
  16.4 71.1 %all-to-all-start = ((bf16[8,32,2048]{2,1,0:T(8,128)(2,1)}), bf16[8,32,2048]{2,1,0:T(8,128)(2,1)S(1)}, u32[]{:S(2)}, u32[]{:S(2)}) async-start(bf16[8,32,2048]{2,1,0:T(8,128)(2,1)} %broadcast_in_dim.8), calls=%async_computation | async-start | bytes 2097152 | tf_op jit(solution)/shard_map/all_to_all | solution.py:149
  20.6 138.6 %all-gather.5.cloned.1.call-start = ((), (), s32[]{:S(2)}) async-start(), calls=%async_computation.5 | async-start | bytes 4325376 | tf_op jit(solution)/shard_map/all_gather | solution.py:201
  66.7 23.6 %copy-start.11 = (bf16[1,384,2048]{2,1,0:T(8,128)(2,1)}, bf16[1,384,2048]{2,1,0:T(8,128)(2,1)S(1)}, u32[]{:S(2)}) copy-start(bf16[1,384,2048]{2,1,0:T(8,128)(2,1)S(1)} %collective-permute-done) | copy-start | bytes 4718596
  87.5 3.1 copy-start.8
  90.4 0.9 copy-start.1
  95.2 5.0 %copy-start.3 = (s32[32,8]{0,1:T(8,128)S(1)}, s32[32,8]{0,1:T(8,128)}, u32[]{:S(2)}) copy-start(s32[32,8]{0,1:T(8,128)} %param.15) | copy-start | bytes 3076
  97.2 91.3 %collective-permute-start.2 = (bf16[1,1024,768]{1,2,0:T(8,128)(2,1)}, bf16[1,1024,768]{1,2,0:T(8,128)(2,1)}, u32[]{:S(2)}, u32[]{:S(2)}) collective-permute-start(bf16[1,1024,768]{1,2,0:T(8,128)(2,1)} %get-tuple-element.28), channel_id=1, source_target_pairs={{0,1},{1,0},{2,3},{3,2},{4,5},{5,4},{6,7},{7,6},{8,9},{9,8},{10,11... | collective-permute-start | bytes 4718600 | tf_op jit(solution)/shard_map/ppermute | solution.py:245
  97.5 91.0 %collective-permute-start.1 = (bf16[1,1024,768]{1,2,0:T(8,128)(2,1)}, bf16[1,1024,768]{1,2,0:T(8,128)(2,1)}, u32[]{:S(2)}, u32[]{:S(2)}) collective-permute-start(bf16[1,1024,768]{1,2,0:T(8,128)(2,1)} %get-tuple-element.29), channel_id=1, source_target_pairs={{0,1},{1,0},{2,3},{3,2},{4,5},{5,4},{6,7},{7,6},{8,9},{9,8},{10,11... | collective-permute-start | bytes 4718600 | tf_op jit(solution)/shard_map/ppermute | solution.py:244
  102.2 8.4 %copy-start.9 = (f32[128]{0:T(128)S(1)}, f32[128]{0:T(128)}, u32[]{:S(2)}) copy-start(f32[128]{0:T(128)} %param.20) | copy-start | bytes 1540
  180.8 6.7 %copy-start.6 = (s32[256]{0:T(256)S(1)}, s32[256]{0:T(256)}, u32[]{:S(2)}) copy-start(s32[256]{0:T(256)} %get-tuple-element.40) | copy-start | bytes 3076
  180.8 24.7 %copy-start = (bf16[32,2048]{1,0:T(8,128)(2,1)S(1)}, bf16[32,2048]{1,0:T(8,128)(2,1)}, u32[]{:S(2)}) copy-start(bf16[32,2048]{1,0:T(8,128)(2,1)} %param.13) | copy-start | bytes 393220
  180.8 24.8 %copy-start.2 = (f32[2048]{0:T(1024)S(1)}, f32[2048]{0:T(1024)}, u32[]{:S(2)}) copy-start(f32[2048]{0:T(1024)} %param.23) | copy-start | bytes 24580
  180.8 23.3 %all-to-all-start.1 = ((bf16[8,32,2048]{2,1,0:T(8,128)(2,1)}), bf16[8,32,2048]{2,1,0:T(8,128)(2,1)}, u32[]{:S(2)}, u32[]{:S(2)}) async-start(bf16[8,32,2048]{2,1,0:T(8,128)(2,1)} %bitcast.82), calls=%async_computation.1 | async-start | bytes 2097152 | tf_op jit(solution)/shard_map/all_to_all | solution.py:234
  270.7 5.5 %copy-start.10 = (bf16[1,384,2048]{2,1,0:T(8,128)(2,1)S(1)}, bf16[1,384,2048]{2,1,0:T(8,128)(2,1)}, u32[]{:S(2)}) copy-start(bf16[1,384,2048]{2,1,0:T(8,128)(2,1)} %param.25) | copy-start | bytes 4718596
  270.7 5.5 %copy-start.12 = (bf16[1,384,2048]{2,1,0:T(8,128)(2,1)S(1)}, bf16[1,384,2048]{2,1,0:T(8,128)(2,1)}, u32[]{:S(2)}) copy-start(bf16[1,384,2048]{2,1,0:T(8,128)(2,1)} %copy-done.11) | copy-start | bytes 4718596
  282.2 6.9 %copy-start.4 = (f32[32,8]{0,1:T(8,128)S(1)}, f32[32,8]{0,1:T(8,128)}, u32[]{:S(2)}) copy-start(f32[32,8]{0,1:T(8,128)} %param.16) | copy-start | bytes 3076
  282.2 7.1 %copy-start.7 = (s32[256]{0:T(256)S(1)}, s32[256]{0:T(256)}, u32[]{:S(2)}) copy-start(s32[256]{0:T(256)} %get-tuple-element.40) | copy-start | bytes 3076
  282.2 59.8 %all-to-all-start.3 = ((bf16[256,2,2048]{2,1,0:T(2,128)(2,1)}), bf16[256,2,2048]{2,1,0:T(2,128)(2,1)S(1)}, u32[]{:S(2)}, u32[]{:S(2)}) async-start(bf16[256,2,2048]{2,1,0:T(2,128)(2,1)} %copy.100), calls=%async_computation.3 | async-start | bytes 4194304 | tf_op jit(solution)/shard_map/all_to_all | solution.py:293
Sparse Core Ops, SparseCore 0:
  9.8 74.2 all-gather.2
  92.2 67.0 all-gather.4

commit v8 on v7

--- a/solution.py
+++ b/solution.py
@@ -64,15 +64,19 @@
     )
 
 
-def attention_sums(q_rows, every_kv, q_pos, q_doc, k_pos, k_doc, scale, chunk):
+def attention_context(q_rows, every_kv, q_pos, q_doc, k_pos, k_doc, scale, chunk, heads):
     rows, width = q_rows.shape
+    tok = rows // heads
     total = every_kv.shape[1]
-
-    def body(q_ref, k_ref, v_ref, qp_ref, qd_ref, kp_ref, kd_ref, num_ref, den_ref):
-        @pl.when(pl.program_id(0) == 0)
+    steps = total // chunk
+
+    def body(q_ref, k_ref, v_ref, qp_ref, qd_ref, kp_ref, kd_ref, out_ref, num_acc, den_acc):
+        step = pl.program_id(0)
+
+        @pl.when(step == 0)
         def _():
-            num_ref[...] = jnp.zeros_like(num_ref)
-            den_ref[...] = jnp.zeros_like(den_ref)
+            num_acc[...] = jnp.zeros_like(num_acc)
+            den_acc[...] = jnp.zeros_like(den_acc)
 
         scores = (
             lax.dot_general(
@@ -86,13 +90,21 @@
         values = v_ref[...]
         values_one = jnp.concatenate([values, jnp.ones_like(values)], axis=1)
         both = jnp.dot(weights, values_one, preferred_element_type=jnp.float32)
-        num_ref[...] += both[:, :width]
-        den_ref[...] += both[:, width : width + 1]
+        num_acc[...] += both[:, :width]
+        den_acc[...] += both[:, width : width + 1]
+
+        @pl.when(step == steps - 1)
+        def _():
+            for head in range(heads):
+                part = slice(head * tok, (head + 1) * tok)
+                out_ref[:, head * width : (head + 1) * width] = (
+                    num_acc[part, :] / den_acc[part, :]
+                ).astype(out_ref.dtype)
 
     whole = lambda i: (0, 0)
     return pl.pallas_call(
         body,
-        grid=(total // chunk,),
+        grid=(steps,),
         in_specs=[
             pl.BlockSpec((rows, width), whole),
             pl.BlockSpec((None, chunk, width), lambda i: (0, i, 0)),
@@ -102,11 +114,9 @@
             pl.BlockSpec((1, chunk), lambda i: (0, i)),
             pl.BlockSpec((1, chunk), lambda i: (0, i)),
         ],
-        out_specs=[pl.BlockSpec((rows, width), whole), pl.BlockSpec((rows, 1), whole)],
-        out_shape=[
-            jax.ShapeDtypeStruct((rows, width), jnp.float32),
-            jax.ShapeDtypeStruct((rows, 1), jnp.float32),
-        ],
+        out_specs=pl.BlockSpec((tok, heads * width), whole),
+        out_shape=jax.ShapeDtypeStruct((tok, heads * width), jnp.bfloat16),
+        scratch_shapes=[pltpu.VMEM((rows, width), jnp.float32), pltpu.VMEM((rows, 1), jnp.float32)],
         compiler_params=pltpu.CompilerParams(dimension_semantics=("arbitrary",)),
     )(q_rows, every_kv, every_kv, q_pos, q_doc, k_pos, k_doc)
 
@@ -204,7 +214,7 @@
     key_pos = mirrored_position(jnp.arange(total_rows, dtype=jnp.int32), count_ctx, tok_ctx)
     key_doc, unused_rope = document_info(key_pos, lengths)
     q_rows = jnp.transpose(queries, (1, 0, 2)).reshape(q_dev * tok_ctx, HEAD_SIZE)
-    sums = attention_sums(
+    context = attention_context(
         q_rows,
         every_kv,
         jnp.tile(query_pos, q_dev)[:, None],
@@ -213,10 +223,8 @@
         key_doc[None, :],
         score_scale,
         chunk,
-    )
-    numerator = jnp.transpose(sums[0].reshape(q_dev, tok_ctx, HEAD_SIZE), (1, 0, 2))
-    denominator = jnp.transpose(sums[1].reshape(q_dev, tok_ctx, 1), (1, 0, 2))
-    context = (numerator / denominator).astype(jnp.bfloat16).reshape(tok_ctx, q_dev * HEAD_SIZE)
+        q_dev,
+    )
     def block_start(block_no):
         holder = jnp.where(block_no < count_ctx, block_no, 2 * count_ctx - 1 - block_no)
         return holder * tok_ctx + jnp.where(block_no < count_ctx, 0, half_rows)

time: 353 us -> 352 us (level)
    ppermute x1, waiting for transfers between devices: 0.01 us -> 4.09 us  [shards(): lax.ppermute(expert_in[:, :rows_half], 'exp', pair)]
  transfers between devices with their start and end apart: 8 -> 8, of which waited for: 6 -> 7; matrix products, arithmetic and copies ran while one was open for 10% -> 9% of each run, Pallas kernels for 4% -> 4%
where the time goes in v8:
time: 352 us; the launch traced here: 351 us
  waiting for transfers between devices  177 us (50%)
  blocking collectives  64.3 us (18%)
  starting transfers between devices  24.2 us (7%)
  local copies, waits for them, and re-layouts  23.1 us (7%)
  matrix products  19.7 us (6%)
  between operations  15.7 us (4%)
  other arithmetic  13.9 us (4%)
  Pallas kernels  13.7 us (4%)
    all_to_all x1, blocking collectives, shards(): lax.all_to_all(outgoing, ('ctx', 'exp'), split_axis=0, concat_axis=0, til...  64.3 us
    all_to_all x1, waiting for transfers between devices, shards(): lax.all_to_all(produced, ('ctx', 'exp'), split_axis=0, concat_axis=0, til...  50.2 us
    all_gather x1, waiting for transfers between devices, shards(): every_kv = lax.all_gather(key_values, 'ctx', axis=1, tiled=True)  45.6 us
    ppermute x1, waiting for transfers between devices, shards(): lax.ppermute(expert_out, 'exp', pair)  43.6 us
    all_gather x1, waiting for transfers between devices, shards(): lax.all_gather(jnp.concatenate([q_weight, kv_local, o_weight.T], axis=1),...  17.4 us
    pallas_call x1, Pallas kernels, attention_context(): pl.pallas_call(body, grid=(steps,), in_specs=[pl.BlockSpec((rows, width),...  13.7 us
    all_to_all x1, waiting for transfers between devices, shards(): lax.all_to_all(attn_part.astype(jnp.bfloat16).reshape(expert_count, tok_d...  12.4 us
  transfers between devices with their start and end apart: 8, of which 7 were waited for; matrix products, arithmetic and copies ran while one was open for 9% of the time, Pallas kernels for 4%

profile of v8, /device:TPU:1, one launch (start us, length us, event | category | flops | bytes accessed | tf_op | source)
XLA Modules:
  0.0 351.2 jit_solution(6476968499776919544)
XLA Ops:
  8.0 1.5 pad_maximum_fusion
  9.6 3.6 %collective-permute-start = (bf16[1,384,2048]{2,1,0:T(8,128)(2,1)}, bf16[1,384,2048]{2,1,0:T(8,128)(2,1)S(1)}, u32[]{:S(2)}, u32[]{:S(2)}) collective-permute-start(bf16[1,384,2048]{2,1,0:T(8,128)(2,1)} %param.25), channel_id=1, source_target_pairs={{0,1},{1,0},{2,3},{3,2},{4,5},{5,4},{6,7},{7,6},{8,9},{9,8},{10,11... | collective-permute-start | bytes 4718600 | tf_op jit(solution)/shard_map/ppermute | solution.py:184
  15.3 1.1 broadcast_in_dim.8
  16.4 4.2 %all-to-all-start = ((bf16[8,32,2048]{2,1,0:T(8,128)(2,1)}), bf16[8,32,2048]{2,1,0:T(8,128)(2,1)S(1)}, u32[]{:S(2)}, u32[]{:S(2)}) async-start(bf16[8,32,2048]{2,1,0:T(8,128)(2,1)} %broadcast_in_dim.8), calls=%async_computation | async-start | bytes 2097152 | tf_op jit(solution)/shard_map/all_to_all | solution.py:159
  23.1 43.6 %collective-permute-done = bf16[1,384,2048]{2,1,0:T(8,128)(2,1)S(1)} collective-permute-done((bf16[1,384,2048]{2,1,0:T(8,128)(2,1)}, bf16[1,384,2048]{2,1,0:T(8,128)(2,1)S(1)}, u32[]{:S(2)}, u32[]{:S(2)}) %collective-permute-start) | collective-permute-done | bytes 1572896 | tf_op jit(solution)/shard_map/ppermute | solution.py:184
  66.7 17.4 %all-gather.3.cloned.1.call-done = bf16[2048,1280]{1,0:T(8,128)(2,1)} async-done(((bf16[64,1280]{1,0:T(8,128)(2,1)}), bf16[2048,1280]{1,0:T(8,128)(2,1)}) %all-gather.3.cloned.1.call-update) | async-done | bytes 5242896 | tf_op jit(solution)/shard_map/all_gather | solution.py:181
  84.2 3.3 all-to-all-done
  87.5 2.9 fusion.7
  92.0 3.2 copy.82
  95.2 2.0 fusion.68
  97.5 2.7 collective-permute-start.1
  104.0 1.3 fusion.55
  105.3 1.9 slice.76
  107.2 2.0 reshape.475
  109.2 1.4 multiply_reduce_fusion
  110.6 1.4 multiply_multiply_fusion
  113.6 45.6 %all-gather.5.cloned.1.call-done.k_ref.v_ref = bf16[2,8192,128]{2,1,0:T(8,128)(2,1)} async-done(((bf16[2,256,128]{2,1,0:T(8,128)(2,1)}), bf16[2,8192,128]{2,1,0:T(8,128)(2,1)}) %all-gather.5.cloned.1.call-update) | async-done | bytes 4194320 | tf_op jit(solution)/shard_map/all_gather | solution.py:211
  159.2 13.7 %shard_map.140 = bf16[256,512]{1,0:T(8,128)(2,1)} custom-call(bf16[1024,128]{1,0:T(8,128)(2,1)} %bitcast.71, bf16[2,8192,128]{2,1,0:T(8,128)(2,1)} %all-gather.5.cloned.1.call-done.k_ref.v_ref, bf16[2,8192,128]{2,1,0:T(8,128)(2,1)} %all-gather.5.cloned.1.call-done.k_ref.v_ref, s32[1024,1]{1,0:T(8,128)} %bitcast.70, s32[1024,1]{1,0:T(8,128)} %bitcast.69, ...), custom_call_target="tpu_custom_call" | custom-call | tf_op jit(solution)/shard_map/pallas_call | solution.py:105
  173.0 3.4 convolution_convert_fusion.1
  176.4 6.4 %all-to-all-start.1 = ((bf16[8,32,2048]{2,1,0:T(8,128)(2,1)}), bf16[8,32,2048]{2,1,0:T(8,128)(2,1)}, u32[]{:S(2)}, u32[]{:S(2)}) async-start(bf16[8,32,2048]{2,1,0:T(8,128)(2,1)} %bitcast.73), calls=%async_computation.1 | async-start | bytes 2097152 | tf_op jit(solution)/shard_map/all_to_all | solution.py:242
  184.1 4.1 %collective-permute-done.1 = bf16[1,1024,768]{1,2,0:T(8,128)(2,1)} collective-permute-done((bf16[1,1024,768]{1,2,0:T(8,128)(2,1)}, bf16[1,1024,768]{1,2,0:T(8,128)(2,1)}, u32[]{:S(2)}, u32[]{:S(2)}) %collective-permute-start.1) | collective-permute-done | bytes 1572896 | tf_op jit(solution)/shard_map/ppermute | solution.py:252
  188.2 12.4 %all-to-all-done.1 = bf16[8,32,2048]{2,1,0:T(8,128)(2,1)} async-done(((bf16[8,32,2048]{2,1,0:T(8,128)(2,1)}), bf16[8,32,2048]{2,1,0:T(8,128)(2,1)}, u32[]{:S(2)}, u32[]{:S(2)}) %all-to-all-start.1) | async-done | bytes 1048608 | tf_op jit(solution)/shard_map/all_to_all | solution.py:242
  200.7 1.4 convert_reduce_fusion.1
  202.2 1.7 convolution_convert_fusion
  203.9 2.2 copy.93
  206.1 64.3 %all_to_all.20 = bf16[256,2,2048]{2,1,0:T(2,128)(2,1)S(1)} all-to-all(bf16[256,2,2048]{2,1,0:T(2,128)(2,1)S(1)} %copy.93), channel_id=1, replica_groups=mesh['ctx'=32,'exp'=8] {'ctx','exp'}, dimensions={0} | all-to-all | bytes 4194304 | tf_op jit(solution)/shard_map/all_to_all | solution.py:292
  270.3 5.5 %fusion.15 = f32[2,256,2,768]{1,3,2,0:T(8,128)S(1)} fusion(bf16[256,2,2048]{2,1,0:T(2,128)(2,1)S(1)} %all_to_all.20, bf16[1,1024,768]{1,2,0:T(8,128)(2,1)} %collective-permute-done.2, bf16[1,1024,768]{1,2,0:T(8,128)(2,1)} %collective-permute-done.1, bf16[1,2048,768]{1,2,0:T(8,128)(2,1)S(1)} %copy.82), kind=kOutput, calls=%fused_computation.22 | convolution fusion | flops 3240099840 | bytes 11534336 | tf_op jit(solution)/shard_map/dcf,sfh->sdch/dot_general | solution.py:293
  275.9 2.4 convert_reduce_fusion
  278.3 3.5 copy.96
  281.8 6.9 %all-to-all-start.3 = ((bf16[256,2,2048]{2,1,0:T(2,128)(2,1)}), bf16[256,2,2048]{2,1,0:T(2,128)(2,1)S(1)}, u32[]{:S(2)}, u32[]{:S(2)}) async-start(bf16[256,2,2048]{2,1,0:T(2,128)(2,1)} %copy.96), calls=%async_computation.3 | async-start | bytes 4194304 | tf_op jit(solution)/shard_map/all_to_all | solution.py:301
  291.4 50.2 %all-to-all-done.3 = bf16[256,2,2048]{2,1,0:T(2,128)(2,1)S(1)} async-done(((bf16[256,2,2048]{2,1,0:T(2,128)(2,1)}), bf16[256,2,2048]{2,1,0:T(2,128)(2,1)S(1)}, u32[]{:S(2)}, u32[]{:S(2)}) %all-to-all-start.3) | async-done | bytes 2097184 | tf_op jit(solution)/shard_map/all_to_all | solution.py:301
  341.6 2.8 fusion.10
  (80 shorter events, 15.6 us)
Async XLA Ops:
  7.2 77.0 %all-gather.3.cloned.1.call-start = ((), (), s32[]{:S(2)}) async-start(), calls=%async_computation.4 | async-start | bytes 5406720 | tf_op jit(solution)/shard_map/all_gather | solution.py:181
  8.0 12.6 %copy-start.5 = (s32[2]{0:T(128)S(1)}, s32[2]{0:T(128)}, u32[]{:S(2)}) copy-start(s32[2]{0:T(128)} %param.14) | copy-start | bytes 28
  9.6 57.2 %collective-permute-start = (bf16[1,384,2048]{2,1,0:T(8,128)(2,1)}, bf16[1,384,2048]{2,1,0:T(8,128)(2,1)S(1)}, u32[]{:S(2)}, u32[]{:S(2)}) collective-permute-start(bf16[1,384,2048]{2,1,0:T(8,128)(2,1)} %param.25), channel_id=1, source_target_pairs={{0,1},{1,0},{2,3},{3,2},{4,5},{5,4},{6,7},{7,6},{8,9},{9,8},{10,11... | collective-permute-start | bytes 4718600 | tf_op jit(solution)/shard_map/ppermute | solution.py:184
  16.4 71.1 %all-to-all-start = ((bf16[8,32,2048]{2,1,0:T(8,128)(2,1)}), bf16[8,32,2048]{2,1,0:T(8,128)(2,1)S(1)}, u32[]{:S(2)}, u32[]{:S(2)}) async-start(bf16[8,32,2048]{2,1,0:T(8,128)(2,1)} %broadcast_in_dim.8), calls=%async_computation | async-start | bytes 2097152 | tf_op jit(solution)/shard_map/all_to_all | solution.py:159
  20.6 138.6 %all-gather.5.cloned.1.call-start = ((), (), s32[]{:S(2)}) async-start(), calls=%async_computation.5 | async-start | bytes 4325376 | tf_op jit(solution)/shard_map/all_gather | solution.py:211
  66.7 23.6 %copy-start.11 = (bf16[1,384,2048]{2,1,0:T(8,128)(2,1)}, bf16[1,384,2048]{2,1,0:T(8,128)(2,1)S(1)}, u32[]{:S(2)}) copy-start(bf16[1,384,2048]{2,1,0:T(8,128)(2,1)S(1)} %collective-permute-done) | copy-start | bytes 4718596
  87.5 3.1 copy-start.8
  90.4 0.9 copy-start.1
  95.2 5.0 %copy-start.3 = (s32[32,8]{0,1:T(8,128)S(1)}, s32[32,8]{0,1:T(8,128)}, u32[]{:S(2)}) copy-start(s32[32,8]{0,1:T(8,128)} %param.15) | copy-start | bytes 3076
  97.2 86.9 %collective-permute-start.2 = (bf16[1,1024,768]{1,2,0:T(8,128)(2,1)}, bf16[1,1024,768]{1,2,0:T(8,128)(2,1)}, u32[]{:S(2)}, u32[]{:S(2)}) collective-permute-start(bf16[1,1024,768]{1,2,0:T(8,128)(2,1)} %get-tuple-element.24), channel_id=1, source_target_pairs={{0,1},{1,0},{2,3},{3,2},{4,5},{5,4},{6,7},{7,6},{8,9},{9,8},{10,11... | collective-permute-start | bytes 4718600 | tf_op jit(solution)/shard_map/ppermute | solution.py:253
  97.5 90.7 %collective-permute-start.1 = (bf16[1,1024,768]{1,2,0:T(8,128)(2,1)}, bf16[1,1024,768]{1,2,0:T(8,128)(2,1)}, u32[]{:S(2)}, u32[]{:S(2)}) collective-permute-start(bf16[1,1024,768]{1,2,0:T(8,128)(2,1)} %get-tuple-element.25), channel_id=1, source_target_pairs={{0,1},{1,0},{2,3},{3,2},{4,5},{5,4},{6,7},{7,6},{8,9},{9,8},{10,11... | collective-permute-start | bytes 4718600 | tf_op jit(solution)/shard_map/ppermute | solution.py:252
  102.2 8.4 %copy-start.9 = (f32[128]{0:T(128)S(1)}, f32[128]{0:T(128)}, u32[]{:S(2)}) copy-start(f32[128]{0:T(128)} %param.20) | copy-start | bytes 1540
  176.4 6.7 %copy-start.6 = (s32[256]{0:T(256)S(1)}, s32[256]{0:T(256)}, u32[]{:S(2)}) copy-start(s32[256]{0:T(256)} %get-tuple-element.36) | copy-start | bytes 3076
  176.4 25.7 %copy-start = (bf16[32,2048]{1,0:T(8,128)(2,1)S(1)}, bf16[32,2048]{1,0:T(8,128)(2,1)}, u32[]{:S(2)}) copy-start(bf16[32,2048]{1,0:T(8,128)(2,1)} %param.13) | copy-start | bytes 393220
  176.4 25.9 %copy-start.2 = (f32[2048]{0:T(1024)S(1)}, f32[2048]{0:T(1024)}, u32[]{:S(2)}) copy-start(f32[2048]{0:T(1024)} %param.23) | copy-start | bytes 24580
  176.4 24.3 %all-to-all-start.1 = ((bf16[8,32,2048]{2,1,0:T(8,128)(2,1)}), bf16[8,32,2048]{2,1,0:T(8,128)(2,1)}, u32[]{:S(2)}, u32[]{:S(2)}) async-start(bf16[8,32,2048]{2,1,0:T(8,128)(2,1)} %bitcast.73), calls=%async_computation.1 | async-start | bytes 2097152 | tf_op jit(solution)/shard_map/all_to_all | solution.py:242
  270.3 5.5 %copy-start.10 = (bf16[1,384,2048]{2,1,0:T(8,128)(2,1)S(1)}, bf16[1,384,2048]{2,1,0:T(8,128)(2,1)}, u32[]{:S(2)}) copy-start(bf16[1,384,2048]{2,1,0:T(8,128)(2,1)} %param.25) | copy-start | bytes 4718596
  270.3 5.5 %copy-start.12 = (bf16[1,384,2048]{2,1,0:T(8,128)(2,1)S(1)}, bf16[1,384,2048]{2,1,0:T(8,128)(2,1)}, u32[]{:S(2)}) copy-start(bf16[1,384,2048]{2,1,0:T(8,128)(2,1)} %copy-done.11) | copy-start | bytes 4718596
  281.8 6.9 %copy-start.4 = (f32[32,8]{0,1:T(8,128)S(1)}, f32[32,8]{0,1:T(8,128)}, u32[]{:S(2)}) copy-start(f32[32,8]{0,1:T(8,128)} %param.16) | copy-start | bytes 3076
  281.8 7.1 %copy-start.7 = (s32[256]{0:T(256)S(1)}, s32[256]{0:T(256)}, u32[]{:S(2)}) copy-start(s32[256]{0:T(256)} %get-tuple-element.36) | copy-start | bytes 3076
  281.8 59.8 %all-to-all-start.3 = ((bf16[256,2,2048]{2,1,0:T(2,128)(2,1)}), bf16[256,2,2048]{2,1,0:T(2,128)(2,1)S(1)}, u32[]{:S(2)}, u32[]{:S(2)}) async-start(bf16[256,2,2048]{2,1,0:T(2,128)(2,1)} %copy.96), calls=%async_computation.3 | async-start | bytes 4194304 | tf_op jit(solution)/shard_map/all_to_all | solution.py:301
Sparse Core Ops, SparseCore 0:
  9.8 74.2 all-gather.2
  92.2 67.0 all-gather.4

commit v9 on v8

--- a/solution.py
+++ b/solution.py
@@ -246,12 +246,8 @@
         concat_axis=0,
         tiled=True,
     )
-    attn_pieces, partner_in_low, partner_in_high = lax.optimization_barrier(
-        (
-            attn_pieces,
-            lax.ppermute(expert_in[:, :rows_half], "exp", pair),
-            lax.ppermute(expert_in[:, rows_half:], "exp", pair),
-        )
+    attn_pieces, partner_in_low = lax.optimization_barrier(
+        (attn_pieces, lax.ppermute(expert_in[:, :rows_half], "exp", pair))
     )
     attn_own = jnp.sum(attn_pieces, axis=0, dtype=jnp.float32)
     residual_mid = hidden.astype(jnp.float32) + attn_own
@@ -286,10 +282,15 @@
         moe_in,
         preferred_element_type=jnp.float32,
     ).astype(jnp.bfloat16)
+    arrived, partner_in_high = lax.optimization_barrier(
+        (
+            lax.all_to_all(outgoing, ("ctx", "exp"), split_axis=0, concat_axis=0, tiled=True),
+            lax.ppermute(expert_in[:, rows_half:], "exp", pair),
+        )
+    )
     partner_in = jnp.concatenate([partner_in_low, partner_in_high], axis=1)
     expert_in_both = jnp.concatenate([expert_in, partner_in], axis=0)
     expert_out_both = jnp.concatenate([expert_out, partner_out], axis=0)
-    arrived = lax.all_to_all(outgoing, ("ctx", "exp"), split_axis=0, concat_axis=0, tiled=True)
     gate_up = jnp.einsum(
         "dcf,sfh->sdch", arrived, expert_in_both, preferred_element_type=jnp.float32
     )

time: 352 us -> 361 us (1.026)
  blocking collectives: 64.3 us -> 0 us
  waiting for transfers between devices: 177 us -> 232 us
  starting transfers between devices: 24.2 us -> 39.4 us
    all_to_all x1 -> x0, blocking collectives: 64.3 us -> none  [shards(): lax.all_to_all(outgoing, ('ctx', 'exp'), split_axis=0, concat_axis=0, til...]
    ppermute x1, waiting for transfers between devices: 0.01 us -> 54.4 us  [shards(): lax.ppermute(expert_in[:, rows_half:], 'exp', pair)]
    all_to_all x0 -> x1, starting transfers between devices: none -> 9.56 us  [shards(): lax.all_to_all(outgoing, ('ctx', 'exp'), split_axis=0, concat_axis=0, til...]
    all_to_all x1, starting transfers between devices: 6.88 us -> 12.5 us  [shards(): lax.all_to_all(produced, ('ctx', 'exp'), split_axis=0, concat_axis=0, til...]
    ppermute x1, waiting for transfers between devices: 4.09 us -> 0.01 us  [shards(): lax.ppermute(expert_in[:, :rows_half], 'exp', pair)]
  transfers between devices with their start and end apart: 8 -> 9, of which waited for: 7 -> 7; matrix products, arithmetic and copies ran while one was open for 9% -> 9% of each run, Pallas kernels for 4% -> 4%
where the time goes in v9:
time: 361 us; the launch traced here: 360 us
  waiting for transfers between devices  232 us (64%)
  starting transfers between devices  39.4 us (11%)
  local copies, waits for them, and re-layouts  24.6 us (7%)
  matrix products  21 us (6%)
  between operations  15.6 us (4%)
  other arithmetic  13.8 us (4%)
  Pallas kernels  13.8 us (4%)
    ppermute x1, waiting for transfers between devices, shards(): lax.ppermute(expert_in[:, rows_half:], 'exp', pair)  54.4 us
    all_to_all x1, waiting for transfers between devices, shards(): lax.all_to_all(produced, ('ctx', 'exp'), split_axis=0, concat_axis=0, til...  50.2 us
    all_gather x1, waiting for transfers between devices, shards(): every_kv = lax.all_gather(key_values, 'ctx', axis=1, tiled=True)  48.1 us
    ppermute x1, waiting for transfers between devices, shards(): lax.ppermute(expert_out, 'exp', pair)  43.7 us
    all_gather x1, waiting for transfers between devices, shards(): lax.all_gather(jnp.concatenate([q_weight, kv_local, o_weight.T], axis=1),...  17.3 us
    all_to_all x1, waiting for transfers between devices, shards(): lax.all_to_all(attn_part.astype(jnp.bfloat16).reshape(expert_count, tok_d...  14.8 us
    pallas_call x1, Pallas kernels, attention_context(): pl.pallas_call(body, grid=(steps,), in_specs=[pl.BlockSpec((rows, width),...  13.8 us
    all_to_all x1, starting transfers between devices, shards(): lax.all_to_all(produced, ('ctx', 'exp'), split_axis=0, concat_axis=0, til...  12.5 us
  transfers between devices with their start and end apart: 9, of which 7 were waited for; matrix products, arithmetic and copies ran while one was open for 9% of the time, Pallas kernels for 4%

profile of v9, /device:TPU:1, one launch (start us, length us, event | category | flops | bytes accessed | tf_op | source)
XLA Modules:
  0.0 360.1 jit_solution(13989980000738911599)
XLA Ops:
  8.0 1.6 pad_maximum_fusion
  9.6 3.6 %collective-permute-start = (bf16[1,384,2048]{2,1,0:T(8,128)(2,1)}, bf16[1,384,2048]{2,1,0:T(8,128)(2,1)S(1)}, u32[]{:S(2)}, u32[]{:S(2)}) collective-permute-start(bf16[1,384,2048]{2,1,0:T(8,128)(2,1)} %param.25), channel_id=1, source_target_pairs={{0,1},{1,0},{2,3},{3,2},{4,5},{5,4},{6,7},{7,6},{8,9},{9,8},{10,11... | collective-permute-start | bytes 4718600 | tf_op jit(solution)/shard_map/ppermute | solution.py:184
  15.3 1.1 broadcast_in_dim.8
  16.4 4.2 %all-to-all-start = ((bf16[8,32,2048]{2,1,0:T(8,128)(2,1)}), bf16[8,32,2048]{2,1,0:T(8,128)(2,1)S(1)}, u32[]{:S(2)}, u32[]{:S(2)}) async-start(bf16[8,32,2048]{2,1,0:T(8,128)(2,1)} %broadcast_in_dim.8), calls=%async_computation | async-start | bytes 2097152 | tf_op jit(solution)/shard_map/all_to_all | solution.py:159
  23.1 43.7 %collective-permute-done = bf16[1,384,2048]{2,1,0:T(8,128)(2,1)S(1)} collective-permute-done((bf16[1,384,2048]{2,1,0:T(8,128)(2,1)}, bf16[1,384,2048]{2,1,0:T(8,128)(2,1)S(1)}, u32[]{:S(2)}, u32[]{:S(2)}) %collective-permute-start) | collective-permute-done | bytes 1572896 | tf_op jit(solution)/shard_map/ppermute | solution.py:184
  66.8 17.3 %all-gather.3.cloned.1.call-done = bf16[2048,1280]{1,0:T(8,128)(2,1)} async-done(((bf16[64,1280]{1,0:T(8,128)(2,1)}), bf16[2048,1280]{1,0:T(8,128)(2,1)}) %all-gather.3.cloned.1.call-update) | async-done | bytes 5242896 | tf_op jit(solution)/shard_map/all_gather | solution.py:181
  84.1 3.4 all-to-all-done
  87.5 2.9 fusion.7
  92.1 3.2 copy.84
  95.3 2.0 fusion.68
  101.4 1.3 fusion.55
  102.7 1.9 slice.76
  104.6 2.0 reshape.475
  106.6 1.4 multiply_reduce_fusion
  108.0 1.4 multiply_multiply_fusion
  111.1 48.1 %all-gather.5.cloned.1.call-done.k_ref.v_ref = bf16[2,8192,128]{2,1,0:T(8,128)(2,1)} async-done(((bf16[2,256,128]{2,1,0:T(8,128)(2,1)}), bf16[2,8192,128]{2,1,0:T(8,128)(2,1)}) %all-gather.5.cloned.1.call-update) | async-done | bytes 4194320 | tf_op jit(solution)/shard_map/all_gather | solution.py:211
  159.1 13.8 %shard_map.140 = bf16[256,512]{1,0:T(8,128)(2,1)} custom-call(bf16[1024,128]{1,0:T(8,128)(2,1)} %bitcast.71, bf16[2,8192,128]{2,1,0:T(8,128)(2,1)} %all-gather.5.cloned.1.call-done.k_ref.v_ref, bf16[2,8192,128]{2,1,0:T(8,128)(2,1)} %all-gather.5.cloned.1.call-done.k_ref.v_ref, s32[1024,1]{1,0:T(8,128)} %bitcast.70, s32[1024,1]{1,0:T(8,128)} %bitcast.69, ...), custom_call_target="tpu_custom_call" | custom-call | tf_op jit(solution)/shard_map/pallas_call | solution.py:105
  172.9 3.4 convolution_convert_fusion.1
  176.3 6.2 %all-to-all-start.1 = ((bf16[8,32,2048]{2,1,0:T(8,128)(2,1)}), bf16[8,32,2048]{2,1,0:T(8,128)(2,1)}, u32[]{:S(2)}, u32[]{:S(2)}) async-start(bf16[8,32,2048]{2,1,0:T(8,128)(2,1)} %bitcast.73), calls=%async_computation.1 | async-start | bytes 2097152 | tf_op jit(solution)/shard_map/all_to_all | solution.py:242
  184.5 14.8 %all-to-all-done.1 = bf16[8,32,2048]{2,1,0:T(8,128)(2,1)} async-done(((bf16[8,32,2048]{2,1,0:T(8,128)(2,1)}), bf16[8,32,2048]{2,1,0:T(8,128)(2,1)}, u32[]{:S(2)}, u32[]{:S(2)}) %all-to-all-start.1) | async-done | bytes 1048608 | tf_op jit(solution)/shard_map/all_to_all | solution.py:242
  199.4 1.4 convert_reduce_fusion.1
  200.9 1.7 convolution_convert_fusion
  202.6 3.5 copy.93
  206.1 9.6 %all-to-all-start.2 = ((bf16[256,2,2048]{2,1,0:T(2,128)(2,1)}), bf16[256,2,2048]{2,1,0:T(2,128)(2,1)}, u32[]{:S(2)}, u32[]{:S(2)}) async-start(bf16[256,2,2048]{2,1,0:T(2,128)(2,1)} %copy.93), calls=%async_computation.2 | async-start | bytes 4194304 | tf_op jit(solution)/shard_map/all_to_all | solution.py:287
  215.7 2.9 collective-permute-start.2
  218.6 54.4 %collective-permute-done.2 = bf16[1,1024,768]{1,2,0:T(8,128)(2,1)} collective-permute-done((bf16[1,1024,768]{1,2,0:T(8,128)(2,1)}, bf16[1,1024,768]{1,2,0:T(8,128)(2,1)}, u32[]{:S(2)}, u32[]{:S(2)}) %collective-permute-start.2) | collective-permute-done | bytes 1572896 | tf_op jit(solution)/shard_map/ppermute | solution.py:288
  273.0 6.2 %fusion.15 = f32[2,256,2,768]{1,3,2,0:T(8,128)S(1)} fusion(bf16[256,2,2048]{2,1,0:T(2,128)(2,1)} %all-to-all-done.2, bf16[1,1024,768]{1,2,0:T(8,128)(2,1)} %collective-permute-done.2, bf16[1,1024,768]{1,2,0:T(8,128)(2,1)} %collective-permute-done.1, bf16[1,2048,768]{1,2,0:T(8,128)(2,1)S(1)} %copy.84), kind=kOutput, calls=%fused_computation.22 | convolution fusion | flops 3240099840 | bytes 11534336 | tf_op jit(solution)/shard_map/dcf,sfh->sdch/dot_general | solution.py:294
  279.2 2.4 convert_reduce_fusion
  281.6 3.5 copy.98
  285.1 12.5 %all-to-all-start.3 = ((bf16[256,2,2048]{2,1,0:T(2,128)(2,1)}), bf16[256,2,2048]{2,1,0:T(2,128)(2,1)S(1)}, u32[]{:S(2)}, u32[]{:S(2)}) async-start(bf16[256,2,2048]{2,1,0:T(2,128)(2,1)} %copy.98), calls=%async_computation.3 | async-start | bytes 4194304 | tf_op jit(solution)/shard_map/all_to_all | solution.py:302
  300.4 50.2 %all-to-all-done.3 = bf16[256,2,2048]{2,1,0:T(2,128)(2,1)S(1)} async-done(((bf16[256,2,2048]{2,1,0:T(2,128)(2,1)}), bf16[256,2,2048]{2,1,0:T(2,128)(2,1)S(1)}, u32[]{:S(2)}, u32[]{:S(2)}) %all-to-all-start.3) | async-done | bytes 2097184 | tf_op jit(solution)/shard_map/all_to_all | solution.py:302
  350.5 2.8 fusion.10
  (83 shorter events, 16.3 us)
Async XLA Ops:
  7.2 76.9 %all-gather.3.cloned.1.call-start = ((), (), s32[]{:S(2)}) async-start(), calls=%async_computation.4 | async-start | bytes 5406720 | tf_op jit(solution)/shard_map/all_gather | solution.py:181
  8.0 12.7 %copy-start.5 = (s32[2]{0:T(128)S(1)}, s32[2]{0:T(128)}, u32[]{:S(2)}) copy-start(s32[2]{0:T(128)} %param.14) | copy-start | bytes 28
  9.6 57.2 %collective-permute-start = (bf16[1,384,2048]{2,1,0:T(8,128)(2,1)}, bf16[1,384,2048]{2,1,0:T(8,128)(2,1)S(1)}, u32[]{:S(2)}, u32[]{:S(2)}) collective-permute-start(bf16[1,384,2048]{2,1,0:T(8,128)(2,1)} %param.25), channel_id=1, source_target_pairs={{0,1},{1,0},{2,3},{3,2},{4,5},{5,4},{6,7},{7,6},{8,9},{9,8},{10,11... | collective-permute-start | bytes 4718600 | tf_op jit(solution)/shard_map/ppermute | solution.py:184
  16.4 71.1 %all-to-all-start = ((bf16[8,32,2048]{2,1,0:T(8,128)(2,1)}), bf16[8,32,2048]{2,1,0:T(8,128)(2,1)S(1)}, u32[]{:S(2)}, u32[]{:S(2)}) async-start(bf16[8,32,2048]{2,1,0:T(8,128)(2,1)} %broadcast_in_dim.8), calls=%async_computation | async-start | bytes 2097152 | tf_op jit(solution)/shard_map/all_to_all | solution.py:159
  20.6 138.5 %all-gather.5.cloned.1.call-start = ((), (), s32[]{:S(2)}) async-start(), calls=%async_computation.5 | async-start | bytes 4325376 | tf_op jit(solution)/shard_map/all_gather | solution.py:211
  66.8 23.6 %copy-start.12 = (bf16[1,384,2048]{2,1,0:T(8,128)(2,1)}, bf16[1,384,2048]{2,1,0:T(8,128)(2,1)S(1)}, u32[]{:S(2)}) copy-start(bf16[1,384,2048]{2,1,0:T(8,128)(2,1)S(1)} %collective-permute-done) | copy-start | bytes 4718596
  87.5 3.1 copy-start.9
  90.4 0.9 copy-start.1
  95.3 2.3 copy-start.3
  97.3 87.3 %collective-permute-start.1 = (bf16[1,1024,768]{1,2,0:T(8,128)(2,1)}, bf16[1,1024,768]{1,2,0:T(8,128)(2,1)}, u32[]{:S(2)}, u32[]{:S(2)}) collective-permute-start(bf16[1,1024,768]{1,2,0:T(8,128)(2,1)} %get-tuple-element.27), channel_id=1, source_target_pairs={{0,1},{1,0},{2,3},{3,2},{4,5},{5,4},{6,7},{7,6},{8,9},{9,8},{10,11... | collective-permute-start | bytes 4718600 | tf_op jit(solution)/shard_map/ppermute | solution.py:250
  99.6 8.4 %copy-start.10 = (f32[128]{0:T(128)S(1)}, f32[128]{0:T(128)}, u32[]{:S(2)}) copy-start(f32[128]{0:T(128)} %param.20) | copy-start | bytes 1540
  176.3 24.5 %copy-start = (bf16[32,2048]{1,0:T(8,128)(2,1)S(1)}, bf16[32,2048]{1,0:T(8,128)(2,1)}, u32[]{:S(2)}) copy-start(bf16[32,2048]{1,0:T(8,128)(2,1)} %param.13) | copy-start | bytes 393220
  176.3 24.6 %copy-start.2 = (f32[2048]{0:T(1024)S(1)}, f32[2048]{0:T(1024)}, u32[]{:S(2)}) copy-start(f32[2048]{0:T(1024)} %param.23) | copy-start | bytes 24580
  176.3 23.0 %all-to-all-start.1 = ((bf16[8,32,2048]{2,1,0:T(8,128)(2,1)}), bf16[8,32,2048]{2,1,0:T(8,128)(2,1)}, u32[]{:S(2)}, u32[]{:S(2)}) async-start(bf16[8,32,2048]{2,1,0:T(8,128)(2,1)} %bitcast.73), calls=%async_computation.1 | async-start | bytes 2097152 | tf_op jit(solution)/shard_map/all_to_all | solution.py:242
  182.8 1.7 copy-start.6
  206.1 66.9 %all-to-all-start.2 = ((bf16[256,2,2048]{2,1,0:T(2,128)(2,1)}), bf16[256,2,2048]{2,1,0:T(2,128)(2,1)}, u32[]{:S(2)}, u32[]{:S(2)}) async-start(bf16[256,2,2048]{2,1,0:T(2,128)(2,1)} %copy.93), calls=%async_computation.2 | async-start | bytes 4194304 | tf_op jit(solution)/shard_map/all_to_all | solution.py:287
  215.7 57.3 %collective-permute-start.2 = (bf16[1,1024,768]{1,2,0:T(8,128)(2,1)}, bf16[1,1024,768]{1,2,0:T(8,128)(2,1)}, u32[]{:S(2)}, u32[]{:S(2)}) collective-permute-start(bf16[1,1024,768]{1,2,0:T(8,128)(2,1)} %get-tuple-element.26), channel_id=1, source_target_pairs={{0,1},{1,0},{2,3},{3,2},{4,5},{5,4},{6,7},{7,6},{8,9},{9,8},{10,11... | collective-permute-start | bytes 4718600 | tf_op jit(solution)/shard_map/ppermute | solution.py:288
  273.0 6.2 %copy-start.11 = (bf16[1,384,2048]{2,1,0:T(8,128)(2,1)S(1)}, bf16[1,384,2048]{2,1,0:T(8,128)(2,1)}, u32[]{:S(2)}) copy-start(bf16[1,384,2048]{2,1,0:T(8,128)(2,1)} %param.25) | copy-start | bytes 4718596
  273.0 6.2 %copy-start.13 = (bf16[1,384,2048]{2,1,0:T(8,128)(2,1)S(1)}, bf16[1,384,2048]{2,1,0:T(8,128)(2,1)}, u32[]{:S(2)}) copy-start(bf16[1,384,2048]{2,1,0:T(8,128)(2,1)} %copy-done.12) | copy-start | bytes 4718596
  285.1 12.5 %copy-start.4 = (f32[32,8]{0,1:T(8,128)S(1)}, f32[32,8]{0,1:T(8,128)}, u32[]{:S(2)}) copy-start(f32[32,8]{0,1:T(8,128)} %param.16) | copy-start | bytes 3076
  285.1 12.7 %copy-start.7 = (s32[256]{0:T(256)S(1)}, s32[256]{0:T(256)}, u32[]{:S(2)}) copy-start(s32[256]{0:T(256)} %copy-done.6) | copy-start | bytes 3076
  285.1 12.7 %copy-start.8 = (s32[256]{0:T(256)S(1)}, s32[256]{0:T(256)}, u32[]{:S(2)}) copy-start(s32[256]{0:T(256)} %get-tuple-element.38) | copy-start | bytes 3076
  285.1 65.4 %all-to-all-start.3 = ((bf16[256,2,2048]{2,1,0:T(2,128)(2,1)}), bf16[256,2,2048]{2,1,0:T(2,128)(2,1)S(1)}, u32[]{:S(2)}, u32[]{:S(2)}) async-start(bf16[256,2,2048]{2,1,0:T(2,128)(2,1)} %copy.98), calls=%async_computation.3 | async-start | bytes 4194304 | tf_op jit(solution)/shard_map/all_to_all | solution.py:302
Sparse Core Ops, SparseCore 0:
  9.8 74.2 all-gather.2
  92.2 66.8 all-gather.4

commit v10 on v8

--- a/solution.py
+++ b/solution.py
@@ -210,7 +210,7 @@
 
     every_kv = lax.all_gather(key_values, "ctx", axis=1, tiled=True)
     total_rows = every_kv.shape[1]
-    chunk = min(1024, total_rows)
+    chunk = min(2048, total_rows)
     key_pos = mirrored_position(jnp.arange(total_rows, dtype=jnp.int32), count_ctx, tok_ctx)
     key_doc, unused_rope = document_info(key_pos, lengths)
     q_rows = jnp.transpose(queries, (1, 0, 2)).reshape(q_dev * tok_ctx, HEAD_SIZE)

time: 352 us -> 352 us (level)
  no operation moved by 1% of the time
where the time goes in v10:
time: 352 us; the launch traced here: 351 us
  waiting for transfers between devices  176 us (50%)
  blocking collectives  65.6 us (19%)
  starting transfers between devices  24.2 us (7%)
  local copies, waits for them, and re-layouts  23.1 us (7%)
  matrix products  19.7 us (6%)
  between operations  15.7 us (4%)
  other arithmetic  13.9 us (4%)
  Pallas kernels  12.7 us (4%)
    all_to_all x1, blocking collectives, shards(): lax.all_to_all(outgoing, ('ctx', 'exp'), split_axis=0, concat_axis=0, til...  65.6 us
    all_to_all x1, waiting for transfers between devices, shards(): lax.all_to_all(produced, ('ctx', 'exp'), split_axis=0, concat_axis=0, til...  50.2 us
    all_gather x1, waiting for transfers between devices, shards(): every_kv = lax.all_gather(key_values, 'ctx', axis=1, tiled=True)  45.6 us
    ppermute x1, waiting for transfers between devices, shards(): lax.ppermute(expert_out, 'exp', pair)  43.6 us
    all_gather x1, waiting for transfers between devices, shards(): lax.all_gather(jnp.concatenate([q_weight, kv_local, o_weight.T], axis=1),...  17.4 us
    pallas_call x1, Pallas kernels, attention_context(): pl.pallas_call(body, grid=(steps,), in_specs=[pl.BlockSpec((rows, width),...  12.7 us
    all_to_all x1, waiting for transfers between devices, shards(): lax.all_to_all(attn_part.astype(jnp.bfloat16).reshape(expert_count, tok_d...  11.1 us
  transfers between devices with their start and end apart: 8, of which 7 were waited for; matrix products, arithmetic and copies ran while one was open for 9% of the time, Pallas kernels for 4%

profile of v10, /device:TPU:1, one launch (start us, length us, event | category | flops | bytes accessed | tf_op | source)
XLA Modules:
  0.0 351.2 jit_solution(12385697108885717716)
XLA Ops:
  8.0 1.5 pad_maximum_fusion
  9.6 3.6 %collective-permute-start = (bf16[1,384,2048]{2,1,0:T(8,128)(2,1)}, bf16[1,384,2048]{2,1,0:T(8,128)(2,1)S(1)}, u32[]{:S(2)}, u32[]{:S(2)}) collective-permute-start(bf16[1,384,2048]{2,1,0:T(8,128)(2,1)} %param.25), channel_id=1, source_target_pairs={{0,1},{1,0},{2,3},{3,2},{4,5},{5,4},{6,7},{7,6},{8,9},{9,8},{10,11... | collective-permute-start | bytes 4718600 | tf_op jit(solution)/shard_map/ppermute | solution.py:184
  15.3 1.1 broadcast_in_dim.8
  16.4 4.2 %all-to-all-start = ((bf16[8,32,2048]{2,1,0:T(8,128)(2,1)}), bf16[8,32,2048]{2,1,0:T(8,128)(2,1)S(1)}, u32[]{:S(2)}, u32[]{:S(2)}) async-start(bf16[8,32,2048]{2,1,0:T(8,128)(2,1)} %broadcast_in_dim.8), calls=%async_computation | async-start | bytes 2097152 | tf_op jit(solution)/shard_map/all_to_all | solution.py:159
  23.1 43.6 %collective-permute-done = bf16[1,384,2048]{2,1,0:T(8,128)(2,1)S(1)} collective-permute-done((bf16[1,384,2048]{2,1,0:T(8,128)(2,1)}, bf16[1,384,2048]{2,1,0:T(8,128)(2,1)S(1)}, u32[]{:S(2)}, u32[]{:S(2)}) %collective-permute-start) | collective-permute-done | bytes 1572896 | tf_op jit(solution)/shard_map/ppermute | solution.py:184
  66.7 17.4 %all-gather.3.cloned.1.call-done = bf16[2048,1280]{1,0:T(8,128)(2,1)} async-done(((bf16[64,1280]{1,0:T(8,128)(2,1)}), bf16[2048,1280]{1,0:T(8,128)(2,1)}) %all-gather.3.cloned.1.call-update) | async-done | bytes 5242896 | tf_op jit(solution)/shard_map/all_gather | solution.py:181
  84.2 3.3 all-to-all-done
  87.5 2.9 fusion.7
  92.0 3.2 copy.82
  95.2 2.0 fusion.68
  97.5 2.7 collective-permute-start.1
  104.0 1.3 fusion.55
  105.3 1.9 slice.76
  107.2 2.0 reshape.475
  109.2 1.4 multiply_reduce_fusion
  110.6 1.4 multiply_multiply_fusion
  113.6 45.6 %all-gather.5.cloned.1.call-done.k_ref.v_ref = bf16[2,8192,128]{2,1,0:T(8,128)(2,1)} async-done(((bf16[2,256,128]{2,1,0:T(8,128)(2,1)}), bf16[2,8192,128]{2,1,0:T(8,128)(2,1)}) %all-gather.5.cloned.1.call-update) | async-done | bytes 4194320 | tf_op jit(solution)/shard_map/all_gather | solution.py:211
  159.2 12.7 %shard_map.140 = bf16[256,512]{1,0:T(8,128)(2,1)} custom-call(bf16[1024,128]{1,0:T(8,128)(2,1)} %bitcast.71, bf16[2,8192,128]{2,1,0:T(8,128)(2,1)} %all-gather.5.cloned.1.call-done.k_ref.v_ref, bf16[2,8192,128]{2,1,0:T(8,128)(2,1)} %all-gather.5.cloned.1.call-done.k_ref.v_ref, s32[1024,1]{1,0:T(8,128)} %bitcast.70, s32[1024,1]{1,0:T(8,128)} %bitcast.69, ...), custom_call_target="tpu_custom_call" | custom-call | tf_op jit(solution)/shard_map/pallas_call | solution.py:105
  171.9 3.4 convolution_convert_fusion.1
  175.3 6.4 %all-to-all-start.1 = ((bf16[8,32,2048]{2,1,0:T(8,128)(2,1)}), bf16[8,32,2048]{2,1,0:T(8,128)(2,1)}, u32[]{:S(2)}, u32[]{:S(2)}) async-start(bf16[8,32,2048]{2,1,0:T(8,128)(2,1)} %bitcast.73), calls=%async_computation.1 | async-start | bytes 2097152 | tf_op jit(solution)/shard_map/all_to_all | solution.py:242
  183.1 5.1 %collective-permute-done.1 = bf16[1,1024,768]{1,2,0:T(8,128)(2,1)} collective-permute-done((bf16[1,1024,768]{1,2,0:T(8,128)(2,1)}, bf16[1,1024,768]{1,2,0:T(8,128)(2,1)}, u32[]{:S(2)}, u32[]{:S(2)}) %collective-permute-start.1) | collective-permute-done | bytes 1572896 | tf_op jit(solution)/shard_map/ppermute | solution.py:252
  188.2 11.1 %all-to-all-done.1 = bf16[8,32,2048]{2,1,0:T(8,128)(2,1)} async-done(((bf16[8,32,2048]{2,1,0:T(8,128)(2,1)}), bf16[8,32,2048]{2,1,0:T(8,128)(2,1)}, u32[]{:S(2)}, u32[]{:S(2)}) %all-to-all-start.1) | async-done | bytes 1048608 | tf_op jit(solution)/shard_map/all_to_all | solution.py:242
  199.4 1.4 convert_reduce_fusion.1
  200.9 1.7 convolution_convert_fusion
  202.6 2.2 copy.93
  204.8 65.6 %all_to_all.20 = bf16[256,2,2048]{2,1,0:T(2,128)(2,1)S(1)} all-to-all(bf16[256,2,2048]{2,1,0:T(2,128)(2,1)S(1)} %copy.93), channel_id=1, replica_groups=mesh['ctx'=32,'exp'=8] {'ctx','exp'}, dimensions={0} | all-to-all | bytes 4194304 | tf_op jit(solution)/shard_map/all_to_all | solution.py:292
  270.3 5.5 %fusion.15 = f32[2,256,2,768]{1,3,2,0:T(8,128)S(1)} fusion(bf16[256,2,2048]{2,1,0:T(2,128)(2,1)S(1)} %all_to_all.20, bf16[1,1024,768]{1,2,0:T(8,128)(2,1)} %collective-permute-done.2, bf16[1,1024,768]{1,2,0:T(8,128)(2,1)} %collective-permute-done.1, bf16[1,2048,768]{1,2,0:T(8,128)(2,1)S(1)} %copy.82), kind=kOutput, calls=%fused_computation.22 | convolution fusion | flops 3240099840 | bytes 11534336 | tf_op jit(solution)/shard_map/dcf,sfh->sdch/dot_general | solution.py:293
  275.9 2.4 convert_reduce_fusion
  278.3 3.5 copy.96
  281.8 6.9 %all-to-all-start.3 = ((bf16[256,2,2048]{2,1,0:T(2,128)(2,1)}), bf16[256,2,2048]{2,1,0:T(2,128)(2,1)S(1)}, u32[]{:S(2)}, u32[]{:S(2)}) async-start(bf16[256,2,2048]{2,1,0:T(2,128)(2,1)} %copy.96), calls=%async_computation.3 | async-start | bytes 4194304 | tf_op jit(solution)/shard_map/all_to_all | solution.py:301
  291.4 50.2 %all-to-all-done.3 = bf16[256,2,2048]{2,1,0:T(2,128)(2,1)S(1)} async-done(((bf16[256,2,2048]{2,1,0:T(2,128)(2,1)}), bf16[256,2,2048]{2,1,0:T(2,128)(2,1)S(1)}, u32[]{:S(2)}, u32[]{:S(2)}) %all-to-all-start.3) | async-done | bytes 2097184 | tf_op jit(solution)/shard_map/all_to_all | solution.py:301
  341.6 2.8 fusion.10
  (80 shorter events, 15.6 us)
Async XLA Ops:
  7.2 77.0 %all-gather.3.cloned.1.call-start = ((), (), s32[]{:S(2)}) async-start(), calls=%async_computation.4 | async-start | bytes 5406720 | tf_op jit(solution)/shard_map/all_gather | solution.py:181
  8.0 12.6 %copy-start.5 = (s32[2]{0:T(128)S(1)}, s32[2]{0:T(128)}, u32[]{:S(2)}) copy-start(s32[2]{0:T(128)} %param.14) | copy-start | bytes 28
  9.6 57.2 %collective-permute-start = (bf16[1,384,2048]{2,1,0:T(8,128)(2,1)}, bf16[1,384,2048]{2,1,0:T(8,128)(2,1)S(1)}, u32[]{:S(2)}, u32[]{:S(2)}) collective-permute-start(bf16[1,384,2048]{2,1,0:T(8,128)(2,1)} %param.25), channel_id=1, source_target_pairs={{0,1},{1,0},{2,3},{3,2},{4,5},{5,4},{6,7},{7,6},{8,9},{9,8},{10,11... | collective-permute-start | bytes 4718600 | tf_op jit(solution)/shard_map/ppermute | solution.py:184
  16.4 71.1 %all-to-all-start = ((bf16[8,32,2048]{2,1,0:T(8,128)(2,1)}), bf16[8,32,2048]{2,1,0:T(8,128)(2,1)S(1)}, u32[]{:S(2)}, u32[]{:S(2)}) async-start(bf16[8,32,2048]{2,1,0:T(8,128)(2,1)} %broadcast_in_dim.8), calls=%async_computation | async-start | bytes 2097152 | tf_op jit(solution)/shard_map/all_to_all | solution.py:159
  20.6 138.6 %all-gather.5.cloned.1.call-start = ((), (), s32[]{:S(2)}) async-start(), calls=%async_computation.5 | async-start | bytes 4325376 | tf_op jit(solution)/shard_map/all_gather | solution.py:211
  66.7 23.6 %copy-start.11 = (bf16[1,384,2048]{2,1,0:T(8,128)(2,1)}, bf16[1,384,2048]{2,1,0:T(8,128)(2,1)S(1)}, u32[]{:S(2)}) copy-start(bf16[1,384,2048]{2,1,0:T(8,128)(2,1)S(1)} %collective-permute-done) | copy-start | bytes 4718596
  87.5 3.1 copy-start.8
  90.4 0.9 copy-start.1
  95.2 5.0 %copy-start.3 = (s32[32,8]{0,1:T(8,128)S(1)}, s32[32,8]{0,1:T(8,128)}, u32[]{:S(2)}) copy-start(s32[32,8]{0,1:T(8,128)} %param.15) | copy-start | bytes 3076
  97.2 85.9 %collective-permute-start.2 = (bf16[1,1024,768]{1,2,0:T(8,128)(2,1)}, bf16[1,1024,768]{1,2,0:T(8,128)(2,1)}, u32[]{:S(2)}, u32[]{:S(2)}) collective-permute-start(bf16[1,1024,768]{1,2,0:T(8,128)(2,1)} %get-tuple-element.24), channel_id=1, source_target_pairs={{0,1},{1,0},{2,3},{3,2},{4,5},{5,4},{6,7},{7,6},{8,9},{9,8},{10,11... | collective-permute-start | bytes 4718600 | tf_op jit(solution)/shard_map/ppermute | solution.py:253
  97.5 90.7 %collective-permute-start.1 = (bf16[1,1024,768]{1,2,0:T(8,128)(2,1)}, bf16[1,1024,768]{1,2,0:T(8,128)(2,1)}, u32[]{:S(2)}, u32[]{:S(2)}) collective-permute-start(bf16[1,1024,768]{1,2,0:T(8,128)(2,1)} %get-tuple-element.25), channel_id=1, source_target_pairs={{0,1},{1,0},{2,3},{3,2},{4,5},{5,4},{6,7},{7,6},{8,9},{9,8},{10,11... | collective-permute-start | bytes 4718600 | tf_op jit(solution)/shard_map/ppermute | solution.py:252
  102.2 8.4 %copy-start.9 = (f32[128]{0:T(128)S(1)}, f32[128]{0:T(128)}, u32[]{:S(2)}) copy-start(f32[128]{0:T(128)} %param.20) | copy-start | bytes 1540
  175.3 6.7 %copy-start.6 = (s32[256]{0:T(256)S(1)}, s32[256]{0:T(256)}, u32[]{:S(2)}) copy-start(s32[256]{0:T(256)} %get-tuple-element.36) | copy-start | bytes 3076
  175.3 25.4 %copy-start = (bf16[32,2048]{1,0:T(8,128)(2,1)S(1)}, bf16[32,2048]{1,0:T(8,128)(2,1)}, u32[]{:S(2)}) copy-start(bf16[32,2048]{1,0:T(8,128)(2,1)} %param.13) | copy-start | bytes 393220
  175.3 25.6 %copy-start.2 = (f32[2048]{0:T(1024)S(1)}, f32[2048]{0:T(1024)}, u32[]{:S(2)}) copy-start(f32[2048]{0:T(1024)} %param.23) | copy-start | bytes 24580
  175.3 24.0 %all-to-all-start.1 = ((bf16[8,32,2048]{2,1,0:T(8,128)(2,1)}), bf16[8,32,2048]{2,1,0:T(8,128)(2,1)}, u32[]{:S(2)}, u32[]{:S(2)}) async-start(bf16[8,32,2048]{2,1,0:T(8,128)(2,1)} %bitcast.73), calls=%async_computation.1 | async-start | bytes 2097152 | tf_op jit(solution)/shard_map/all_to_all | solution.py:242
  270.3 5.5 %copy-start.10 = (bf16[1,384,2048]{2,1,0:T(8,128)(2,1)S(1)}, bf16[1,384,2048]{2,1,0:T(8,128)(2,1)}, u32[]{:S(2)}) copy-start(bf16[1,384,2048]{2,1,0:T(8,128)(2,1)} %param.25) | copy-start | bytes 4718596
  270.3 5.5 %copy-start.12 = (bf16[1,384,2048]{2,1,0:T(8,128)(2,1)S(1)}, bf16[1,384,2048]{2,1,0:T(8,128)(2,1)}, u32[]{:S(2)}) copy-start(bf16[1,384,2048]{2,1,0:T(8,128)(2,1)} %copy-done.11) | copy-start | bytes 4718596
  281.8 6.9 %copy-start.4 = (f32[32,8]{0,1:T(8,128)S(1)}, f32[32,8]{0,1:T(8,128)}, u32[]{:S(2)}) copy-start(f32[32,8]{0,1:T(8,128)} %param.16) | copy-start | bytes 3076
  281.8 7.1 %copy-start.7 = (s32[256]{0:T(256)S(1)}, s32[256]{0:T(256)}, u32[]{:S(2)}) copy-start(s32[256]{0:T(256)} %get-tuple-element.36) | copy-start | bytes 3076
  281.8 59.8 %all-to-all-start.3 = ((bf16[256,2,2048]{2,1,0:T(2,128)(2,1)}), bf16[256,2,2048]{2,1,0:T(2,128)(2,1)S(1)}, u32[]{:S(2)}, u32[]{:S(2)}) async-start(bf16[256,2,2048]{2,1,0:T(2,128)(2,1)} %copy.96), calls=%async_computation.3 | async-start | bytes 4194304 | tf_op jit(solution)/shard_map/all_to_all | solution.py:301
Sparse Core Ops, SparseCore 0:
  9.8 74.2 all-gather.2
  92.2 67.0 all-gather.4

commit v11 on v8

--- a/solution.py
+++ b/solution.py
@@ -181,16 +181,15 @@
             lax.all_gather(
                 jnp.concatenate([q_weight, kv_local, o_weight.T], axis=1), "ctx", axis=0, tiled=True
             ),
-            lax.ppermute(expert_out, "exp", pair),
+            lax.ppermute(lax.optimization_barrier((expert_out, normed))[0], "exp", pair),
         )
     )
     kv_width = kv_local.shape[1]
-    projected = jnp.dot(
-        normed, weights_all[:, : q_width + kv_width], preferred_element_type=jnp.float32
-    )
+    key_value_plain = jnp.dot(
+        normed, weights_all[:, q_width : q_width + kv_width], preferred_element_type=jnp.float32
+    )
+    q_raw = jnp.dot(normed, weights_all[:, :q_width], preferred_element_type=jnp.float32)
     o_turned = weights_all[:, q_width + kv_width :]
-    q_raw = projected[:, :q_width]
-    key_value_plain = projected[:, q_width:]
     queries = rotate(
         rms_scale(q_raw.reshape(tok_ctx, q_dev, HEAD_SIZE), q_gain), query_rope
     ).astype(jnp.bfloat16)

time: 352 us -> 358 us (1.017)
  blocking collectives: 64.3 us -> 91.7 us
  waiting for transfers between devices: 177 us -> 161 us
  starting transfers between devices: 24.2 us -> 16.3 us
  matrix products: 19.7 us -> 23.4 us
    all_to_all x0 -> x1, blocking collectives: none -> 27.6 us  [shards(): lax.all_to_all(jnp.broadcast_to(normed_own[None], (expert_count,) + norme...]
    all_gather x1, waiting for transfers between devices: 17.4 us -> 0.01 us  [shards(): lax.all_gather(jnp.concatenate([q_weight, kv_local, o_weight.T], axis=1),...]
    ppermute x1, waiting for transfers between devices: 43.6 us -> 51.6 us  [shards(): lax.ppermute(lax.optimization_barrier((expert_out, normed))[0], 'exp', pair)]
    dot_general x0 -> x2, local copies, waits for them, and re-layouts: none -> 7.15 us  [shards(): jnp.dot(normed, weights_all[:, :q_width], preferred_element_type=jnp.floa...]
    all_to_all x1 -> x0, starting transfers between devices: 4.19 us -> none  [shards(): lax.all_to_all(jnp.broadcast_to(normed_own[None], (expert_count,) + norme...]
    ppermute x1, waiting for transfers between devices: 4.09 us -> 0.01 us  [shards(): lax.ppermute(expert_in[:, :rows_half], 'exp', pair)]
    ppermute x1, starting transfers between devices: 3.65 us -> 0.01 us  [shards(): lax.ppermute(lax.optimization_barrier((expert_out, normed))[0], 'exp', pair)]
  transfers between devices with their start and end apart: 8 -> 7, of which waited for: 7 -> 5; matrix products, arithmetic and copies ran while one was open for 9% -> 9% of each run, Pallas kernels for 4% -> 4%
where the time goes in v11:
time: 358 us
  waiting for transfers between devices  161 us (45%)
  blocking collectives  91.7 us (26%)
  local copies, waits for them, and re-layouts  25.6 us (7%)
  matrix products  23.4 us (7%)
  starting transfers between devices  16.3 us (5%)
  between operations  15.7 us (4%)
  Pallas kernels  13.8 us (4%)
  other arithmetic  10.4 us (3%)
    all_to_all x1, blocking collectives, shards(): lax.all_to_all(outgoing, ('ctx', 'exp'), split_axis=0, concat_axis=0, til...  64.1 us
    ppermute x1, waiting for transfers between devices, shards(): lax.ppermute(lax.optimization_barrier((expert_out, normed))[0], 'exp', pair)  51.6 us
    all_to_all x1, waiting for transfers between devices, shards(): lax.all_to_all(produced, ('ctx', 'exp'), split_axis=0, concat_axis=0, til...  50.2 us
    all_gather x1, waiting for transfers between devices, shards(): every_kv = lax.all_gather(key_values, 'ctx', axis=1, tiled=True)  43.2 us
    all_to_all x1, blocking collectives, shards(): lax.all_to_all(jnp.broadcast_to(normed_own[None], (expert_count,) + norme...  27.6 us
    pallas_call x1, Pallas kernels, attention_context(): pl.pallas_call(body, grid=(steps,), in_specs=[pl.BlockSpec((rows, width),...  13.8 us
    all_to_all x1, waiting for transfers between devices, shards(): lax.all_to_all(attn_part.astype(jnp.bfloat16).reshape(expert_count, tok_d...  13.3 us
  transfers between devices with their start and end apart: 7, of which 5 were waited for; matrix products, arithmetic and copies ran while one was open for 9% of the time, Pallas kernels for 4%

profile of v11, /device:TPU:1, one launch (start us, length us, event | category | flops | bytes accessed | tf_op | source)
XLA Modules:
  0.0 357.5 jit_solution(1168482274258869102)
XLA Ops:
  8.0 1.7 pad_maximum_fusion
  9.7 1.0 fusion.25
  10.8 1.0 fusion.27
  11.9 27.6 %all_to_all.20 = bf16[8,32,2048]{2,1,0:T(8,128)(2,1)S(1)} all-to-all(bf16[8,32,2048]{2,1,0:T(8,128)(2,1)S(1)} %broadcast_in_dim.8), channel_id=1, replica_groups=mesh['ctx'=32,'exp'=8] {'exp'}, dimensions={0} | all-to-all | bytes 2097152 | tf_op jit(solution)/shard_map/all_to_all | solution.py:159
  42.2 51.6 %collective-permute-done = bf16[1,384,2048]{2,1,0:T(8,128)(2,1)} collective-permute-done((bf16[1,384,2048]{2,1,0:T(8,128)(2,1)S(1)}, bf16[1,384,2048]{2,1,0:T(8,128)(2,1)}, u32[]{:S(2)}, u32[]{:S(2)}) %collective-permute-start) | collective-permute-done | bytes 1572896 | tf_op jit(solution)/shard_map/ppermute | solution.py:184
  93.9 1.7 fusion.17
  97.2 3.2 copy.71
  100.4 2.0 fusion.68
  102.5 2.9 collective-permute-start.2
  106.3 1.0 copy.95
  107.4 1.0 copy.97
  108.9 1.3 fusion.55
  110.3 3.2 slice_bitcast_fusion
  113.4 4.0 %copy.65 = bf16[512,2048]{1,0:T(8,128)(2,1)} copy(bf16[512,2048]{0,1:T(8,128)(2,1)} %slice_bitcast_fusion) | data formatting | bytes 4194304 | tf_op jit(solution)/shard_map/dot_general | solution.py:191
  117.4 2.7 multiply_reduce_fusion
  121.2 43.2 %all-gather.5.cloned.1.call-done.k_ref.v_ref = bf16[2,8192,128]{2,1,0:T(8,128)(2,1)} async-done(((bf16[2,256,128]{2,1,0:T(8,128)(2,1)}), bf16[2,8192,128]{2,1,0:T(8,128)(2,1)}) %all-gather.5.cloned.1.call-update) | async-done | bytes 4194320 | tf_op jit(solution)/shard_map/all_gather | solution.py:210
  164.4 13.8 %shard_map.140 = bf16[256,512]{1,0:T(8,128)(2,1)} custom-call(bf16[1024,128]{1,0:T(8,128)(2,1)} %bitcast.79, bf16[2,8192,128]{2,1,0:T(8,128)(2,1)} %all-gather.5.cloned.1.call-done.k_ref.v_ref, bf16[2,8192,128]{2,1,0:T(8,128)(2,1)} %all-gather.5.cloned.1.call-done.k_ref.v_ref, s32[1024,1]{1,0:T(8,128)} %bitcast.76, s32[1024,1]{1,0:T(8,128)} %bitcast.77, ...), custom_call_target="tpu_custom_call" | custom-call | tf_op jit(solution)/shard_map/pallas_call | solution.py:105
  178.2 3.4 convolution_convert_fusion.1
  181.6 6.4 %all-to-all-start.1 = ((bf16[8,32,2048]{2,1,0:T(8,128)(2,1)}), bf16[8,32,2048]{2,1,0:T(8,128)(2,1)}, u32[]{:S(2)}, u32[]{:S(2)}) async-start(bf16[8,32,2048]{2,1,0:T(8,128)(2,1)} %bitcast.82), calls=%async_computation.1 | async-start | bytes 2097152 | tf_op jit(solution)/shard_map/all_to_all | solution.py:241
  190.0 2.2 collective-permute-done.2
  192.3 13.3 %all-to-all-done.1 = bf16[8,32,2048]{2,1,0:T(8,128)(2,1)} async-done(((bf16[8,32,2048]{2,1,0:T(8,128)(2,1)}), bf16[8,32,2048]{2,1,0:T(8,128)(2,1)}, u32[]{:S(2)}, u32[]{:S(2)}) %all-to-all-start.1) | async-done | bytes 1048608 | tf_op jit(solution)/shard_map/all_to_all | solution.py:241
  205.6 1.4 convert_reduce_fusion.1
  207.2 1.7 convolution_convert_fusion
  208.8 2.2 copy.82
  211.0 64.1 %all_to_all.21 = bf16[256,2,2048]{2,1,0:T(2,128)(2,1)S(1)} all-to-all(bf16[256,2,2048]{2,1,0:T(2,128)(2,1)S(1)} %copy.82), channel_id=1, replica_groups=mesh['ctx'=32,'exp'=8] {'ctx','exp'}, dimensions={0} | all-to-all | bytes 4194304 | tf_op jit(solution)/shard_map/all_to_all | solution.py:291
  275.1 5.5 %fusion.13 = f32[2,256,2,768]{1,3,2,0:T(8,128)S(1)} fusion(bf16[256,2,2048]{2,1,0:T(2,128)(2,1)S(1)} %all_to_all.21, bf16[1,1024,768]{1,2,0:T(8,128)(2,1)} %collective-permute-done.2, bf16[1,1024,768]{1,2,0:T(8,128)(2,1)} %collective-permute-done.1, bf16[1,2048,768]{1,2,0:T(8,128)(2,1)S(1)} %copy.71), kind=kOutput, calls=%fused_computation.21 | convolution fusion | flops 3240099840 | bytes 11534336 | tf_op jit(solution)/shard_map/dcf,sfh->sdch/dot_general | solution.py:292
  280.6 4.0 %convert_reduce_fusion = bf16[256,2,2048]{2,0,1:T(8,128)(2,1)S(1)} fusion(bf16[1,384,2048]{2,1,0:T(8,128)(2,1)} %collective-permute-done, bf16[1,384,2048]{2,1,0:T(8,128)(2,1)S(1)} %copy-done.10, f32[2,256,2,768]{1,3,2,0:T(8,128)S(1)} %fusion.13), kind=kOutput, calls=%fused_computation.6 | convolution fusion | flops 1617690624 | bytes 8388608 | tf_op jit(solution)/shard_map/sdch,shf->sdcf/dot_general | solution.py:296
  284.6 3.5 copy.85
  288.1 6.9 %all-to-all-start.3 = ((bf16[256,2,2048]{2,1,0:T(2,128)(2,1)}), bf16[256,2,2048]{2,1,0:T(2,128)(2,1)S(1)}, u32[]{:S(2)}, u32[]{:S(2)}) async-start(bf16[256,2,2048]{2,1,0:T(2,128)(2,1)} %copy.85), calls=%async_computation.3 | async-start | bytes 4194304 | tf_op jit(solution)/shard_map/all_to_all | solution.py:300
  296.0 1.0 constant_dynamic-slice_fusion
  297.7 50.2 %all-to-all-done.3 = bf16[256,2,2048]{2,1,0:T(2,128)(2,1)S(1)} async-done(((bf16[256,2,2048]{2,1,0:T(2,128)(2,1)}), bf16[256,2,2048]{2,1,0:T(2,128)(2,1)S(1)}, u32[]{:S(2)}, u32[]{:S(2)}) %all-to-all-start.3) | async-done | bytes 2097184 | tf_op jit(solution)/shard_map/all_to_all | solution.py:300
  347.9 2.8 fusion.8
  (75 shorter events, 10.3 us)
Async XLA Ops:
  7.2 86.7 %all-gather.3.cloned.1.call-start = ((), (), s32[]{:S(2)}) async-start(), calls=%async_computation.4 | async-start | bytes 5406720 | tf_op jit(solution)/shard_map/all_gather | solution.py:181
  8.0 31.6 %copy-start.9 = (bf16[1,384,2048]{2,1,0:T(8,128)(2,1)S(1)}, bf16[1,384,2048]{2,1,0:T(8,128)(2,1)}, u32[]{:S(2)}) copy-start(bf16[1,384,2048]{2,1,0:T(8,128)(2,1)} %param.25) | copy-start | bytes 4718596
  8.0 31.6 %copy-start.5 = (s32[2]{0:T(128)S(1)}, s32[2]{0:T(128)}, u32[]{:S(2)}) copy-start(s32[2]{0:T(128)} %param.14) | copy-start | bytes 28
  9.7 154.7 %all-gather.5.cloned.1.call-start = ((), (), s32[]{:S(2)}) async-start(), calls=%async_computation.5 | async-start | bytes 4325376 | tf_op jit(solution)/shard_map/all_gather | solution.py:210
  11.9 83.8 %copy-start.7 = (f32[128]{0:T(128)S(1)}, f32[128]{0:T(128)}, u32[]{:S(2)}) copy-start(f32[128]{0:T(128)} %param.21) | copy-start | bytes 1540
  39.6 57.6 %copy-start.1 = (bf16[8,32,2048]{2,1,0:T(8,128)(2,1)}, bf16[8,32,2048]{2,1,0:T(8,128)(2,1)S(1)}, u32[]{:S(2)}) copy-start(bf16[8,32,2048]{2,1,0:T(8,128)(2,1)S(1)} %all_to_all.20) | copy-start | bytes 3145732
  39.6 54.3 %collective-permute-start = (bf16[1,384,2048]{2,1,0:T(8,128)(2,1)S(1)}, bf16[1,384,2048]{2,1,0:T(8,128)(2,1)}, u32[]{:S(2)}, u32[]{:S(2)}) collective-permute-start(bf16[1,384,2048]{2,1,0:T(8,128)(2,1)S(1)} %copy-done.9), channel_id=1, source_target_pairs={{0,1},{1,0},{2,3},{3,2},{4,5},{5,4},{6,7},{7,6},{8,9},{9,8},{10,11... | collective-permute-start | bytes 4718600 | tf_op jit(solution)/shard_map/ppermute | solution.py:184
  100.4 5.0 %copy-start.3 = (s32[32,8]{0,1:T(8,128)S(1)}, s32[32,8]{0,1:T(8,128)}, u32[]{:S(2)}) copy-start(s32[32,8]{0,1:T(8,128)} %param.15) | copy-start | bytes 3076
  102.4 87.6 %collective-permute-start.1 = (bf16[1,1024,768]{1,2,0:T(8,128)(2,1)}, bf16[1,1024,768]{1,2,0:T(8,128)(2,1)}, u32[]{:S(2)}, u32[]{:S(2)}) collective-permute-start(bf16[1,1024,768]{1,2,0:T(8,128)(2,1)} %get-tuple-element.25), channel_id=1, source_target_pairs={{0,1},{1,0},{2,3},{3,2},{4,5},{5,4},{6,7},{7,6},{8,9},{9,8},{10,11... | collective-permute-start | bytes 4718600 | tf_op jit(solution)/shard_map/ppermute | solution.py:251
  102.5 89.8 %collective-permute-start.2 = (bf16[1,1024,768]{1,2,0:T(8,128)(2,1)}, bf16[1,1024,768]{1,2,0:T(8,128)(2,1)}, u32[]{:S(2)}, u32[]{:S(2)}) collective-permute-start(bf16[1,1024,768]{1,2,0:T(8,128)(2,1)} %get-tuple-element.24), channel_id=1, source_target_pairs={{0,1},{1,0},{2,3},{3,2},{4,5},{5,4},{6,7},{7,6},{8,9},{9,8},{10,11... | collective-permute-start | bytes 4718600 | tf_op jit(solution)/shard_map/ppermute | solution.py:252
  117.4 2.7 copy-start.8
  181.6 25.4 %copy-start = (bf16[32,2048]{1,0:T(8,128)(2,1)S(1)}, bf16[32,2048]{1,0:T(8,128)(2,1)}, u32[]{:S(2)}) copy-start(bf16[32,2048]{1,0:T(8,128)(2,1)} %param.13) | copy-start | bytes 393220
  181.6 25.6 %copy-start.2 = (f32[2048]{0:T(1024)S(1)}, f32[2048]{0:T(1024)}, u32[]{:S(2)}) copy-start(f32[2048]{0:T(1024)} %param.23) | copy-start | bytes 24580
  181.6 24.0 %all-to-all-start.1 = ((bf16[8,32,2048]{2,1,0:T(8,128)(2,1)}), bf16[8,32,2048]{2,1,0:T(8,128)(2,1)}, u32[]{:S(2)}, u32[]{:S(2)}) async-start(bf16[8,32,2048]{2,1,0:T(8,128)(2,1)} %bitcast.82), calls=%async_computation.1 | async-start | bytes 2097152 | tf_op jit(solution)/shard_map/all_to_all | solution.py:241
  275.1 5.5 %copy-start.10 = (bf16[1,384,2048]{2,1,0:T(8,128)(2,1)S(1)}, bf16[1,384,2048]{2,1,0:T(8,128)(2,1)}, u32[]{:S(2)}) copy-start(bf16[1,384,2048]{2,1,0:T(8,128)(2,1)} %param.25) | copy-start | bytes 4718596
  288.1 6.9 %copy-start.4 = (f32[32,8]{0,1:T(8,128)S(1)}, f32[32,8]{0,1:T(8,128)}, u32[]{:S(2)}) copy-start(f32[32,8]{0,1:T(8,128)} %param.16) | copy-start | bytes 3076
  288.1 7.1 %copy-start.6 = (s32[256]{0:T(256)S(1)}, s32[256]{0:T(256)}, u32[]{:S(2)}) copy-start(s32[256]{0:T(256)} %get-tuple-element.38) | copy-start | bytes 3076
  288.1 59.8 %all-to-all-start.3 = ((bf16[256,2,2048]{2,1,0:T(2,128)(2,1)}), bf16[256,2,2048]{2,1,0:T(2,128)(2,1)S(1)}, u32[]{:S(2)}, u32[]{:S(2)}) async-start(bf16[256,2,2048]{2,1,0:T(2,128)(2,1)} %copy.85), calls=%async_computation.3 | async-start | bytes 4194304 | tf_op jit(solution)/shard_map/all_to_all | solution.py:300
Sparse Core Ops, SparseCore 0:
  9.8 73.7 all-gather.2
  97.3 67.0 all-gather.4

commit v12 on v11

--- a/solution.py
+++ b/solution.py
@@ -181,7 +181,7 @@
             lax.all_gather(
                 jnp.concatenate([q_weight, kv_local, o_weight.T], axis=1), "ctx", axis=0, tiled=True
             ),
-            lax.ppermute(lax.optimization_barrier((expert_out, normed))[0], "exp", pair),
+            lax.ppermute(expert_out, "exp", pair),
         )
     )
     kv_width = kv_local.shape[1]

time: 358 us -> 351 us (0.980)
  blocking collectives: 91.7 us -> 64.3 us
  waiting for transfers between devices: 161 us -> 173 us
  starting transfers between devices: 16.3 us -> 24.3 us
    all_to_all x1 -> x0, blocking collectives: 27.6 us -> none  [shards(): lax.all_to_all(jnp.broadcast_to(normed_own[None], (expert_count,) + norme...]
    all_gather x1, waiting for transfers between devices: 0.01 us -> 17.3 us  [shards(): lax.all_gather(jnp.concatenate([q_weight, kv_local, o_weight.T], axis=1),...]
    ppermute x1, waiting for transfers between devices: 51.6 us -> 43.4 us  [shards(): lax.ppermute(expert_out, 'exp', pair)]
    all_to_all x0 -> x1, starting transfers between devices: none -> 4.32 us  [shards(): lax.all_to_all(jnp.broadcast_to(normed_own[None], (expert_count,) + norme...]
    ppermute x1, starting transfers between devices: 0.01 us -> 3.65 us  [shards(): lax.ppermute(expert_out, 'exp', pair)]
  transfers between devices with their start and end apart: 7 -> 8, of which waited for: 5 -> 7; matrix products, arithmetic and copies ran while one was open for 9% -> 10% of each run, Pallas kernels for 4% -> 4%
where the time goes in v12:
time: 351 us; the launch traced here: 350 us
  waiting for transfers between devices  173 us (49%)
  blocking collectives  64.3 us (18%)
  local copies, waits for them, and re-layouts  26.4 us (8%)
  starting transfers between devices  24.3 us (7%)
  matrix products  22.2 us (6%)
  between operations  15.7 us (4%)
  Pallas kernels  13.8 us (4%)
  other arithmetic  10.4 us (3%)
    all_to_all x1, blocking collectives, shards(): lax.all_to_all(outgoing, ('ctx', 'exp'), split_axis=0, concat_axis=0, til...  64.3 us
    all_to_all x1, waiting for transfers between devices, shards(): lax.all_to_all(produced, ('ctx', 'exp'), split_axis=0, concat_axis=0, til...  50.2 us
    ppermute x1, waiting for transfers between devices, shards(): lax.ppermute(expert_out, 'exp', pair)  43.4 us
    all_gather x1, waiting for transfers between devices, shards(): every_kv = lax.all_gather(key_values, 'ctx', axis=1, tiled=True)  43.1 us
    all_gather x1, waiting for transfers between devices, shards(): lax.all_gather(jnp.concatenate([q_weight, kv_local, o_weight.T], axis=1),...  17.3 us
    pallas_call x1, Pallas kernels, attention_context(): pl.pallas_call(body, grid=(steps,), in_specs=[pl.BlockSpec((rows, width),...  13.8 us
    all_to_all x1, waiting for transfers between devices, shards(): lax.all_to_all(attn_part.astype(jnp.bfloat16).reshape(expert_count, tok_d...  12.4 us
    dot_general x2, local copies, waits for them, and re-layouts, shards(): jnp.dot(normed, weights_all[:, :q_width], preferred_element_type=jnp.floa...  7.12 us
  transfers between devices with their start and end apart: 8, of which 7 were waited for; matrix products, arithmetic and copies ran while one was open for 10% of the time, Pallas kernels for 4%

profile of v12, /device:TPU:1, one launch (start us, length us, event | category | flops | bytes accessed | tf_op | source)
XLA Modules:
  0.0 350.4 jit_solution(8351954313107347895)
XLA Ops:
  8.0 1.5 pad_maximum_fusion
  9.6 3.6 %collective-permute-start = (bf16[1,384,2048]{2,1,0:T(8,128)(2,1)}, bf16[1,384,2048]{2,1,0:T(8,128)(2,1)S(1)}, u32[]{:S(2)}, u32[]{:S(2)}) collective-permute-start(bf16[1,384,2048]{2,1,0:T(8,128)(2,1)} %param.25), channel_id=1, source_target_pairs={{0,1},{1,0},{2,3},{3,2},{4,5},{5,4},{6,7},{7,6},{8,9},{9,8},{10,11... | collective-permute-start | bytes 4718600 | tf_op jit(solution)/shard_map/ppermute | solution.py:184
  15.3 1.1 broadcast_in_dim.8
  16.4 4.3 %all-to-all-start = ((bf16[8,32,2048]{2,1,0:T(8,128)(2,1)}), bf16[8,32,2048]{2,1,0:T(8,128)(2,1)S(1)}, u32[]{:S(2)}, u32[]{:S(2)}) async-start(bf16[8,32,2048]{2,1,0:T(8,128)(2,1)} %broadcast_in_dim.8), calls=%async_computation | async-start | bytes 2097152 | tf_op jit(solution)/shard_map/all_to_all | solution.py:159
  23.4 43.4 %collective-permute-done = bf16[1,384,2048]{2,1,0:T(8,128)(2,1)S(1)} collective-permute-done((bf16[1,384,2048]{2,1,0:T(8,128)(2,1)}, bf16[1,384,2048]{2,1,0:T(8,128)(2,1)S(1)}, u32[]{:S(2)}, u32[]{:S(2)}) %collective-permute-start) | collective-permute-done | bytes 1572896 | tf_op jit(solution)/shard_map/ppermute | solution.py:184
  66.8 17.3 %all-gather.3.cloned.1.call-done = bf16[2048,1280]{1,0:T(8,128)(2,1)} async-done(((bf16[64,1280]{1,0:T(8,128)(2,1)}), bf16[2048,1280]{1,0:T(8,128)(2,1)}) %all-gather.3.cloned.1.call-update) | async-done | bytes 5242896 | tf_op jit(solution)/shard_map/all_gather | solution.py:181
  84.1 3.4 all-to-all-done
  87.5 2.0 fusion.17
  91.2 3.2 copy.71
  94.4 2.0 fusion.68
  96.7 2.7 collective-permute-start.2
  101.4 1.0 copy.97
  102.9 1.4 fusion.55
  104.3 3.2 slice_bitcast_fusion
  107.5 4.0 %copy.65 = bf16[512,2048]{1,0:T(8,128)(2,1)} copy(bf16[512,2048]{0,1:T(8,128)(2,1)} %slice_bitcast_fusion) | data formatting | bytes 4194304 | tf_op jit(solution)/shard_map/dot_general | solution.py:191
  111.4 2.7 multiply_reduce_fusion
  115.2 43.1 %all-gather.5.cloned.1.call-done.k_ref.v_ref = bf16[2,8192,128]{2,1,0:T(8,128)(2,1)} async-done(((bf16[2,256,128]{2,1,0:T(8,128)(2,1)}), bf16[2,8192,128]{2,1,0:T(8,128)(2,1)}) %all-gather.5.cloned.1.call-update) | async-done | bytes 4194320 | tf_op jit(solution)/shard_map/all_gather | solution.py:210
  158.3 13.8 %shard_map.140 = bf16[256,512]{1,0:T(8,128)(2,1)} custom-call(bf16[1024,128]{1,0:T(8,128)(2,1)} %bitcast.79, bf16[2,8192,128]{2,1,0:T(8,128)(2,1)} %all-gather.5.cloned.1.call-done.k_ref.v_ref, bf16[2,8192,128]{2,1,0:T(8,128)(2,1)} %all-gather.5.cloned.1.call-done.k_ref.v_ref, s32[1024,1]{1,0:T(8,128)} %bitcast.76, s32[1024,1]{1,0:T(8,128)} %bitcast.77, ...), custom_call_target="tpu_custom_call" | custom-call | tf_op jit(solution)/shard_map/pallas_call | solution.py:105
  172.1 3.4 convolution_convert_fusion.1
  175.5 6.4 %all-to-all-start.1 = ((bf16[8,32,2048]{2,1,0:T(8,128)(2,1)}), bf16[8,32,2048]{2,1,0:T(8,128)(2,1)}, u32[]{:S(2)}, u32[]{:S(2)}) async-start(bf16[8,32,2048]{2,1,0:T(8,128)(2,1)} %bitcast.82), calls=%async_computation.1 | async-start | bytes 2097152 | tf_op jit(solution)/shard_map/all_to_all | solution.py:241
  183.9 3.5 collective-permute-done.2
  187.4 12.4 %all-to-all-done.1 = bf16[8,32,2048]{2,1,0:T(8,128)(2,1)} async-done(((bf16[8,32,2048]{2,1,0:T(8,128)(2,1)}), bf16[8,32,2048]{2,1,0:T(8,128)(2,1)}, u32[]{:S(2)}, u32[]{:S(2)}) %all-to-all-start.1) | async-done | bytes 1048608 | tf_op jit(solution)/shard_map/all_to_all | solution.py:241
  199.8 1.4 convert_reduce_fusion.1
  201.3 1.7 convolution_convert_fusion
  203.0 2.2 copy.82
  205.2 64.3 %all_to_all.20 = bf16[256,2,2048]{2,1,0:T(2,128)(2,1)S(1)} all-to-all(bf16[256,2,2048]{2,1,0:T(2,128)(2,1)S(1)} %copy.82), channel_id=1, replica_groups=mesh['ctx'=32,'exp'=8] {'ctx','exp'}, dimensions={0} | all-to-all | bytes 4194304 | tf_op jit(solution)/shard_map/all_to_all | solution.py:291
  269.5 5.5 %fusion.13 = f32[2,256,2,768]{1,3,2,0:T(8,128)S(1)} fusion(bf16[256,2,2048]{2,1,0:T(2,128)(2,1)S(1)} %all_to_all.20, bf16[1,1024,768]{1,2,0:T(8,128)(2,1)} %collective-permute-done.2, bf16[1,1024,768]{1,2,0:T(8,128)(2,1)} %collective-permute-done.1, bf16[1,2048,768]{1,2,0:T(8,128)(2,1)S(1)} %copy.71), kind=kOutput, calls=%fused_computation.21 | convolution fusion | flops 3240099840 | bytes 11534336 | tf_op jit(solution)/shard_map/dcf,sfh->sdch/dot_general | solution.py:292
  275.0 2.4 convert_reduce_fusion
  277.5 3.5 copy.85
  281.0 6.9 %all-to-all-start.3 = ((bf16[256,2,2048]{2,1,0:T(2,128)(2,1)}), bf16[256,2,2048]{2,1,0:T(2,128)(2,1)S(1)}, u32[]{:S(2)}, u32[]{:S(2)}) async-start(bf16[256,2,2048]{2,1,0:T(2,128)(2,1)} %copy.85), calls=%async_computation.3 | async-start | bytes 4194304 | tf_op jit(solution)/shard_map/all_to_all | solution.py:300
  290.6 50.2 %all-to-all-done.3 = bf16[256,2,2048]{2,1,0:T(2,128)(2,1)S(1)} async-done(((bf16[256,2,2048]{2,1,0:T(2,128)(2,1)}), bf16[256,2,2048]{2,1,0:T(2,128)(2,1)S(1)}, u32[]{:S(2)}, u32[]{:S(2)}) %all-to-all-start.3) | async-done | bytes 2097184 | tf_op jit(solution)/shard_map/all_to_all | solution.py:300
  340.7 2.8 fusion.8
  (78 shorter events, 14.4 us)
Async XLA Ops:
  7.2 76.9 %all-gather.3.cloned.1.call-start = ((), (), s32[]{:S(2)}) async-start(), calls=%async_computation.4 | async-start | bytes 5406720 | tf_op jit(solution)/shard_map/all_gather | solution.py:181
  8.0 12.8 %copy-start.5 = (s32[2]{0:T(128)S(1)}, s32[2]{0:T(128)}, u32[]{:S(2)}) copy-start(s32[2]{0:T(128)} %param.14) | copy-start | bytes 28
  9.6 57.2 %collective-permute-start = (bf16[1,384,2048]{2,1,0:T(8,128)(2,1)}, bf16[1,384,2048]{2,1,0:T(8,128)(2,1)S(1)}, u32[]{:S(2)}, u32[]{:S(2)}) collective-permute-start(bf16[1,384,2048]{2,1,0:T(8,128)(2,1)} %param.25), channel_id=1, source_target_pairs={{0,1},{1,0},{2,3},{3,2},{4,5},{5,4},{6,7},{7,6},{8,9},{9,8},{10,11... | collective-permute-start | bytes 4718600 | tf_op jit(solution)/shard_map/ppermute | solution.py:184
  16.4 73.3 %copy-start.7 = (f32[128]{0:T(128)S(1)}, f32[128]{0:T(128)}, u32[]{:S(2)}) copy-start(f32[128]{0:T(128)} %param.21) | copy-start | bytes 1540
  16.4 71.1 %all-to-all-start = ((bf16[8,32,2048]{2,1,0:T(8,128)(2,1)}), bf16[8,32,2048]{2,1,0:T(8,128)(2,1)S(1)}, u32[]{:S(2)}, u32[]{:S(2)}) async-start(bf16[8,32,2048]{2,1,0:T(8,128)(2,1)} %broadcast_in_dim.8), calls=%async_computation | async-start | bytes 2097152 | tf_op jit(solution)/shard_map/all_to_all | solution.py:159
  20.7 137.6 %all-gather.5.cloned.1.call-start = ((), (), s32[]{:S(2)}) async-start(), calls=%async_computation.5 | async-start | bytes 4325376 | tf_op jit(solution)/shard_map/all_gather | solution.py:210
  66.8 24.4 %copy-start.10 = (bf16[1,384,2048]{2,1,0:T(8,128)(2,1)}, bf16[1,384,2048]{2,1,0:T(8,128)(2,1)S(1)}, u32[]{:S(2)}) copy-start(bf16[1,384,2048]{2,1,0:T(8,128)(2,1)S(1)} %collective-permute-done) | copy-start | bytes 4718596
  87.5 3.6 %copy-start.1 = (bf16[8,32,2048]{2,1,0:T(8,128)(2,1)}, bf16[8,32,2048]{2,1,0:T(8,128)(2,1)S(1)}, u32[]{:S(2)}) copy-start(bf16[8,32,2048]{2,1,0:T(8,128)(2,1)S(1)} %all-to-all-done) | copy-start | bytes 3145732
  94.3 5.0 %copy-start.3 = (s32[32,8]{0,1:T(8,128)S(1)}, s32[32,8]{0,1:T(8,128)}, u32[]{:S(2)}) copy-start(s32[32,8]{0,1:T(8,128)} %param.15) | copy-start | bytes 3076
  96.4 87.5 %collective-permute-start.1 = (bf16[1,1024,768]{1,2,0:T(8,128)(2,1)}, bf16[1,1024,768]{1,2,0:T(8,128)(2,1)}, u32[]{:S(2)}, u32[]{:S(2)}) collective-permute-start(bf16[1,1024,768]{1,2,0:T(8,128)(2,1)} %get-tuple-element.23), channel_id=1, source_target_pairs={{0,1},{1,0},{2,3},{3,2},{4,5},{5,4},{6,7},{7,6},{8,9},{9,8},{10,11... | collective-permute-start | bytes 4718600 | tf_op jit(solution)/shard_map/ppermute | solution.py:251
  96.7 90.7 %collective-permute-start.2 = (bf16[1,1024,768]{1,2,0:T(8,128)(2,1)}, bf16[1,1024,768]{1,2,0:T(8,128)(2,1)}, u32[]{:S(2)}, u32[]{:S(2)}) collective-permute-start(bf16[1,1024,768]{1,2,0:T(8,128)(2,1)} %get-tuple-element.22), channel_id=1, source_target_pairs={{0,1},{1,0},{2,3},{3,2},{4,5},{5,4},{6,7},{7,6},{8,9},{9,8},{10,11... | collective-permute-start | bytes 4718600 | tf_op jit(solution)/shard_map/ppermute | solution.py:252
  111.4 2.7 copy-start.8
  175.5 25.7 %copy-start = (bf16[32,2048]{1,0:T(8,128)(2,1)S(1)}, bf16[32,2048]{1,0:T(8,128)(2,1)}, u32[]{:S(2)}) copy-start(bf16[32,2048]{1,0:T(8,128)(2,1)} %param.13) | copy-start | bytes 393220
  175.5 25.9 %copy-start.2 = (f32[2048]{0:T(1024)S(1)}, f32[2048]{0:T(1024)}, u32[]{:S(2)}) copy-start(f32[2048]{0:T(1024)} %param.23) | copy-start | bytes 24580
  175.5 24.3 %all-to-all-start.1 = ((bf16[8,32,2048]{2,1,0:T(8,128)(2,1)}), bf16[8,32,2048]{2,1,0:T(8,128)(2,1)}, u32[]{:S(2)}, u32[]{:S(2)}) async-start(bf16[8,32,2048]{2,1,0:T(8,128)(2,1)} %bitcast.82), calls=%async_computation.1 | async-start | bytes 2097152 | tf_op jit(solution)/shard_map/all_to_all | solution.py:241
  269.5 5.5 %copy-start.9 = (bf16[1,384,2048]{2,1,0:T(8,128)(2,1)S(1)}, bf16[1,384,2048]{2,1,0:T(8,128)(2,1)}, u32[]{:S(2)}) copy-start(bf16[1,384,2048]{2,1,0:T(8,128)(2,1)} %param.25) | copy-start | bytes 4718596
  269.5 5.5 %copy-start.11 = (bf16[1,384,2048]{2,1,0:T(8,128)(2,1)S(1)}, bf16[1,384,2048]{2,1,0:T(8,128)(2,1)}, u32[]{:S(2)}) copy-start(bf16[1,384,2048]{2,1,0:T(8,128)(2,1)} %copy-done.10) | copy-start | bytes 4718596
  280.9 6.9 %copy-start.4 = (f32[32,8]{0,1:T(8,128)S(1)}, f32[32,8]{0,1:T(8,128)}, u32[]{:S(2)}) copy-start(f32[32,8]{0,1:T(8,128)} %param.16) | copy-start | bytes 3076
  281.0 7.1 %copy-start.6 = (s32[256]{0:T(256)S(1)}, s32[256]{0:T(256)}, u32[]{:S(2)}) copy-start(s32[256]{0:T(256)} %get-tuple-element.36) | copy-start | bytes 3076
  281.0 59.8 %all-to-all-start.3 = ((bf16[256,2,2048]{2,1,0:T(2,128)(2,1)}), bf16[256,2,2048]{2,1,0:T(2,128)(2,1)S(1)}, u32[]{:S(2)}, u32[]{:S(2)}) async-start(bf16[256,2,2048]{2,1,0:T(2,128)(2,1)} %copy.85), calls=%async_computation.3 | async-start | bytes 4194304 | tf_op jit(solution)/shard_map/all_to_all | solution.py:300
Sparse Core Ops, SparseCore 0:
  9.8 74.2 all-gather.2
  91.3 67.0 all-gather.4

commit v13 on v8

--- a/solution.py
+++ b/solution.py
@@ -85,7 +85,8 @@
             )
             * scale
         )
-        allowed = (qd_ref[...] == kd_ref[...]) & (kp_ref[...] <= qp_ref[...])
+        start = qd_ref[...]
+        allowed = (kp_ref[...] - start).astype(jnp.uint32) <= (qp_ref[...] - start).astype(jnp.uint32)
         weights = jnp.where(allowed, jnp.exp(scores), 0.0).astype(jnp.bfloat16)
         values = v_ref[...]
         values_one = jnp.concatenate([values, jnp.ones_like(values)], axis=1)
@@ -218,7 +219,7 @@
         q_rows,
         every_kv,
         jnp.tile(query_pos, q_dev)[:, None],
-        jnp.tile(query_doc, q_dev)[:, None],
+        jnp.tile(query_pos - query_rope, q_dev)[:, None],
         key_pos[None, :],
         key_doc[None, :],
         score_scale,

time: 352 us -> 352 us (level)
  no operation moved by 1% of the time
where the time goes in v13:
time: 352 us; the launch traced here: 351 us
  waiting for transfers between devices  176 us (50%)
  blocking collectives  64.2 us (18%)
  starting transfers between devices  24.2 us (7%)
  local copies, waits for them, and re-layouts  23.1 us (7%)
  matrix products  19.7 us (6%)
  between operations  15.7 us (4%)
  other arithmetic  14.5 us (4%)
  Pallas kernels  13.7 us (4%)
    all_to_all x1, blocking collectives, shards(): lax.all_to_all(outgoing, ('ctx', 'exp'), split_axis=0, concat_axis=0, til...  64.2 us
    all_to_all x1, waiting for transfers between devices, shards(): lax.all_to_all(produced, ('ctx', 'exp'), split_axis=0, concat_axis=0, til...  50.2 us
    all_gather x1, waiting for transfers between devices, shards(): every_kv = lax.all_gather(key_values, 'ctx', axis=1, tiled=True)  44.9 us
    ppermute x1, waiting for transfers between devices, shards(): lax.ppermute(expert_out, 'exp', pair)  43.6 us
    all_gather x1, waiting for transfers between devices, shards(): lax.all_gather(jnp.concatenate([q_weight, kv_local, o_weight.T], axis=1),...  17.4 us
    pallas_call x1, Pallas kernels, attention_context(): pl.pallas_call(body, grid=(steps,), in_specs=[pl.BlockSpec((rows, width),...  13.7 us
    all_to_all x1, waiting for transfers between devices, shards(): lax.all_to_all(attn_part.astype(jnp.bfloat16).reshape(expert_count, tok_d...  12.5 us
  transfers between devices with their start and end apart: 8, of which 7 were waited for; matrix products, arithmetic and copies ran while one was open for 9% of the time, Pallas kernels for 4%

profile of v13, /device:TPU:1, one launch (start us, length us, event | category | flops | bytes accessed | tf_op | source)
XLA Modules:
  0.0 351.2 jit_solution(13970872958585174015)
XLA Ops:
  8.0 1.5 pad_maximum_fusion
  9.6 3.6 %collective-permute-start = (bf16[1,384,2048]{2,1,0:T(8,128)(2,1)}, bf16[1,384,2048]{2,1,0:T(8,128)(2,1)S(1)}, u32[]{:S(2)}, u32[]{:S(2)}) collective-permute-start(bf16[1,384,2048]{2,1,0:T(8,128)(2,1)} %param.25), channel_id=1, source_target_pairs={{0,1},{1,0},{2,3},{3,2},{4,5},{5,4},{6,7},{7,6},{8,9},{9,8},{10,11... | collective-permute-start | bytes 4718600 | tf_op jit(solution)/shard_map/ppermute | solution.py:185
  16.4 4.2 %all-to-all-start = ((bf16[8,32,2048]{2,1,0:T(8,128)(2,1)}), bf16[8,32,2048]{2,1,0:T(8,128)(2,1)S(1)}, u32[]{:S(2)}, u32[]{:S(2)}) async-start(bf16[8,32,2048]{2,1,0:T(8,128)(2,1)} %broadcast_in_dim.8), calls=%async_computation | async-start | bytes 2097152 | tf_op jit(solution)/shard_map/all_to_all | solution.py:160
  23.1 43.6 %collective-permute-done = bf16[1,384,2048]{2,1,0:T(8,128)(2,1)S(1)} collective-permute-done((bf16[1,384,2048]{2,1,0:T(8,128)(2,1)}, bf16[1,384,2048]{2,1,0:T(8,128)(2,1)S(1)}, u32[]{:S(2)}, u32[]{:S(2)}) %collective-permute-start) | collective-permute-done | bytes 1572896 | tf_op jit(solution)/shard_map/ppermute | solution.py:185
  66.8 17.4 %all-gather.3.cloned.1.call-done = bf16[2048,1280]{1,0:T(8,128)(2,1)} async-done(((bf16[64,1280]{1,0:T(8,128)(2,1)}), bf16[2048,1280]{1,0:T(8,128)(2,1)}) %all-gather.3.cloned.1.call-update) | async-done | bytes 5242896 | tf_op jit(solution)/shard_map/all_gather | solution.py:182
  84.1 3.4 all-to-all-done
  87.5 2.9 fusion.7
  92.0 3.2 copy.82
  95.2 2.0 fusion.66
  97.5 2.7 collective-permute-start.1
  100.5 1.2 and_select_fusion.3
  104.6 1.3 fusion.55
  105.9 1.9 slice.76
  107.8 2.0 reshape.479
  109.8 1.4 multiply_reduce_fusion
  111.3 1.4 multiply_multiply_fusion
  114.3 44.9 %all-gather.5.cloned.1.call-done.k_ref.v_ref = bf16[2,8192,128]{2,1,0:T(8,128)(2,1)} async-done(((bf16[2,256,128]{2,1,0:T(8,128)(2,1)}), bf16[2,8192,128]{2,1,0:T(8,128)(2,1)}) %all-gather.5.cloned.1.call-update) | async-done | bytes 4194320 | tf_op jit(solution)/shard_map/all_gather | solution.py:212
  159.2 13.7 %shard_map.140 = bf16[256,512]{1,0:T(8,128)(2,1)} custom-call(bf16[1024,128]{1,0:T(8,128)(2,1)} %bitcast.71, bf16[2,8192,128]{2,1,0:T(8,128)(2,1)} %all-gather.5.cloned.1.call-done.k_ref.v_ref, bf16[2,8192,128]{2,1,0:T(8,128)(2,1)} %all-gather.5.cloned.1.call-done.k_ref.v_ref, s32[1024,1]{1,0:T(8,128)} %bitcast.69, s32[1024,1]{1,0:T(8,128)} %bitcast.70, ...), custom_call_target="tpu_custom_call" | custom-call | tf_op jit(solution)/shard_map/pallas_call | solution.py:106
  173.0 3.4 convolution_convert_fusion.1
  176.4 6.5 %all-to-all-start.1 = ((bf16[8,32,2048]{2,1,0:T(8,128)(2,1)}), bf16[8,32,2048]{2,1,0:T(8,128)(2,1)}, u32[]{:S(2)}, u32[]{:S(2)}) async-start(bf16[8,32,2048]{2,1,0:T(8,128)(2,1)} %bitcast.73), calls=%async_computation.1 | async-start | bytes 2097152 | tf_op jit(solution)/shard_map/all_to_all | solution.py:243
  184.2 4.0 %collective-permute-done.1 = bf16[1,1024,768]{1,2,0:T(8,128)(2,1)} collective-permute-done((bf16[1,1024,768]{1,2,0:T(8,128)(2,1)}, bf16[1,1024,768]{1,2,0:T(8,128)(2,1)}, u32[]{:S(2)}, u32[]{:S(2)}) %collective-permute-start.1) | collective-permute-done | bytes 1572896 | tf_op jit(solution)/shard_map/ppermute | solution.py:253
  188.3 12.5 %all-to-all-done.1 = bf16[8,32,2048]{2,1,0:T(8,128)(2,1)} async-done(((bf16[8,32,2048]{2,1,0:T(8,128)(2,1)}), bf16[8,32,2048]{2,1,0:T(8,128)(2,1)}, u32[]{:S(2)}, u32[]{:S(2)}) %all-to-all-start.1) | async-done | bytes 1048608 | tf_op jit(solution)/shard_map/all_to_all | solution.py:243
  200.7 1.4 convert_reduce_fusion.1
  202.3 1.7 convolution_convert_fusion
  204.0 2.2 copy.93
  206.1 64.2 %all_to_all.20 = bf16[256,2,2048]{2,1,0:T(2,128)(2,1)S(1)} all-to-all(bf16[256,2,2048]{2,1,0:T(2,128)(2,1)S(1)} %copy.93), channel_id=1, replica_groups=mesh['ctx'=32,'exp'=8] {'ctx','exp'}, dimensions={0} | all-to-all | bytes 4194304 | tf_op jit(solution)/shard_map/all_to_all | solution.py:293
  270.4 5.5 %fusion.15 = f32[2,256,2,768]{1,3,2,0:T(8,128)S(1)} fusion(bf16[256,2,2048]{2,1,0:T(2,128)(2,1)S(1)} %all_to_all.20, bf16[1,1024,768]{1,2,0:T(8,128)(2,1)} %collective-permute-done.2, bf16[1,1024,768]{1,2,0:T(8,128)(2,1)} %collective-permute-done.1, bf16[1,2048,768]{1,2,0:T(8,128)(2,1)S(1)} %copy.82), kind=kOutput, calls=%fused_computation.22 | convolution fusion | flops 3240099840 | bytes 11534336 | tf_op jit(solution)/shard_map/dcf,sfh->sdch/dot_general | solution.py:294
  275.9 2.4 convert_reduce_fusion
  278.3 3.5 copy.96
  281.8 6.9 %all-to-all-start.3 = ((bf16[256,2,2048]{2,1,0:T(2,128)(2,1)}), bf16[256,2,2048]{2,1,0:T(2,128)(2,1)S(1)}, u32[]{:S(2)}, u32[]{:S(2)}) async-start(bf16[256,2,2048]{2,1,0:T(2,128)(2,1)} %copy.96), calls=%async_computation.3 | async-start | bytes 4194304 | tf_op jit(solution)/shard_map/all_to_all | solution.py:302
  291.4 50.2 %all-to-all-done.3 = bf16[256,2,2048]{2,1,0:T(2,128)(2,1)S(1)} async-done(((bf16[256,2,2048]{2,1,0:T(2,128)(2,1)}), bf16[256,2,2048]{2,1,0:T(2,128)(2,1)S(1)}, u32[]{:S(2)}, u32[]{:S(2)}) %all-to-all-start.3) | async-done | bytes 2097184 | tf_op jit(solution)/shard_map/all_to_all | solution.py:302
  341.6 2.8 fusion.10
  (82 shorter events, 16.1 us)
Async XLA Ops:
  7.2 77.0 %all-gather.3.cloned.1.call-start = ((), (), s32[]{:S(2)}) async-start(), calls=%async_computation.4 | async-start | bytes 5406720 | tf_op jit(solution)/shard_map/all_gather | solution.py:182
  8.0 12.6 %copy-start.5 = (s32[2]{0:T(128)S(1)}, s32[2]{0:T(128)}, u32[]{:S(2)}) copy-start(s32[2]{0:T(128)} %param.14) | copy-start | bytes 28
  9.6 57.2 %collective-permute-start = (bf16[1,384,2048]{2,1,0:T(8,128)(2,1)}, bf16[1,384,2048]{2,1,0:T(8,128)(2,1)S(1)}, u32[]{:S(2)}, u32[]{:S(2)}) collective-permute-start(bf16[1,384,2048]{2,1,0:T(8,128)(2,1)} %param.25), channel_id=1, source_target_pairs={{0,1},{1,0},{2,3},{3,2},{4,5},{5,4},{6,7},{7,6},{8,9},{9,8},{10,11... | collective-permute-start | bytes 4718600 | tf_op jit(solution)/shard_map/ppermute | solution.py:185
  16.4 71.1 %all-to-all-start = ((bf16[8,32,2048]{2,1,0:T(8,128)(2,1)}), bf16[8,32,2048]{2,1,0:T(8,128)(2,1)S(1)}, u32[]{:S(2)}, u32[]{:S(2)}) async-start(bf16[8,32,2048]{2,1,0:T(8,128)(2,1)} %broadcast_in_dim.8), calls=%async_computation | async-start | bytes 2097152 | tf_op jit(solution)/shard_map/all_to_all | solution.py:160
  20.6 138.6 %all-gather.5.cloned.1.call-start = ((), (), s32[]{:S(2)}) async-start(), calls=%async_computation.5 | async-start | bytes 4325376 | tf_op jit(solution)/shard_map/all_gather | solution.py:212
  66.8 23.6 %copy-start.12 = (bf16[1,384,2048]{2,1,0:T(8,128)(2,1)}, bf16[1,384,2048]{2,1,0:T(8,128)(2,1)S(1)}, u32[]{:S(2)}) copy-start(bf16[1,384,2048]{2,1,0:T(8,128)(2,1)S(1)} %collective-permute-done) | copy-start | bytes 4718596
  87.5 3.1 copy-start.9
  90.4 0.9 copy-start.1
  95.2 5.0 %copy-start.3 = (s32[32,8]{0,1:T(8,128)S(1)}, s32[32,8]{0,1:T(8,128)}, u32[]{:S(2)}) copy-start(s32[32,8]{0,1:T(8,128)} %param.15) | copy-start | bytes 3076
  97.2 87.0 %collective-permute-start.2 = (bf16[1,1024,768]{1,2,0:T(8,128)(2,1)}, bf16[1,1024,768]{1,2,0:T(8,128)(2,1)}, u32[]{:S(2)}, u32[]{:S(2)}) collective-permute-start(bf16[1,1024,768]{1,2,0:T(8,128)(2,1)} %get-tuple-element.24), channel_id=1, source_target_pairs={{0,1},{1,0},{2,3},{3,2},{4,5},{5,4},{6,7},{7,6},{8,9},{9,8},{10,11... | collective-permute-start | bytes 4718600 | tf_op jit(solution)/shard_map/ppermute | solution.py:254
  97.5 90.7 %collective-permute-start.1 = (bf16[1,1024,768]{1,2,0:T(8,128)(2,1)}, bf16[1,1024,768]{1,2,0:T(8,128)(2,1)}, u32[]{:S(2)}, u32[]{:S(2)}) collective-permute-start(bf16[1,1024,768]{1,2,0:T(8,128)(2,1)} %get-tuple-element.25), channel_id=1, source_target_pairs={{0,1},{1,0},{2,3},{3,2},{4,5},{5,4},{6,7},{7,6},{8,9},{9,8},{10,11... | collective-permute-start | bytes 4718600 | tf_op jit(solution)/shard_map/ppermute | solution.py:253
  102.8 8.4 %copy-start.10 = (f32[128]{0:T(128)S(1)}, f32[128]{0:T(128)}, u32[]{:S(2)}) copy-start(f32[128]{0:T(128)} %param.20) | copy-start | bytes 1540
  176.4 6.8 %copy-start.6 = (s32[256]{0:T(256)S(1)}, s32[256]{0:T(256)}, u32[]{:S(2)}) copy-start(s32[256]{0:T(256)} %get-tuple-element.36) | copy-start | bytes 3076
  176.4 25.7 %copy-start = (bf16[32,2048]{1,0:T(8,128)(2,1)S(1)}, bf16[32,2048]{1,0:T(8,128)(2,1)}, u32[]{:S(2)}) copy-start(bf16[32,2048]{1,0:T(8,128)(2,1)} %param.13) | copy-start | bytes 393220
  176.4 25.9 %copy-start.2 = (f32[2048]{0:T(1024)S(1)}, f32[2048]{0:T(1024)}, u32[]{:S(2)}) copy-start(f32[2048]{0:T(1024)} %param.23) | copy-start | bytes 24580
  176.4 24.3 %all-to-all-start.1 = ((bf16[8,32,2048]{2,1,0:T(8,128)(2,1)}), bf16[8,32,2048]{2,1,0:T(8,128)(2,1)}, u32[]{:S(2)}, u32[]{:S(2)}) async-start(bf16[8,32,2048]{2,1,0:T(8,128)(2,1)} %bitcast.73), calls=%async_computation.1 | async-start | bytes 2097152 | tf_op jit(solution)/shard_map/all_to_all | solution.py:243
  183.1 5.1 %copy-start.7 = (s32[256]{0:T(256)}, s32[256]{0:T(256)S(1)}, u32[]{:S(2)}) copy-start(s32[256]{0:T(256)S(1)} %add_add_fusion) | copy-start | bytes 3076
  270.3 5.5 %copy-start.11 = (bf16[1,384,2048]{2,1,0:T(8,128)(2,1)S(1)}, bf16[1,384,2048]{2,1,0:T(8,128)(2,1)}, u32[]{:S(2)}) copy-start(bf16[1,384,2048]{2,1,0:T(8,128)(2,1)} %param.25) | copy-start | bytes 4718596
  270.3 5.5 %copy-start.13 = (bf16[1,384,2048]{2,1,0:T(8,128)(2,1)S(1)}, bf16[1,384,2048]{2,1,0:T(8,128)(2,1)}, u32[]{:S(2)}) copy-start(bf16[1,384,2048]{2,1,0:T(8,128)(2,1)} %copy-done.12) | copy-start | bytes 4718596
  281.8 6.9 %copy-start.4 = (f32[32,8]{0,1:T(8,128)S(1)}, f32[32,8]{0,1:T(8,128)}, u32[]{:S(2)}) copy-start(f32[32,8]{0,1:T(8,128)} %param.16) | copy-start | bytes 3076
  281.8 7.1 %copy-start.8 = (s32[256]{0:T(256)S(1)}, s32[256]{0:T(256)}, u32[]{:S(2)}) copy-start(s32[256]{0:T(256)} %copy-done.7) | copy-start | bytes 3076
  281.8 59.8 %all-to-all-start.3 = ((bf16[256,2,2048]{2,1,0:T(2,128)(2,1)}), bf16[256,2,2048]{2,1,0:T(2,128)(2,1)S(1)}, u32[]{:S(2)}, u32[]{:S(2)}) async-start(bf16[256,2,2048]{2,1,0:T(2,128)(2,1)} %copy.96), calls=%async_computation.3 | async-start | bytes 4194304 | tf_op jit(solution)/shard_map/all_to_all | solution.py:302
Sparse Core Ops, SparseCore 0:
  9.8 74.2 all-gather.2
  92.2 67.0 all-gather.4
